TPU v7x, 512 devices: a whole 4x4x16 slice. The times are simulated.
512 devices in a mesh: tm: 128 (over z, y, core), chan: 4 (over x).
Axes of the slice: x: 4, y: 4, z: 16, core: 2. Of those that a mesh axis runs over, the one named last changes fastest.
Arguments:
- series: bfloat16 [32768, 512], P('tm', 'chan'), may hold values from -6 to 6
- proj_weight: bfloat16 [512, 3, 512], P(None, None, 'chan'), may hold values from -0.25 to 0.25
- proj_bias: float32 [3, 512], P(None, 'chan'), may hold values from -6 to 6
- short_taps: float32 [3, 3, 512], P(None, None, 'chan'), may hold values from -6 to 6
- short_bias: float32 [3, 512], P(None, 'chan'), may hold values from -6 to 6
- spectrum: float32 [2, 128, 2, 256, 512], P(None, 'tm', None, None, 'chan'), may hold values from -6 to 6
- skip_gain: float32 [512], P('chan'), may hold values from -6 to 6
- out_weight: bfloat16 [512, 512], replicated, may hold values from -0.25 to 0.25
- out_bias: float32 [512], P('chan'), may hold values from -6 to 6
Outputs:
- mixed_out: bfloat16 [32768, 512], P('tm', 'chan')
All inputs are finite; a program needn't handle non-finite values.
Results may differ from a plain program's by a relative error of at most 0.009.
Values may be sent and summed in bfloat16 or wider, within the bound.
No kernel may reach another device: no remote copies, remote signals or barrier semaphores. Data moves between devices by JAX's collectives and lax.ppermute only.
A program may use at most 64 MiB of HBM per device.

v0:
```python
import math

import jax
import jax.numpy as jnp
from jax import lax
from jax.sharding import PartitionSpec as P


def from_behind(array, axis, by):
    length = lax.axis_size(axis)
    pairs = [(i, i + by) for i in range(length) if 0 <= i + by < length]
    return lax.ppermute(array, axis, pairs)


def partner_2(block, axis, bit):
    count = lax.axis_size(axis)
    route = []
    for low in range(count):
        high = low | 1 << bit
        if high != low and high < count:
            route += [(low, high), (high, low)]
    return lax.ppermute(block, axis, route)


def reverse_bits(values, digits):
    result = jnp.zeros_like(values)
    for bit_level in range(digits):
        result = result | (values >> bit_level & 1) << digits - 1 - bit_level
    return result


def turning(numer, denom):
    angle = numer.astype(jnp.float32) * (-2.0 * math.pi / denom)
    return (jnp.cos(angle), jnp.sin(angle))


def complex_times(stacked, real_part, imag_part):
    return jnp.stack(
        [
            stacked[0] * real_part - stacked[1] * imag_part,
            stacked[0] * imag_part + stacked[1] * real_part,
        ]
    )


def dft_rows(signals, period, inverse):
    indices = jnp.arange(period, dtype=jnp.int32)
    cosine, sine_part = turning(indices[:, None] * indices[None, :] % period, period)
    if inverse:
        sine_part = -sine_part
    stacked = jnp.concatenate([cosine, sine_part], 0)
    result = jnp.einsum("bt,retc->rebc", stacked, signals, precision=lax.Precision.HIGHEST)
    real_out = result[0, :, :period] - result[1, :, period:]
    imag_out = result[1, :, :period] + result[0, :, period:]
    return jnp.stack([real_out, imag_out])


def shards(
    series,
    proj_weight,
    proj_bias,
    short_taps,
    short_bias,
    spectrum,
    skip_gain,
    out_weight,
    out_bias,
):
    steps_dev = series.shape[0]
    model_width = proj_weight.shape[0]
    channels = proj_weight.shape[2]
    flat_weight = proj_weight.reshape(model_width, 3 * channels)
    weight_rows = flat_weight
    projected = jnp.dot(
        lax.all_gather(series, "chan", axis=1, tiled=True),
        weight_rows,
        preferred_element_type=jnp.float32,
    )
    projected = (projected.reshape(steps_dev, 3, channels) + proj_bias).astype(jnp.bfloat16)
    taps_count = short_taps.shape[0]
    earlier = from_behind(projected[steps_dev - taps_count + 1 :], "tm", 1)
    extended = jnp.concatenate([earlier, projected], 0).astype(jnp.float32)
    streams = short_bias + short_taps[0] * extended[taps_count - 1 :]
    for offset in range(1, taps_count):
        streams = (
            streams
            + short_taps[offset]
            * extended[taps_count - 1 - offset : taps_count - 1 - offset + steps_dev]
        )
    streams = lax.optimization_barrier(streams.astype(jnp.bfloat16)).astype(jnp.float32)
    gate_out = streams[:, 0]
    mixed_in = lax.optimization_barrier((streams[:, 1] * streams[:, 2]).astype(jnp.bfloat16))
    signal = mixed_in.astype(jnp.float32)
    tm_count = lax.axis_size("tm")
    digits = tm_count.bit_length() - 1
    own_index = lax.axis_index("tm")
    period = 2 * tm_count * steps_dev
    positions = jnp.arange(steps_dev, dtype=jnp.int32)
    own_rows = 2 * reverse_bits(own_index, digits) + jnp.arange(2, dtype=jnp.int32)
    twist_cos, twist_sin = turning(own_rows[:, None] * positions[None, :] % period, period)
    twist_cos, twist_sin = (twist_cos[:, :, None], twist_sin[:, :, None])
    half_cos, half_sin = turning(own_index, 2 * tm_count)
    zero_field = jnp.zeros_like(signal)
    current = jnp.stack(
        [jnp.stack([signal, signal * half_cos]), jnp.stack([zero_field, signal * half_sin])]
    )
    for bit_level in reversed(range(digits)):
        partner = partner_2(current, "tm", bit_level)
        half_span = 1 << bit_level
        rot_cos, rot_sin = turning(own_index % half_span, 2 * half_span)
        upper_half = own_index >> bit_level & 1 == 1
        current = jnp.where(
            upper_half, complex_times(partner - current, rot_cos, rot_sin), current + partner
        )
    twisted = complex_times(current, twist_cos, twist_sin)
    spectral = dft_rows(twisted, steps_dev, False)
    response = spectrum.reshape(2, 2, steps_dev, channels)
    product = complex_times(spectral, response[0], response[1])
    returned = dft_rows(product, steps_dev, True)
    current = complex_times(returned, twist_cos, -twist_sin)
    for bit_level in range(digits):
        partner = partner_2(current, "tm", bit_level)
        half_span = 1 << bit_level
        rot_cos, rot_sin = turning(own_index % half_span, 2 * half_span)
        rot_sin = -rot_sin
        upper_half = own_index >> bit_level & 1 == 1
        current = jnp.where(
            upper_half,
            partner - complex_times(current, rot_cos, rot_sin),
            current + complex_times(partner, rot_cos, rot_sin),
        )
    convolved = current[0, 0] + half_cos * current[0, 1] + half_sin * current[1, 1]
    convolved = convolved * (1.0 / period)
    gated_rows = ((convolved + skip_gain * signal) * gate_out).astype(jnp.bfloat16)
    column_start = lax.axis_index("chan") * channels
    weight_rows = lax.dynamic_slice_in_dim(out_weight, column_start, channels, 0)
    partial_value = jnp.dot(gated_rows, weight_rows, preferred_element_type=jnp.float32)
    mixed_out = lax.psum_scatter(partial_value, "chan", scatter_dimension=1, tiled=True)
    return (mixed_out + out_bias).astype(jnp.bfloat16)


def solution(mesh):
    return jax.shard_map(
        shards,
        mesh=mesh,
        in_specs=(
            P("tm", "chan"),
            P(None, None, "chan"),
            P(None, "chan"),
            P(None, None, "chan"),
            P(None, "chan"),
            P(None, "tm", None, None, "chan"),
            P("chan"),
            P(),
            P("chan"),
        ),
        out_specs=P("tm", "chan"),
        check_vma=False,
    )
```

profile of v0, /device:TPU:1, one launch (start us, length us, event | category | flops | bytes accessed | tf_op | source)
XLA Modules:
  0.0 432.7 jit_solution(13473676994499568312)
XLA Ops:
  6.5 1.2 copy.14
  7.8 10.3 %all_gather.3 = bf16[256,512]{1,0:T(8,128)(2,1)S(1)} all-gather(bf16[256,128]{1,0:T(8,128)(2,1)S(1)} %copy-done.5), channel_id=1, replica_groups=mesh['tm'=128,'chan'=4] {'chan'}, dimensions={1}, use_global_device_ids=true | all-gather | bytes 327680 | tf_op jit(solution)/shard_map/all_gather | solution.py:75
  18.1 0.3 fusion
  18.5 6.3 %collective-permute-start = (bf16[2,3,128]{2,0,1:T(2,128)(2,1)S(1)}, bf16[2,3,128]{2,0,1:T(2,128)(2,1)S(1)}, u32[]{:S(2)}, u32[]{:S(2)}) collective-permute-start(bf16[2,3,128]{2,0,1:T(2,128)(2,1)S(1)} %slice.304), channel_id=1, source_target_pairs={{0,4},{4,8},{8,12},{12,16},{16,20},{20,24},{24,28},{28,32},{32,36}... | collective-permute-start | bytes 4616 | tf_op jit(solution)/shard_map/ppermute | solution.py:12
  24.9 3.1 collective-permute-done
  28.1 0.7 copy-done.8
  29.0 0.6 copy-done.2
  29.7 12.8 %collective-permute-start.1 = (f32[2,2,256,128]{3,2,1,0:T(8,128)S(1)}, f32[2,2,256,128]{3,2,1,0:T(8,128)S(1)}, u32[]{:S(2)}, u32[]{:S(2)}) collective-permute-start(f32[2,2,256,128]{3,2,1,0:T(8,128)S(1)} %pad_maximum_fusion.2), channel_id=1, source_target_pairs={{0,256},{256,0},{4,260},{260,4},{8,264},{264,8},{12,268},{268,12},... | collective-permute-start | bytes 1572872 | tf_op jit(solution)/shard_map/ppermute | solution.py:22
  42.7 12.0 %collective-permute-done.1 = f32[2,2,256,128]{3,2,1,0:T(8,128)S(1)} collective-permute-done((f32[2,2,256,128]{3,2,1,0:T(8,128)S(1)}, f32[2,2,256,128]{3,2,1,0:T(8,128)S(1)}, u32[]{:S(2)}, u32[]{:S(2)}) %collective-permute-start.1) | collective-permute-done | bytes 524320 | tf_op jit(solution)/shard_map/ppermute | solution.py:22
  54.9 31.2 %collective-permute-start.2 = (f32[2,2,256,128]{3,2,1,0:T(8,128)S(1)}, f32[2,2,256,128]{3,2,1,0:T(8,128)S(1)}, u32[]{:S(2)}, u32[]{:S(2)}) collective-permute-start(f32[2,2,256,128]{3,2,1,0:T(8,128)S(1)} %maximum_select_fusion), channel_id=1, source_target_pairs={{0,128},{128,0},{4,132},{132,4},{8,136},{136,8},{12,140},{140,12},... | collective-permute-start | bytes 1572872 | tf_op jit(solution)/shard_map/ppermute | solution.py:22
  86.3 47.9 %collective-permute-done.2 = f32[2,2,256,128]{3,2,1,0:T(8,128)S(1)} collective-permute-done((f32[2,2,256,128]{3,2,1,0:T(8,128)S(1)}, f32[2,2,256,128]{3,2,1,0:T(8,128)S(1)}, u32[]{:S(2)}, u32[]{:S(2)}) %collective-permute-start.2) | collective-permute-done | bytes 524320 | tf_op jit(solution)/shard_map/ppermute | solution.py:22
  134.5 1.9 collective-permute-start.3
  136.6 23.5 %collective-permute-done.3 = f32[2,2,256,128]{3,2,1,0:T(8,128)S(1)} collective-permute-done((f32[2,2,256,128]{3,2,1,0:T(8,128)S(1)}, f32[2,2,256,128]{3,2,1,0:T(8,128)S(1)}, u32[]{:S(2)}, u32[]{:S(2)}) %collective-permute-start.3) | collective-permute-done | bytes 524320 | tf_op jit(solution)/shard_map/ppermute | solution.py:22
  160.4 1.9 collective-permute-start.4
  162.5 12.8 %collective-permute-done.4 = f32[2,2,256,128]{3,2,1,0:T(8,128)S(1)} collective-permute-done((f32[2,2,256,128]{3,2,1,0:T(8,128)S(1)}, f32[2,2,256,128]{3,2,1,0:T(8,128)S(1)}, u32[]{:S(2)}, u32[]{:S(2)}) %collective-permute-start.4) | collective-permute-done | bytes 524320 | tf_op jit(solution)/shard_map/ppermute | solution.py:22
  175.5 4.5 %collective-permute-start.5 = (f32[2,2,256,128]{3,2,1,0:T(8,128)S(1)}, f32[2,2,256,128]{3,2,1,0:T(8,128)S(1)}, u32[]{:S(2)}, u32[]{:S(2)}) collective-permute-start(f32[2,2,256,128]{3,2,1,0:T(8,128)S(1)} %maximum_select_fusion.3), channel_id=1, source_target_pairs={{0,16},{16,0},{4,20},{20,4},{8,24},{24,8},{12,28},{28,12},{32,48},... | collective-permute-start | bytes 1572872 | tf_op jit(solution)/shard_map/ppermute | solution.py:22
  180.2 10.8 %collective-permute-done.5 = f32[2,2,256,128]{3,2,1,0:T(8,128)S(1)} collective-permute-done((f32[2,2,256,128]{3,2,1,0:T(8,128)S(1)}, f32[2,2,256,128]{3,2,1,0:T(8,128)S(1)}, u32[]{:S(2)}, u32[]{:S(2)}) %collective-permute-start.5) | collective-permute-done | bytes 524320 | tf_op jit(solution)/shard_map/ppermute | solution.py:22
  191.2 3.3 collective-permute-start.6
  195.1 9.4 %collective-permute-done.6 = f32[2,2,256,128]{3,2,1,0:T(8,128)S(1)} collective-permute-done((f32[2,2,256,128]{3,2,1,0:T(8,128)S(1)}, f32[2,2,256,128]{3,2,1,0:T(8,128)S(1)}, u32[]{:S(2)}, u32[]{:S(2)}) %collective-permute-start.6) | collective-permute-done | bytes 524320 | tf_op jit(solution)/shard_map/ppermute | solution.py:22
  204.7 5.0 %collective-permute-start.7 = (f32[2,2,256,128]{3,2,1,0:T(8,128)S(1)}, f32[2,2,256,128]{3,2,1,0:T(8,128)S(1)}, u32[]{:S(2)}, u32[]{:S(2)}) collective-permute-start(f32[2,2,256,128]{3,2,1,0:T(8,128)S(1)} %maximum_select_fusion.5), channel_id=1, source_target_pairs={{0,4},{4,0},{8,12},{12,8},{16,20},{20,16},{24,28},{28,24},{32,36},... | collective-permute-start | bytes 1572872 | tf_op jit(solution)/shard_map/ppermute | solution.py:22
  209.7 1.0 fusion.48
  210.7 1.0 fusion.46
  212.1 0.2 multiply_subtract_fusion.15
  212.3 1.9 convolution_bitcast_fusion.1
  214.3 1.0 convolution_bitcast_fusion
  215.3 0.2 multiply_subtract_fusion.13
  215.6 1.9 collective-permute-start.8
  217.5 1.8 collective-permute-done.8
  219.4 0.9 fusion.13
  220.3 3.2 collective-permute-start.9
  223.5 1.1 multiply_subtract_fusion.11
  224.6 11.1 %collective-permute-done.9 = f32[2,2,256,128]{3,2,1,0:T(8,128)S(1)} collective-permute-done((f32[2,2,256,128]{3,2,1,0:T(8,128)}, f32[2,2,256,128]{3,2,1,0:T(8,128)S(1)}, u32[]{:S(2)}, u32[]{:S(2)}) %collective-permute-start.9) | collective-permute-done | bytes 524320 | tf_op jit(solution)/shard_map/ppermute | solution.py:22
  235.8 0.7 copy-done.1
  236.5 1.3 fusion.14
  237.8 4.5 %collective-permute-start.10 = (f32[2,2,256,128]{3,2,1,0:T(8,128)S(1)}, f32[2,2,256,128]{3,2,1,0:T(8,128)S(1)}, u32[]{:S(2)}, u32[]{:S(2)}) collective-permute-start(f32[2,2,256,128]{3,2,1,0:T(8,128)S(1)} %fusion.14), channel_id=1, source_target_pairs={{0,16},{16,0},{4,20},{20,4},{8,24},{24,8},{12,28},{28,12},{32,48},... | collective-permute-start | bytes 1572872 | tf_op jit(solution)/shard_map/ppermute | solution.py:22
  242.4 11.3 %collective-permute-done.10 = f32[2,2,256,128]{3,2,1,0:T(8,128)S(1)} collective-permute-done((f32[2,2,256,128]{3,2,1,0:T(8,128)S(1)}, f32[2,2,256,128]{3,2,1,0:T(8,128)S(1)}, u32[]{:S(2)}, u32[]{:S(2)}) %collective-permute-start.10) | collective-permute-done | bytes 524320 | tf_op jit(solution)/shard_map/ppermute | solution.py:22
  253.9 2.5 collective-permute-start.11
  256.4 11.0 %collective-permute-done.11 = f32[2,2,256,128]{3,2,1,0:T(8,128)S(1)} collective-permute-done((f32[2,2,256,128]{3,2,1,0:T(8,128)S(1)}, f32[2,2,256,128]{3,2,1,0:T(8,128)S(1)}, u32[]{:S(2)}, u32[]{:S(2)}) %collective-permute-start.11) | collective-permute-done | bytes 524320 | tf_op jit(solution)/shard_map/ppermute | solution.py:22
  267.6 3.4 collective-permute-start.12
  271.1 24.1 %collective-permute-done.12 = f32[2,2,256,128]{3,2,1,0:T(8,128)S(1)} collective-permute-done((f32[2,2,256,128]{3,2,1,0:T(8,128)S(1)}, f32[2,2,256,128]{3,2,1,0:T(8,128)S(1)}, u32[]{:S(2)}, u32[]{:S(2)}) %collective-permute-start.12) | collective-permute-done | bytes 524320 | tf_op jit(solution)/shard_map/ppermute | solution.py:22
  295.3 1.9 collective-permute-start.13
  297.3 61.7 %collective-permute-done.13 = f32[2,2,256,128]{3,2,1,0:T(8,128)S(1)} collective-permute-done((f32[2,2,256,128]{3,2,1,0:T(8,128)S(1)}, f32[2,2,256,128]{3,2,1,0:T(8,128)S(1)}, u32[]{:S(2)}, u32[]{:S(2)}) %collective-permute-start.13) | collective-permute-done | bytes 524320 | tf_op jit(solution)/shard_map/ppermute | solution.py:22
  359.2 7.4 %collective-permute-start.14 = (f32[2,2,256,128]{3,2,1,0:T(8,128)S(1)}, f32[2,2,256,128]{3,2,1,0:T(8,128)S(1)}, u32[]{:S(2)}, u32[]{:S(2)}) collective-permute-start(f32[2,2,256,128]{3,2,1,0:T(8,128)S(1)} %fusion.18), channel_id=1, source_target_pairs={{0,256},{256,0},{4,260},{260,4},{8,264},{264,8},{12,268},{268,12},... | collective-permute-start | bytes 1572872 | tf_op jit(solution)/shard_map/ppermute | solution.py:22
  366.7 17.2 %collective-permute-done.14 = f32[2,2,256,128]{3,2,1,0:T(8,128)S(1)} collective-permute-done((f32[2,2,256,128]{3,2,1,0:T(8,128)S(1)}, f32[2,2,256,128]{3,2,1,0:T(8,128)S(1)}, u32[]{:S(2)}, u32[]{:S(2)}) %collective-permute-start.14) | collective-permute-done | bytes 524320 | tf_op jit(solution)/shard_map/ppermute | solution.py:22
  384.1 0.7 copy-done.3
  384.8 1.0 fusion.44
  385.9 38.4 %reduce-scatter.2.cloned.1.call-done = f32[256,128]{1,0:T(8,128)} async-done(((f32[256,512]{1,0:T(8,128)}), f32[256,128]{1,0:T(8,128)}) %reduce-scatter.2.cloned.1.call-update) | async-done | bytes 131088 | tf_op jit(solution)/shard_map/reduce_scatter | solution.py:138
  424.3 1.5 add_convert_fusion
  (77 shorter events, 3.6 us)
Async XLA Ops:
  6.5 377.6 %copy-start = (bf16[512,512]{1,0:T(8,128)(2,1)S(1)}, bf16[512,512]{1,0:T(8,128)(2,1)}, u32[]{:S(2)}) copy-start(bf16[512,512]{1,0:T(8,128)(2,1)} %param.16) | copy-start | bytes 1572868
  6.5 1.2 copy-start.5
  6.5 417.8 %reduce-scatter.2.cloned.1.call-start = ((), (), s32[]{:S(2)}) async-start(), calls=%async_computation.1 | async-start | bytes 655360 | tf_op jit(solution)/shard_map/reduce_scatter | solution.py:138
  7.8 10.3 %copy-start.7 = (f32[3,128]{1,0:T(4,128)S(1)}, f32[3,128]{1,0:T(4,128)}, u32[]{:S(2)}) copy-start(f32[3,128]{1,0:T(4,128)} %param.11) | copy-start | bytes 4612
  18.1 6.6 %copy-start.6 = (f32[3,3,128]{2,1,0:T(4,128)S(1)}, f32[3,3,128]{2,1,0:T(4,128)}, u32[]{:S(2)}) copy-start(f32[3,3,128]{2,1,0:T(4,128)} %param.12) | copy-start | bytes 13828
  18.5 9.6 %collective-permute-start = (bf16[2,3,128]{2,0,1:T(2,128)(2,1)S(1)}, bf16[2,3,128]{2,0,1:T(2,128)(2,1)S(1)}, u32[]{:S(2)}, u32[]{:S(2)}) collective-permute-start(bf16[2,3,128]{2,0,1:T(2,128)(2,1)S(1)} %slice.304), channel_id=1, source_target_pairs={{0,4},{4,8},{8,12},{12,16},{16,20},{20,24},{24,28},{28,32},{32,36}... | collective-permute-start | bytes 4616 | tf_op jit(solution)/shard_map/ppermute | solution.py:12
  28.1 0.7 copy-start.8
  29.0 0.6 copy-start.2
  29.7 25.0 %collective-permute-start.1 = (f32[2,2,256,128]{3,2,1,0:T(8,128)S(1)}, f32[2,2,256,128]{3,2,1,0:T(8,128)S(1)}, u32[]{:S(2)}, u32[]{:S(2)}) collective-permute-start(f32[2,2,256,128]{3,2,1,0:T(8,128)S(1)} %pad_maximum_fusion.2), channel_id=1, source_target_pairs={{0,256},{256,0},{4,260},{260,4},{8,264},{264,8},{12,268},{268,12},... | collective-permute-start | bytes 1572872 | tf_op jit(solution)/shard_map/ppermute | solution.py:22
  54.9 79.3 %collective-permute-start.2 = (f32[2,2,256,128]{3,2,1,0:T(8,128)S(1)}, f32[2,2,256,128]{3,2,1,0:T(8,128)S(1)}, u32[]{:S(2)}, u32[]{:S(2)}) collective-permute-start(f32[2,2,256,128]{3,2,1,0:T(8,128)S(1)} %maximum_select_fusion), channel_id=1, source_target_pairs={{0,128},{128,0},{4,132},{132,4},{8,136},{136,8},{12,140},{140,12},... | collective-permute-start | bytes 1572872 | tf_op jit(solution)/shard_map/ppermute | solution.py:22
  134.5 25.6 %collective-permute-start.3 = (f32[2,2,256,128]{3,2,1,0:T(8,128)S(1)}, f32[2,2,256,128]{3,2,1,0:T(8,128)S(1)}, u32[]{:S(2)}, u32[]{:S(2)}) collective-permute-start(f32[2,2,256,128]{3,2,1,0:T(8,128)S(1)} %maximum_select_fusion.1), channel_id=1, source_target_pairs={{0,64},{64,0},{4,68},{68,4},{8,72},{72,8},{12,76},{76,12},{16,80},... | collective-permute-start | bytes 1572872 | tf_op jit(solution)/shard_map/ppermute | solution.py:22
  160.4 14.9 %collective-permute-start.4 = (f32[2,2,256,128]{3,2,1,0:T(8,128)S(1)}, f32[2,2,256,128]{3,2,1,0:T(8,128)S(1)}, u32[]{:S(2)}, u32[]{:S(2)}) collective-permute-start(f32[2,2,256,128]{3,2,1,0:T(8,128)S(1)} %maximum_select_fusion.2), channel_id=1, source_target_pairs={{0,32},{32,0},{4,36},{36,4},{8,40},{40,8},{12,44},{44,12},{16,48},... | collective-permute-start | bytes 1572872 | tf_op jit(solution)/shard_map/ppermute | solution.py:22
  175.5 15.5 %collective-permute-start.5 = (f32[2,2,256,128]{3,2,1,0:T(8,128)S(1)}, f32[2,2,256,128]{3,2,1,0:T(8,128)S(1)}, u32[]{:S(2)}, u32[]{:S(2)}) collective-permute-start(f32[2,2,256,128]{3,2,1,0:T(8,128)S(1)} %maximum_select_fusion.3), channel_id=1, source_target_pairs={{0,16},{16,0},{4,20},{20,4},{8,24},{24,8},{12,28},{28,12},{32,48},... | collective-permute-start | bytes 1572872 | tf_op jit(solution)/shard_map/ppermute | solution.py:22
  191.1 3.6 copy-start.4
  191.2 13.3 %collective-permute-start.6 = (f32[2,2,256,128]{3,2,1,0:T(8,128)S(1)}, f32[2,2,256,128]{3,2,1,0:T(8,128)S(1)}, u32[]{:S(2)}, u32[]{:S(2)}) collective-permute-start(f32[2,2,256,128]{3,2,1,0:T(8,128)S(1)} %maximum_select_fusion.4), channel_id=1, source_target_pairs={{0,8},{8,0},{4,12},{12,4},{16,24},{24,16},{20,28},{28,20},{32,40},... | collective-permute-start | bytes 1572872 | tf_op jit(solution)/shard_map/ppermute | solution.py:22
  204.7 7.1 %collective-permute-start.7 = (f32[2,2,256,128]{3,2,1,0:T(8,128)S(1)}, f32[2,2,256,128]{3,2,1,0:T(8,128)S(1)}, u32[]{:S(2)}, u32[]{:S(2)}) collective-permute-start(f32[2,2,256,128]{3,2,1,0:T(8,128)S(1)} %maximum_select_fusion.5), channel_id=1, source_target_pairs={{0,4},{4,0},{8,12},{12,8},{16,20},{20,16},{24,28},{28,24},{32,36},... | collective-permute-start | bytes 1572872 | tf_op jit(solution)/shard_map/ppermute | solution.py:22
  215.6 3.8 collective-permute-start.8
  220.3 15.4 %collective-permute-start.9 = (f32[2,2,256,128]{3,2,1,0:T(8,128)}, f32[2,2,256,128]{3,2,1,0:T(8,128)S(1)}, u32[]{:S(2)}, u32[]{:S(2)}) collective-permute-start(f32[2,2,256,128]{3,2,1,0:T(8,128)} %fusion.13), channel_id=1, source_target_pairs={{0,8},{8,0},{4,12},{12,4},{16,24},{24,16},{20,28},{28,20},{32,40},... | collective-permute-start | bytes 1572872 | tf_op jit(solution)/shard_map/ppermute | solution.py:22
  235.8 0.8 copy-start.1
  237.8 15.9 %collective-permute-start.10 = (f32[2,2,256,128]{3,2,1,0:T(8,128)S(1)}, f32[2,2,256,128]{3,2,1,0:T(8,128)S(1)}, u32[]{:S(2)}, u32[]{:S(2)}) collective-permute-start(f32[2,2,256,128]{3,2,1,0:T(8,128)S(1)} %fusion.14), channel_id=1, source_target_pairs={{0,16},{16,0},{4,20},{20,4},{8,24},{24,8},{12,28},{28,12},{32,48},... | collective-permute-start | bytes 1572872 | tf_op jit(solution)/shard_map/ppermute | solution.py:22
  253.9 13.5 %collective-permute-start.11 = (f32[2,2,256,128]{3,2,1,0:T(8,128)S(1)}, f32[2,2,256,128]{3,2,1,0:T(8,128)S(1)}, u32[]{:S(2)}, u32[]{:S(2)}) collective-permute-start(f32[2,2,256,128]{3,2,1,0:T(8,128)S(1)} %fusion.15), channel_id=1, source_target_pairs={{0,32},{32,0},{4,36},{36,4},{8,40},{40,8},{12,44},{44,12},{16,48},... | collective-permute-start | bytes 1572872 | tf_op jit(solution)/shard_map/ppermute | solution.py:22
  267.6 27.6 %collective-permute-start.12 = (f32[2,2,256,128]{3,2,1,0:T(8,128)S(1)}, f32[2,2,256,128]{3,2,1,0:T(8,128)S(1)}, u32[]{:S(2)}, u32[]{:S(2)}) collective-permute-start(f32[2,2,256,128]{3,2,1,0:T(8,128)S(1)} %fusion.16), channel_id=1, source_target_pairs={{0,64},{64,0},{4,68},{68,4},{8,72},{72,8},{12,76},{76,12},{16,80},... | collective-permute-start | bytes 1572872 | tf_op jit(solution)/shard_map/ppermute | solution.py:22
  295.3 63.7 %collective-permute-start.13 = (f32[2,2,256,128]{3,2,1,0:T(8,128)S(1)}, f32[2,2,256,128]{3,2,1,0:T(8,128)S(1)}, u32[]{:S(2)}, u32[]{:S(2)}) collective-permute-start(f32[2,2,256,128]{3,2,1,0:T(8,128)S(1)} %fusion.17), channel_id=1, source_target_pairs={{0,128},{128,0},{4,132},{132,4},{8,136},{136,8},{12,140},{140,12},... | collective-permute-start | bytes 1572872 | tf_op jit(solution)/shard_map/ppermute | solution.py:22
  359.2 24.7 %collective-permute-start.14 = (f32[2,2,256,128]{3,2,1,0:T(8,128)S(1)}, f32[2,2,256,128]{3,2,1,0:T(8,128)S(1)}, u32[]{:S(2)}, u32[]{:S(2)}) collective-permute-start(f32[2,2,256,128]{3,2,1,0:T(8,128)S(1)} %fusion.18), channel_id=1, source_target_pairs={{0,256},{256,0},{4,260},{260,4},{8,264},{264,8},{12,268},{268,12},... | collective-permute-start | bytes 1572872 | tf_op jit(solution)/shard_map/ppermute | solution.py:22
  384.0 0.8 copy-start.3
  384.0 0.8 copy-start.9
  385.8 38.5 %copy-start.10 = (f32[128]{0:T(128)S(1)}, f32[128]{0:T(128)}, u32[]{:S(2)}) copy-start(f32[128]{0:T(128)} %param.17) | copy-start | bytes 1540
Sparse Core Ops, SparseCore 0:
  386.0 38.2 reduce-scatter.1
where the time goes:
time: 435 us; the launch traced here: 433 us
  waiting for transfers between devices  296 us (68%)
  starting transfers between devices  91.9 us (21%)
  between operations  15.2 us (3%)
  other arithmetic  10.4 us (2%)
  blocking collectives  10.3 us (2%)
    ppermute x14, waiting for transfers between devices, partner_2(): return lax.ppermute(block, axis, route)  255 us
    ppermute x14, starting transfers between devices, partner_2(): return lax.ppermute(block, axis, route)  85.6 us
    reduce_scatter x1, waiting for transfers between devices, shards(): lax.psum_scatter(partial_value, 'chan', scatter_dimension=1, tiled=True)  38.4 us
    all_gather x1, blocking collectives, shards(): lax.all_gather(series, 'chan', axis=1, tiled=True)  10.3 us
  transfers between devices with their start and end apart: 16, of which 15 were waited for; matrix products, arithmetic and copies ran while one was open for 1% of the time, Pallas kernels for 0%

commit v1 on v0

v1 whole, which is shorter than its diff:
```python
import math

import jax
import jax.numpy as jnp
import numpy as np
from jax import lax
from jax.sharding import PartitionSpec as P

HI = lax.Precision.HIGHEST


def from_behind(array, axis, by):
    length = lax.axis_size(axis)
    pairs = [(i, i + by) for i in range(length) if 0 <= i + by < length]
    return lax.ppermute(array, axis, pairs)


def reverse_bits_np(values, digits):
    result = np.zeros_like(values)
    for bit_level in range(digits):
        result = result | (((values >> bit_level) & 1) << (digits - 1 - bit_level))
    return result


def dft_tables(tm_count, steps_dev):
    rows = 2 * tm_count
    digits = tm_count.bit_length() - 1
    r = np.arange(rows)
    k1 = 2 * reverse_bits_np(r // 2, digits) + (r % 2)
    m = np.arange(tm_count)
    t = np.arange(steps_dev)
    b = np.arange(steps_dev)
    period = rows * steps_dev
    ang1 = 2 * np.pi * ((k1[:, None] * m[None, :]) % rows) / rows
    ang2 = 2 * np.pi * ((t[:, None] * b[None, :]) % steps_dev) / steps_dev
    angt = 2 * np.pi * ((k1[:, None] * t[None, :]) % period) / period
    f32 = lambda a: jnp.asarray(a.astype(np.float32))
    return dict(
        c1=f32(np.cos(ang1)), s1=f32(np.sin(ang1)),
        c2=f32(np.cos(ang2)), s2=f32(np.sin(ang2)),
        ct=f32(np.cos(angt)), st=f32(np.sin(angt)),
        period=period,
    )


def mm(a, b):
    return jnp.dot(a, b, precision=HI, preferred_element_type=jnp.float32)


def long_conv(x, h, tab):
    c1, s1, c2, s2, ct, st = (tab[k] for k in ("c1", "s1", "c2", "s2", "ct", "st"))
    ar = mm(c1, x)
    ai = -mm(s1, x)
    tr = ar * ct + ai * st
    ti = ai * ct - ar * st
    zr = mm(tr, c2) + mm(ti, s2)
    zi = mm(ti, c2) - mm(tr, s2)
    yr = h[0] * zr - h[1] * zi
    yi = h[0] * zi + h[1] * zr
    br = mm(yr, c2) - mm(yi, s2)
    bi = mm(yi, c2) + mm(yr, s2)
    ur = br * ct - bi * st
    ui = bi * ct + br * st
    y = lax.dot_general(c1, ur, (((0,), (0,)), ((), ())), precision=HI,
                        preferred_element_type=jnp.float32)
    y = y - lax.dot_general(s1, ui, (((0,), (0,)), ((), ())), precision=HI,
                            preferred_element_type=jnp.float32)
    return y * (1.0 / tab["period"])


def shards(series, proj_weight, proj_bias, short_taps, short_bias, spectrum,
           skip_gain, out_weight, out_bias):
    steps_dev = series.shape[0]
    model_width = proj_weight.shape[0]
    channels = proj_weight.shape[2]
    tm_count = lax.axis_size("tm")
    tab = dft_tables(tm_count, steps_dev)

    flat_weight = proj_weight.reshape(model_width, 3 * channels)
    projected = jnp.dot(
        lax.all_gather(series, "chan", axis=1, tiled=True),
        flat_weight,
        preferred_element_type=jnp.float32,
    )
    projected = (projected.reshape(steps_dev, 3, channels) + proj_bias).astype(jnp.bfloat16)
    taps_count = short_taps.shape[0]
    earlier = from_behind(projected[steps_dev - taps_count + 1:], "tm", 1)
    extended = jnp.concatenate([earlier, projected], 0).astype(jnp.float32)
    streams = short_bias + short_taps[0] * extended[taps_count - 1:]
    for offset in range(1, taps_count):
        streams = (
            streams
            + short_taps[offset]
            * extended[taps_count - 1 - offset: taps_count - 1 - offset + steps_dev]
        )
    streams = streams.astype(jnp.bfloat16)
    gate_out = streams[:, 0]
    mixed_in = (streams[:, 1].astype(jnp.float32) * streams[:, 2].astype(jnp.float32)).astype(jnp.bfloat16)

    pair = jnp.stack([mixed_in, gate_out])[:, None]
    pair = lax.all_to_all(pair, "tm", 3, 1, tiled=True)
    signal_bf = pair[0, :, :, 0]
    gate_own = pair[1, :, :, 0].astype(jnp.float32)
    h = lax.all_to_all(spectrum, "tm", 4, 1, tiled=True)
    h = h.reshape(2, 2 * tm_count, steps_dev)

    signal = signal_bf.astype(jnp.float32)
    convolved = long_conv(signal, h, tab)
    skip = lax.dynamic_index_in_dim(skip_gain, lax.axis_index("tm"), 0, keepdims=False)
    gated = ((convolved + skip * signal) * gate_own).astype(jnp.bfloat16)

    gated = lax.all_to_all(gated[:, :, None], "tm", 0, 2, tiled=True)
    gated = lax.all_gather(gated[0], "chan", axis=1, tiled=True)
    column_start = lax.axis_index("chan") * channels
    weight_cols = lax.dynamic_slice_in_dim(out_weight, column_start, channels, 1)
    mixed_out = jnp.dot(gated, weight_cols, preferred_element_type=jnp.float32) + out_bias
    return mixed_out.astype(jnp.bfloat16)


def solution(mesh):
    return jax.shard_map(
        shards,
        mesh=mesh,
        in_specs=(
            P("tm", "chan"),
            P(None, None, "chan"),
            P(None, "chan"),
            P(None, None, "chan"),
            P(None, "chan"),
            P(None, "tm", None, None, "chan"),
            P("chan"),
            P(),
            P("chan"),
        ),
        out_specs=P("tm", "chan"),
        check_vma=False,
    )
```

time: 435 us -> 141 us (0.32)
  waiting for transfers between devices: 296 us -> 57.8 us
  starting transfers between devices: 91.9 us -> 41 us
  between operations: 15.2 us -> 0.34 us
  blocking collectives: 10.3 us -> 20.1 us
  other arithmetic: 10.4 us -> 1.24 us
  local copies, waits for them, and re-layouts: 4.29 us -> 10.7 us
    ppermute x14 -> x0, waiting for transfers between devices: 255 us -> none  [partner_2(): return lax.ppermute(block, axis, route)]
    ppermute x14 -> x0, starting transfers between devices: 85.6 us -> none  [partner_2(): return lax.ppermute(block, axis, route)]
    all_to_all x0 -> x3, waiting for transfers between devices: none -> 54.5 us  [the longest x1 24.7 us: shards(): h = lax.all_to_all(spectrum, 'tm', 4, 1, tiled=True)]
    reduce_scatter x1 -> x0, waiting for transfers between devices: 38.4 us -> none  [shards(): lax.psum_scatter(partial_value, 'chan', scatter_dimension=1, tiled=True)]
    all_to_all x0 -> x3, starting transfers between devices: none -> 34.7 us  [the longest x1 18.2 us: shards(): pair = lax.all_to_all(pair, 'tm', 3, 1, tiled=True)]
    all_gather x0 -> x1, blocking collectives: none -> 9.8 us  [shards(): gated = lax.all_gather(gated[0], 'chan', axis=1, tiled=True)]
  transfers between devices with their start and end apart: 16 -> 4, of which waited for: 15 -> 4; matrix products, arithmetic and copies ran while one was open for 1% -> 3% of each run, Pallas kernels for 0% -> 0%
where the time goes in v1:
time: 141 us; the launch traced here: 139 us
  waiting for transfers between devices  57.8 us (41%)
  starting transfers between devices  41 us (29%)
  blocking collectives  20.1 us (14%)
  local copies, waits for them, and re-layouts  10.7 us (8%)
  matrix products  8.38 us (6%)
    all_to_all x1, waiting for transfers between devices, shards(): h = lax.all_to_all(spectrum, 'tm', 4, 1, tiled=True)  24.7 us
    all_to_all x1, starting transfers between devices, shards(): pair = lax.all_to_all(pair, 'tm', 3, 1, tiled=True)  18.2 us
    all_to_all x1, waiting for transfers between devices, shards(): pair = lax.all_to_all(pair, 'tm', 3, 1, tiled=True)  15 us
    all_to_all x1, waiting for transfers between devices, shards(): gated = lax.all_to_all(gated[:, :, None], 'tm', 0, 2, tiled=True)  14.8 us
    all_gather x1, blocking collectives, shards(): lax.all_gather(series, 'chan', axis=1, tiled=True)  10.3 us
    all_gather x1, blocking collectives, shards(): gated = lax.all_gather(gated[0], 'chan', axis=1, tiled=True)  9.8 us
    all_to_all x1, starting transfers between devices, shards(): gated = lax.all_to_all(gated[:, :, None], 'tm', 0, 2, tiled=True)  9.22 us
    unnamed x44, local copies, waits for them, and re-layouts  8.47 us
  transfers between devices with their start and end apart: 4, of which 4 were waited for; matrix products, arithmetic and copies ran while one was open for 3% of the time, Pallas kernels for 0%

profile of v1, /device:TPU:1, one launch (start us, length us, event | category | flops | bytes accessed | tf_op | source)
XLA Modules:
  0.0 139.5 jit_solution(8496077110473266639)
XLA Ops:
  0.0 1.2 copy.32
  1.3 10.3 %all_gather.6 = bf16[256,512]{1,0:T(8,128)(2,1)S(1)} all-gather(bf16[256,128]{1,0:T(8,128)(2,1)S(1)} %copy-done.13), channel_id=1, replica_groups=mesh['tm'=128,'chan'=4] {'chan'}, dimensions={1}, use_global_device_ids=true | all-gather | bytes 327680 | tf_op jit(solution)/shard_map/all_gather | solution.py:81
  11.6 0.3 fusion
  11.9 6.3 %collective-permute-start = (bf16[2,3,128]{2,0,1:T(2,128)(2,1)S(1)}, bf16[2,3,128]{2,0,1:T(2,128)(2,1)S(1)}, u32[]{:S(2)}, u32[]{:S(2)}) collective-permute-start(bf16[2,3,128]{2,0,1:T(2,128)(2,1)S(1)} %slice.63), channel_id=1, source_target_pairs={{0,4},{4,8},{8,12},{12,16},{16,20},{20,24},{24,28},{28,32},{32,36}... | collective-permute-start | bytes 4616 | tf_op jit(solution)/shard_map/ppermute | solution.py:15
  18.2 3.3 %collective-permute-done = bf16[2,3,128]{2,0,1:T(2,128)(2,1)S(1)} collective-permute-done((bf16[2,3,128]{2,0,1:T(2,128)(2,1)S(1)}, bf16[2,3,128]{2,0,1:T(2,128)(2,1)S(1)}, u32[]{:S(2)}, u32[]{:S(2)}) %collective-permute-start) | collective-permute-done | bytes 1568 | tf_op jit(solution)/shard_map/ppermute | solution.py:15
  21.6 0.7 copy-done.16
  22.2 0.1 fusion.9
  22.5 0.8 copy.33
  23.3 18.2 %all-to-all-start.1 = ((bf16[2,1,256,128]{2,0,1,3:T(2,128)(2,1)}), bf16[2,1,256,128]{2,0,1,3:T(2,128)(2,1)S(1)}, u32[]{:S(2)}, u32[]{:S(2)}) async-start(bf16[2,1,256,128]{2,0,1,3:T(2,128)(2,1)} %copy.33), calls=%async_computation.1 | async-start | bytes 262144 | tf_op jit(solution)/shard_map/all_to_all | solution.py:101
  41.5 1.0 copy.31
  42.5 15.0 %all-to-all-done.1 = bf16[2,1,256,128]{2,0,1,3:T(2,128)(2,1)S(1)} async-done(((bf16[2,1,256,128]{2,0,1,3:T(2,128)(2,1)}), bf16[2,1,256,128]{2,0,1,3:T(2,128)(2,1)S(1)}, u32[]{:S(2)}, u32[]{:S(2)}) %all-to-all-start.1) | async-done | bytes 131104 | tf_op jit(solution)/shard_map/all_to_all | solution.py:101
  57.5 7.2 %all-to-all-start = ((f32[2,1,2,256,128]{3,2,1,0,4:T(2,128)}), f32[2,1,2,256,128]{3,2,1,0,4:T(2,128)S(1)}, u32[]{:S(2)}, u32[]{:S(2)}) async-start(f32[2,1,2,256,128]{3,2,1,0,4:T(2,128)} %copy.31), calls=%async_computation | async-start | bytes 1048576 | tf_op jit(solution)/shard_map/all_to_all | solution.py:104
  64.7 0.6 copy-done.18
  65.4 0.6 dynamic_slice.7
  66.0 0.1 copy.34
  66.1 0.8 copy-done.11
  66.9 0.3 convolution_negate_fusion
  67.2 0.3 fusion.26
  67.4 0.4 copy-done.3
  67.8 0.1 copy-done.6
  67.9 0.2 copy-done.2
  68.2 0.4 fusion.23
  68.5 0.5 copy-done.1
  69.1 0.1 copy-done.5
  69.2 1.1 fusion.24
  70.3 0.4 convolution_add_fusion.2
  70.7 24.7 %all-to-all-done = f32[2,1,2,256,128]{3,2,1,0,4:T(2,128)S(1)} async-done(((f32[2,1,2,256,128]{3,2,1,0,4:T(2,128)}), f32[2,1,2,256,128]{3,2,1,0,4:T(2,128)S(1)}, u32[]{:S(2)}, u32[]{:S(2)}) %all-to-all-start) | async-done | bytes 524320 | tf_op jit(solution)/shard_map/all_to_all | solution.py:104
  95.4 0.2 fusion.28
  95.6 0.2 squeeze.23
  95.8 0.2 squeeze.21
  96.0 0.8 copy-done.7
  96.7 1.4 multiply_subtract_fusion
  98.1 0.4 fusion.30
  98.5 0.4 fusion.29
  98.9 0.4 convolution_add_fusion.1
  99.3 0.4 convolution_subtract_fusion
  99.6 0.5 copy-done.9
  100.2 0.6 fusion.18
  100.8 0.3 copy-done.12
  101.1 1.2 fusion.7
  102.3 0.1 copy.36
  102.5 0.5 broadcast.5
  103.0 1.0 reduce
  104.0 0.7 reshape.55
  104.6 9.2 %all-to-all-start.2 = ((bf16[128,2,128]{2,1,0:T(2,128)(2,1)}), bf16[128,2,128]{2,1,0:T(2,128)(2,1)S(1)}, u32[]{:S(2)}, u32[]{:S(2)}) async-start(bf16[128,2,128]{2,1,0:T(2,128)(2,1)} %reshape.55), calls=%async_computation.2 | async-start | bytes 131072 | tf_op jit(solution)/shard_map/all_to_all | solution.py:112
  113.9 14.8 %all-to-all-done.2 = bf16[128,2,128]{2,1,0:T(2,128)(2,1)S(1)} async-done(((bf16[128,2,128]{2,1,0:T(2,128)(2,1)}), bf16[128,2,128]{2,1,0:T(2,128)(2,1)S(1)}, u32[]{:S(2)}, u32[]{:S(2)}) %all-to-all-start.2) | async-done | bytes 65568 | tf_op jit(solution)/shard_map/all_to_all | solution.py:112
  128.8 9.8 %all-gather = bf16[1,256,512,1]{1,2,3,0:T(8,128)(2,1)S(1)} all-gather(bf16[1,256,128,1]{1,2,3,0:T(8,128)(2,1)S(1)} %bitcast.98), channel_id=2, replica_groups=mesh['tm'=128,'chan'=4] {'chan'}, dimensions={2}, use_global_device_ids=true | all-gather | bytes 327680 | tf_op jit(solution)/shard_map/all_gather | solution.py:113
  138.6 0.9 fusion.6
  (35 shorter events, 0.2 us)
Async XLA Ops:
  0.0 138.6 %copy-start = (bf16[512,512]{1,0:T(8,128)(2,1)S(1)}, bf16[512,512]{1,0:T(8,128)(2,1)}, u32[]{:S(2)}) copy-start(bf16[512,512]{1,0:T(8,128)(2,1)} %param.22) | copy-start | bytes 1572868
  0.0 1.2 copy-start.13
  1.2 10.3 %copy-start.15 = (f32[3,128]{1,0:T(4,128)S(1)}, f32[3,128]{1,0:T(4,128)}, u32[]{:S(2)}) copy-start(f32[3,128]{1,0:T(4,128)} %param.17) | copy-start | bytes 4612
  11.6 6.6 %copy-start.14 = (f32[3,3,128]{2,1,0:T(4,128)S(1)}, f32[3,3,128]{2,1,0:T(4,128)}, u32[]{:S(2)}) copy-start(f32[3,3,128]{2,1,0:T(4,128)} %param.18) | copy-start | bytes 13828
  11.9 9.6 %collective-permute-start = (bf16[2,3,128]{2,0,1:T(2,128)(2,1)S(1)}, bf16[2,3,128]{2,0,1:T(2,128)(2,1)S(1)}, u32[]{:S(2)}, u32[]{:S(2)}) collective-permute-start(bf16[2,3,128]{2,0,1:T(2,128)(2,1)S(1)} %slice.63), channel_id=1, source_target_pairs={{0,4},{4,8},{8,12},{12,16},{16,20},{20,24},{24,28},{28,32},{32,36}... | collective-permute-start | bytes 4616 | tf_op jit(solution)/shard_map/ppermute | solution.py:15
  21.5 0.7 copy-start.16
  22.4 19.1 %copy-start.10 = (f32[2,1,2,256,128]{4,3,2,1,0:T(8,128)S(1)}, f32[2,1,2,256,128]{4,3,2,1,0:T(8,128)}, u32[]{:S(2)}) copy-start(f32[2,1,2,256,128]{4,3,2,1,0:T(8,128)} %param.20) | copy-start | bytes 1572868
  23.3 34.2 %all-to-all-start.1 = ((bf16[2,1,256,128]{2,0,1,3:T(2,128)(2,1)}), bf16[2,1,256,128]{2,0,1,3:T(2,128)(2,1)S(1)}, u32[]{:S(2)}, u32[]{:S(2)}) async-start(bf16[2,1,256,128]{2,0,1,3:T(2,128)(2,1)} %copy.33), calls=%async_computation.1 | async-start | bytes 262144 | tf_op jit(solution)/shard_map/all_to_all | solution.py:101
  57.5 37.9 %all-to-all-start = ((f32[2,1,2,256,128]{3,2,1,0,4:T(2,128)}), f32[2,1,2,256,128]{3,2,1,0,4:T(2,128)S(1)}, u32[]{:S(2)}, u32[]{:S(2)}) async-start(f32[2,1,2,256,128]{3,2,1,0,4:T(2,128)} %copy.31), calls=%async_computation | async-start | bytes 1048576 | tf_op jit(solution)/shard_map/all_to_all | solution.py:104
  64.7 0.7 copy-start.18
  66.0 0.9 copy-start.11
  66.0 1.2 copy-start.8
  66.9 1.0 copy-start.3
  66.9 1.0 copy-start.6
  67.2 1.0 copy-start.2
  68.1 0.9 copy-start.1
  68.1 1.0 copy-start.5
  69.2 1.1 copy-start.4
  95.8 1.0 copy-start.7
  99.2 0.9 copy-start.9
  100.2 0.9 copy-start.12
  104.6 24.1 %all-to-all-start.2 = ((bf16[128,2,128]{2,1,0:T(2,128)(2,1)}), bf16[128,2,128]{2,1,0:T(2,128)(2,1)S(1)}, u32[]{:S(2)}, u32[]{:S(2)}) async-start(bf16[128,2,128]{2,1,0:T(2,128)(2,1)} %reshape.55), calls=%async_computation.2 | async-start | bytes 131072 | tf_op jit(solution)/shard_map/all_to_all | solution.py:112
  128.7 9.8 %copy-start.17 = (f32[128]{0:T(128)S(1)}, f32[128]{0:T(128)}, u32[]{:S(2)}) copy-start(f32[128]{0:T(128)} %param.23) | copy-start | bytes 1540

commit v2 on v1

--- a/solution.py
+++ b/solution.py
@@ -97,12 +97,14 @@
     gate_out = streams[:, 0]
     mixed_in = (streams[:, 1].astype(jnp.float32) * streams[:, 2].astype(jnp.float32)).astype(jnp.bfloat16)
 
-    pair = jnp.stack([mixed_in, gate_out])[:, None]
-    pair = lax.all_to_all(pair, "tm", 3, 1, tiled=True)
-    signal_bf = pair[0, :, :, 0]
-    gate_own = pair[1, :, :, 0].astype(jnp.float32)
-    h = lax.all_to_all(spectrum, "tm", 4, 1, tiled=True)
-    h = h.reshape(2, 2 * tm_count, steps_dev)
+    send = jnp.concatenate(
+        [spectrum.reshape(-1, channels), mixed_in.astype(jnp.float32), gate_out.astype(jnp.float32)], 0)
+    recv = lax.all_to_all(send[None], "tm", 2, 0, tiled=True)[:, :, 0]
+    spec_len = spectrum.size // channels
+    h = recv[:, :spec_len].reshape(tm_count, 2, spec_len // 2)
+    h = jnp.stack([h[:, 0].reshape(2 * tm_count, steps_dev), h[:, 1].reshape(2 * tm_count, steps_dev)])
+    signal_bf = recv[:, spec_len:spec_len + steps_dev]
+    gate_own = recv[:, spec_len + steps_dev:]
 
     signal = signal_bf.astype(jnp.float32)
     convolved = long_conv(signal, h, tab)

time: 141 us -> 133 us (0.943)
  starting transfers between devices: 41 us -> 33.7 us
  matrix products: 8.38 us -> 6.97 us
    all_to_all x2 -> x1, starting transfers between devices: 25.5 us -> 18.2 us  [shards(): recv = lax.all_to_all(send[None], 'tm', 2, 0, tiled=True)[:, :, 0]]
    dot_general x10, matrix products: 5.31 us -> 3.88 us  [mm(): return jnp.dot(a, b, precision=HI, preferred_element_type=jnp.float32)]
    unnamed x44 -> x39, local copies, waits for them, and re-layouts: 8.47 us -> 7.24 us
    all_to_all x2 -> x1, waiting for transfers between devices: 39.7 us -> 40.4 us  [shards(): recv = lax.all_to_all(send[None], 'tm', 2, 0, tiled=True)[:, :, 0]]
  transfers between devices with their start and end apart: 4 -> 3, of which waited for: 4 -> 3; matrix products, arithmetic and copies ran while one was open for 3% -> 1% of each run, Pallas kernels for 0% -> 0%
where the time goes in v2:
time: 133 us; the launch traced here: 131 us
  waiting for transfers between devices  58.3 us (44%)
  starting transfers between devices  33.7 us (25%)
  blocking collectives  20.2 us (15%)
  local copies, waits for them, and re-layouts  10.5 us (8%)
  matrix products  6.97 us (5%)
    all_to_all x1, waiting for transfers between devices, shards(): recv = lax.all_to_all(send[None], 'tm', 2, 0, tiled=True)[:, :, 0]  40.4 us
    all_to_all x1, starting transfers between devices, shards(): recv = lax.all_to_all(send[None], 'tm', 2, 0, tiled=True)[:, :, 0]  18.2 us
    all_to_all x1, waiting for transfers between devices, shards(): gated = lax.all_to_all(gated[:, :, None], 'tm', 0, 2, tiled=True)  14.8 us
    all_gather x1, blocking collectives, shards(): lax.all_gather(series, 'chan', axis=1, tiled=True)  10.4 us
    all_gather x1, blocking collectives, shards(): gated = lax.all_gather(gated[0], 'chan', axis=1, tiled=True)  9.8 us
    all_to_all x1, starting transfers between devices, shards(): gated = lax.all_to_all(gated[:, :, None], 'tm', 0, 2, tiled=True)  9.21 us
    unnamed x39, local copies, waits for them, and re-layouts  7.24 us
    ppermute x1, starting transfers between devices, from_behind(): return lax.ppermute(array, axis, pairs)  6.27 us
  transfers between devices with their start and end apart: 3, of which 3 were waited for; matrix products, arithmetic and copies ran while one was open for 1% of the time, Pallas kernels for 0%

profile of v2, /device:TPU:1, one launch (start us, length us, event | category | flops | bytes accessed | tf_op | source)
XLA Modules:
  0.0 131.4 jit_solution(11264655801105573432)
XLA Ops:
  0.0 1.2 copy.33
  1.3 10.4 %all_gather.6 = bf16[256,512]{1,0:T(8,128)(2,1)S(1)} all-gather(bf16[256,128]{1,0:T(8,128)(2,1)S(1)} %copy-done.10), channel_id=1, replica_groups=mesh['tm'=128,'chan'=4] {'chan'}, dimensions={1}, use_global_device_ids=true | all-gather | bytes 327680 | tf_op jit(solution)/shard_map/all_gather | solution.py:81
  11.7 0.3 fusion
  12.1 6.3 %collective-permute-start = (bf16[2,3,128]{2,0,1:T(2,128)(2,1)S(1)}, bf16[2,3,128]{2,0,1:T(2,128)(2,1)S(1)}, u32[]{:S(2)}, u32[]{:S(2)}) collective-permute-start(bf16[2,3,128]{2,0,1:T(2,128)(2,1)S(1)} %slice.60), channel_id=1, source_target_pairs={{0,4},{4,8},{8,12},{12,16},{16,20},{20,24},{24,28},{28,32},{32,36}... | collective-permute-start | bytes 4616 | tf_op jit(solution)/shard_map/ppermute | solution.py:15
  18.4 0.2 copy.42
  18.6 3.1 %collective-permute-done = bf16[2,3,128]{2,0,1:T(2,128)(2,1)S(1)} collective-permute-done((bf16[2,3,128]{2,0,1:T(2,128)(2,1)S(1)}, bf16[2,3,128]{2,0,1:T(2,128)(2,1)S(1)}, u32[]{:S(2)}, u32[]{:S(2)}) %collective-permute-start) | collective-permute-done | bytes 1568 | tf_op jit(solution)/shard_map/ppermute | solution.py:15
  21.7 0.7 copy-done.13
  22.4 0.1 fusion.9
  22.6 0.1 copy.35
  22.7 0.1 copy.34
  22.8 0.1 pad_maximum_fusion
  22.8 1.4 %broadcast_in_dim.4 = f32[1,1536,128]{1,0,2:T(1,128)} reshape(f32[1536,128]{0,1:T(8,128)S(1)} %pad_maximum_fusion) | data formatting | bytes 1572864 | tf_op jit(solution)/shard_map/broadcast_in_dim | solution.py:102
  24.3 18.2 %all-to-all-start = ((f32[1,1536,128]{1,0,2:T(1,128)}), f32[1,1536,128]{1,0,2:T(1,128)S(1)}, u32[]{:S(2)}, u32[]{:S(2)}) async-start(f32[1,1536,128]{1,0,2:T(1,128)} %broadcast_in_dim.4), calls=%async_computation | async-start | bytes 1572864 | tf_op jit(solution)/shard_map/all_to_all | solution.py:102
  42.5 0.0 copy-start.15
  42.5 0.6 copy-done.15
  43.2 0.6 dynamic_slice.7
  43.7 40.4 %all-to-all-done = f32[1,1536,128]{1,0,2:T(1,128)S(1)} async-done(((f32[1,1536,128]{1,0,2:T(1,128)}), f32[1,1536,128]{1,0,2:T(1,128)S(1)}, u32[]{:S(2)}, u32[]{:S(2)}) %all-to-all-start) | async-done | bytes 786464 | tf_op jit(solution)/shard_map/all_to_all | solution.py:102
  84.2 0.6 copy.36
  84.8 0.1 copy.45
  85.0 0.1 copy.44
  85.1 0.0 copy-start.9
  85.2 0.8 copy-done.9
  86.1 0.4 convolution_negate_fusion
  86.4 0.5 copy-done.8
  87.0 0.4 fusion.24
  87.4 0.6 copy-done.2
  87.9 0.1 copy-done.3
  88.0 0.4 fusion.26
  88.4 0.6 copy-done.1
  89.0 0.1 copy-done.5
  89.0 0.4 fusion.27
  89.4 0.5 copy-done.4
  90.0 0.4 convolution_add_fusion.2
  90.4 0.4 multiply_subtract_fusion
  90.8 0.4 fusion.34
  91.2 0.4 fusion.33
  91.6 0.4 convolution_add_fusion.1
  92.0 0.4 convolution_subtract_fusion
  92.4 0.6 fusion.18
  93.0 1.3 fusion.7
  94.2 0.1 copy.40
  94.4 0.5 broadcast.5
  94.9 1.0 reduce
  95.9 0.7 reshape.31
  96.6 9.2 %all-to-all-start.1 = ((bf16[128,2,128]{2,1,0:T(2,128)(2,1)}), bf16[128,2,128]{2,1,0:T(2,128)(2,1)S(1)}, u32[]{:S(2)}, u32[]{:S(2)}) async-start(bf16[128,2,128]{2,1,0:T(2,128)(2,1)} %reshape.31), calls=%async_computation.1 | async-start | bytes 131072 | tf_op jit(solution)/shard_map/all_to_all | solution.py:114
  105.8 14.8 %all-to-all-done.1 = bf16[128,2,128]{2,1,0:T(2,128)(2,1)S(1)} async-done(((bf16[128,2,128]{2,1,0:T(2,128)(2,1)}), bf16[128,2,128]{2,1,0:T(2,128)(2,1)S(1)}, u32[]{:S(2)}, u32[]{:S(2)}) %all-to-all-start.1) | async-done | bytes 65568 | tf_op jit(solution)/shard_map/all_to_all | solution.py:114
  120.7 9.8 %all-gather = bf16[1,256,512,1]{1,2,3,0:T(8,128)(2,1)S(1)} all-gather(bf16[1,256,128,1]{1,2,3,0:T(8,128)(2,1)S(1)} %bitcast.96), channel_id=2, replica_groups=mesh['tm'=128,'chan'=4] {'chan'}, dimensions={2}, use_global_device_ids=true | all-gather | bytes 327680 | tf_op jit(solution)/shard_map/all_gather | solution.py:115
  130.5 0.9 fusion.6
  (32 shorter events, 0.3 us)
Async XLA Ops:
  0.0 130.5 %copy-start = (bf16[512,512]{1,0:T(8,128)(2,1)S(1)}, bf16[512,512]{1,0:T(8,128)(2,1)}, u32[]{:S(2)}) copy-start(bf16[512,512]{1,0:T(8,128)(2,1)} %param.22) | copy-start | bytes 1572868
  0.0 1.2 copy-start.10
  0.0 11.7 %copy-start.12 = (f32[3,128]{1,0:T(4,128)S(1)}, f32[3,128]{1,0:T(4,128)}, u32[]{:S(2)}) copy-start(f32[3,128]{1,0:T(4,128)} %param.17) | copy-start | bytes 4612
  1.3 17.1 %copy-start.7 = (f32[2,1,2,256,128]{4,3,2,1,0:T(8,128)S(1)}, f32[2,1,2,256,128]{4,3,2,1,0:T(8,128)}, u32[]{:S(2)}) copy-start(f32[2,1,2,256,128]{4,3,2,1,0:T(8,128)} %param.20) | copy-start | bytes 1572868
  11.7 6.6 %copy-start.11 = (f32[3,3,128]{2,1,0:T(4,128)S(1)}, f32[3,3,128]{2,1,0:T(4,128)}, u32[]{:S(2)}) copy-start(f32[3,3,128]{2,1,0:T(4,128)} %param.18) | copy-start | bytes 13828
  12.1 9.6 %collective-permute-start = (bf16[2,3,128]{2,0,1:T(2,128)(2,1)S(1)}, bf16[2,3,128]{2,0,1:T(2,128)(2,1)S(1)}, u32[]{:S(2)}, u32[]{:S(2)}) collective-permute-start(bf16[2,3,128]{2,0,1:T(2,128)(2,1)S(1)} %slice.60), channel_id=1, source_target_pairs={{0,4},{4,8},{8,12},{12,16},{16,20},{20,24},{24,28},{28,32},{32,36}... | collective-permute-start | bytes 4616 | tf_op jit(solution)/shard_map/ppermute | solution.py:15
  21.7 0.7 copy-start.13
  24.3 59.9 %all-to-all-start = ((f32[1,1536,128]{1,0,2:T(1,128)}), f32[1,1536,128]{1,0,2:T(1,128)S(1)}, u32[]{:S(2)}, u32[]{:S(2)}) async-start(f32[1,1536,128]{1,0,2:T(1,128)} %broadcast_in_dim.4), calls=%async_computation | async-start | bytes 1572864 | tf_op jit(solution)/shard_map/all_to_all | solution.py:102
  42.5 0.7 copy-start.15
  85.1 0.9 copy-start.9
  86.0 0.9 copy-start.8
  86.1 1.3 copy-start.6
  87.0 1.0 copy-start.2
  87.0 1.0 copy-start.3
  88.0 0.9 copy-start.1
  88.0 1.0 copy-start.5
  89.0 0.9 copy-start.4
  96.6 24.0 %all-to-all-start.1 = ((bf16[128,2,128]{2,1,0:T(2,128)(2,1)}), bf16[128,2,128]{2,1,0:T(2,128)(2,1)S(1)}, u32[]{:S(2)}, u32[]{:S(2)}) async-start(bf16[128,2,128]{2,1,0:T(2,128)(2,1)} %reshape.31), calls=%async_computation.1 | async-start | bytes 131072 | tf_op jit(solution)/shard_map/all_to_all | solution.py:114
  120.7 9.8 %copy-start.14 = (f32[128]{0:T(128)S(1)}, f32[128]{0:T(128)}, u32[]{:S(2)}) copy-start(f32[128]{0:T(128)} %param.23) | copy-start | bytes 1540

commit v3 on v2

--- a/solution.py
+++ b/solution.py
@@ -82,7 +82,8 @@
         flat_weight,
         preferred_element_type=jnp.float32,
     )
-    projected = (projected.reshape(steps_dev, 3, channels) + proj_bias).astype(jnp.bfloat16)
+    projected = lax.reduce_precision(projected.reshape(steps_dev, 3, channels) + proj_bias, 8, 7)
+    projected = projected.astype(jnp.bfloat16)
     taps_count = short_taps.shape[0]
     earlier = from_behind(projected[steps_dev - taps_count + 1:], "tm", 1)
     extended = jnp.concatenate([earlier, projected], 0).astype(jnp.float32)
@@ -93,18 +94,18 @@
             + short_taps[offset]
             * extended[taps_count - 1 - offset: taps_count - 1 - offset + steps_dev]
         )
-    streams = streams.astype(jnp.bfloat16)
-    gate_out = streams[:, 0]
-    mixed_in = (streams[:, 1].astype(jnp.float32) * streams[:, 2].astype(jnp.float32)).astype(jnp.bfloat16)
+    streams = lax.reduce_precision(streams, 8, 7)
+    gate_out = streams[:, 0].astype(jnp.bfloat16)
+    mixed_in = (streams[:, 1] * streams[:, 2]).astype(jnp.bfloat16)
 
     send = jnp.concatenate(
-        [spectrum.reshape(-1, channels), mixed_in.astype(jnp.float32), gate_out.astype(jnp.float32)], 0)
+        [spectrum.reshape(-1, channels).astype(jnp.bfloat16), mixed_in, gate_out], 0)
     recv = lax.all_to_all(send[None], "tm", 2, 0, tiled=True)[:, :, 0]
     spec_len = spectrum.size // channels
-    h = recv[:, :spec_len].reshape(tm_count, 2, spec_len // 2)
+    h = recv[:, :spec_len].astype(jnp.float32).reshape(tm_count, 2, spec_len // 2)
     h = jnp.stack([h[:, 0].reshape(2 * tm_count, steps_dev), h[:, 1].reshape(2 * tm_count, steps_dev)])
     signal_bf = recv[:, spec_len:spec_len + steps_dev]
-    gate_own = recv[:, spec_len + steps_dev:]
+    gate_own = recv[:, spec_len + steps_dev:].astype(jnp.float32)
 
     signal = signal_bf.astype(jnp.float32)
     convolved = long_conv(signal, h, tab)

time: 133 us -> 119 us (0.89)
  waiting for transfers between devices: 58.3 us -> 42.2 us
  other arithmetic: 1.29 us -> 4.28 us
    all_to_all x1, waiting for transfers between devices: 40.4 us -> 24.1 us  [shards(): recv = lax.all_to_all(send[None], 'tm', 2, 0, tiled=True)[:, :, 0]]
    unnamed x1 -> x2, other arithmetic: 1.01 us -> 4.01 us
    unnamed x39 -> x41, local copies, waits for them, and re-layouts: 7.24 us -> 7.93 us
where the time goes in v3:
time: 119 us; the launch traced here: 117 us
  waiting for transfers between devices  42.2 us (35%)
  starting transfers between devices  33.4 us (28%)
  blocking collectives  20.1 us (17%)
  local copies, waits for them, and re-layouts  10.2 us (9%)
  matrix products  6.68 us (6%)
  other arithmetic  4.28 us (4%)
    all_to_all x1, waiting for transfers between devices, shards(): recv = lax.all_to_all(send[None], 'tm', 2, 0, tiled=True)[:, :, 0]  24.1 us
    all_to_all x1, starting transfers between devices, shards(): recv = lax.all_to_all(send[None], 'tm', 2, 0, tiled=True)[:, :, 0]  18.2 us
    all_to_all x1, waiting for transfers between devices, shards(): gated = lax.all_to_all(gated[:, :, None], 'tm', 0, 2, tiled=True)  14.8 us
    all_gather x1, blocking collectives, shards(): lax.all_gather(series, 'chan', axis=1, tiled=True)  10.3 us
    all_gather x1, blocking collectives, shards(): gated = lax.all_gather(gated[0], 'chan', axis=1, tiled=True)  9.81 us
    all_to_all x1, starting transfers between devices, shards(): gated = lax.all_to_all(gated[:, :, None], 'tm', 0, 2, tiled=True)  8.93 us
    unnamed x41, local copies, waits for them, and re-layouts  7.93 us
    ppermute x1, starting transfers between devices, from_behind(): return lax.ppermute(array, axis, pairs)  6.27 us
  transfers between devices with their start and end apart: 3, of which 3 were waited for; matrix products, arithmetic and copies ran while one was open for 1% of the time, Pallas kernels for 0%

profile of v3, /device:TPU:1, one launch (start us, length us, event | category | flops | bytes accessed | tf_op | source)
XLA Modules:
  0.0 117.3 jit_solution(11269751780875471940)
XLA Ops:
  0.0 1.2 %copy.32 = bf16[512,3,128]{0,2,1:T(8,128)(2,1)S(1)} copy(bf16[512,3,128]{2,0,1:T(8,128)(2,1)} %param.16) | data formatting | bytes 786432 | tf_op args[1]
  1.3 10.3 %all_gather.6 = bf16[256,512]{1,0:T(8,128)(2,1)S(1)} all-gather(bf16[256,128]{1,0:T(8,128)(2,1)S(1)} %copy-done.10), channel_id=1, replica_groups=mesh['tm'=128,'chan'=4] {'chan'}, dimensions={1}, use_global_device_ids=true | all-gather | bytes 327680 | tf_op jit(solution)/shard_map/all_gather | solution.py:81
  11.6 0.3 fusion.1
  11.9 6.3 %collective-permute-start = (bf16[2,3,128]{2,0,1:T(2,128)(2,1)S(1)}, bf16[2,3,128]{2,0,1:T(2,128)(2,1)S(1)}, u32[]{:S(2)}, u32[]{:S(2)}) collective-permute-start(bf16[2,3,128]{2,0,1:T(2,128)(2,1)S(1)} %slice.61), channel_id=1, source_target_pairs={{0,4},{4,8},{8,12},{12,16},{16,20},{20,24},{24,28},{28,32},{32,36}... | collective-permute-start | bytes 4616 | tf_op jit(solution)/shard_map/ppermute | solution.py:15
  18.3 3.2 %collective-permute-done = bf16[2,3,128]{2,0,1:T(2,128)(2,1)S(1)} collective-permute-done((bf16[2,3,128]{2,0,1:T(2,128)(2,1)S(1)}, bf16[2,3,128]{2,0,1:T(2,128)(2,1)S(1)}, u32[]{:S(2)}, u32[]{:S(2)}) %collective-permute-start) | collective-permute-done | bytes 1568 | tf_op jit(solution)/shard_map/ppermute | solution.py:15
  21.6 0.7 copy-done.12
  22.2 0.1 fusion.10
  22.5 0.7 copy.33
  23.2 0.5 broadcast.5
  23.7 3.0 %reduce = bf16[128,1536]{1,0:T(8,128)(2,1)S(1)} reduce(bf16[128,1,1536]{2,1,0:T(2,128)(2,1)S(1)} %bitcast.85, bf16[]{:T(256)} %broadcast.5), dimensions={1}, to_apply=%bitcast.62.reduce_sub_computation | reduce | bytes 786434
  26.7 0.8 reshape.28
  27.5 18.2 %all-to-all-start = ((bf16[128,2,768]{2,1,0:T(2,128)(2,1)}), bf16[128,2,768]{2,1,0:T(2,128)(2,1)S(1)}, u32[]{:S(2)}, u32[]{:S(2)}) async-start(bf16[128,2,768]{2,1,0:T(2,128)(2,1)} %reshape.28), calls=%async_computation | async-start | bytes 786432 | tf_op jit(solution)/shard_map/all_to_all | solution.py:103
  45.8 0.6 copy-done.15
  46.5 0.6 dynamic_slice.7
  47.1 24.1 %all-to-all-done = bf16[128,2,768]{2,1,0:T(2,128)(2,1)S(1)} async-done(((bf16[128,2,768]{2,1,0:T(2,128)(2,1)}), bf16[128,2,768]{2,1,0:T(2,128)(2,1)S(1)}, u32[]{:S(2)}, u32[]{:S(2)}) %all-to-all-start) | async-done | bytes 393248 | tf_op jit(solution)/shard_map/all_to_all | solution.py:103
  71.2 0.3 reshape.29
  71.5 0.7 copy.34
  72.2 0.1 copy.42
  72.4 0.1 copy.41
  72.6 0.0 copy-start.9
  72.6 0.0 copy-start.7
  72.6 0.8 copy-done.9
  73.5 0.3 convolution_negate_fusion
  73.8 0.0 copy-start.2
  73.8 0.3 fusion.30
  74.1 0.4 copy-done.3
  74.4 0.1 copy-done.6
  74.5 0.2 copy-done.2
  74.8 0.4 fusion.25
  75.2 0.5 copy-done.1
  75.7 0.1 copy-done.5
  75.8 0.4 fusion.26
  76.2 0.5 copy-done.4
  76.7 0.4 convolution_add_fusion.2
  77.1 0.4 multiply_subtract_fusion
  77.6 0.4 fusion.35
  77.9 0.4 fusion.34
  78.3 0.4 convolution_add_fusion.1
  78.7 0.4 convolution_subtract_fusion
  79.1 0.6 fusion.19
  79.7 1.2 %fusion.8 = bf16[128,256,1]{0,1,2:T(8,128)(2,1)S(1)} fusion(f32[256,128]{1,0:T(8,128)S(1)} %fusion.19, f32[256,128]{1,0:T(8,128)S(1)} %copy-done.9, f32[256,256]{1,0:T(8,128)S(1)} %convolution_subtract_fusion, f32[256,256]{1,0:T(8,128)S(1)} %copy-done.1, f32[256,256]{1,0:T(8,128)S(1)} %convolution_add_fusion.1, f32[256,256]{1,0:T(8,128)S(1)} %copy-done.3, ...), kind=kOutput, calls=%fused_computation.16 | convolution fusion | flops 101122048 | bytes 1507332 | tf_op jit(solution)/shard_map/dot_general | solution.py:66
  80.9 0.1 copy.38
  81.1 1.0 reduce.1
  82.1 0.7 reshape.30
  82.7 8.9 %all-to-all-start.1 = ((bf16[128,2,128]{2,1,0:T(2,128)(2,1)}), bf16[128,2,128]{2,1,0:T(2,128)(2,1)S(1)}, u32[]{:S(2)}, u32[]{:S(2)}) async-start(bf16[128,2,128]{2,1,0:T(2,128)(2,1)} %reshape.30), calls=%async_computation.1 | async-start | bytes 131072 | tf_op jit(solution)/shard_map/all_to_all | solution.py:115
  91.7 14.8 %all-to-all-done.1 = bf16[128,2,128]{2,1,0:T(2,128)(2,1)S(1)} async-done(((bf16[128,2,128]{2,1,0:T(2,128)(2,1)}), bf16[128,2,128]{2,1,0:T(2,128)(2,1)S(1)}, u32[]{:S(2)}, u32[]{:S(2)}) %all-to-all-start.1) | async-done | bytes 65568 | tf_op jit(solution)/shard_map/all_to_all | solution.py:115
  106.5 9.8 %all-gather = bf16[1,256,512,1]{1,2,3,0:T(8,128)(2,1)S(1)} all-gather(bf16[1,256,128,1]{1,2,3,0:T(8,128)(2,1)S(1)} %bitcast.95), channel_id=2, replica_groups=mesh['tm'=128,'chan'=4] {'chan'}, dimensions={2}, use_global_device_ids=true | all-gather | bytes 327680 | tf_op jit(solution)/shard_map/all_gather | solution.py:116
  116.4 0.9 fusion.7
  (33 shorter events, 0.4 us)
Async XLA Ops:
  0.0 116.4 %copy-start = (bf16[512,512]{1,0:T(8,128)(2,1)S(1)}, bf16[512,512]{1,0:T(8,128)(2,1)}, u32[]{:S(2)}) copy-start(bf16[512,512]{1,0:T(8,128)(2,1)} %param.22) | copy-start | bytes 1572868
  0.0 1.2 %copy-start.10 = (bf16[256,128]{1,0:T(8,128)(2,1)S(1)}, bf16[256,128]{1,0:T(8,128)(2,1)}, u32[]{:S(2)}) copy-start(bf16[256,128]{1,0:T(8,128)(2,1)} %param.15) | copy-start | bytes 196612
  1.2 10.3 %copy-start.14 = (f32[3,128]{1,0:T(4,128)S(1)}, f32[3,128]{1,0:T(4,128)}, u32[]{:S(2)}) copy-start(f32[3,128]{1,0:T(4,128)} %param.17) | copy-start | bytes 4612
  11.6 6.6 %copy-start.11 = (f32[3,3,128]{2,1,0:T(4,128)S(1)}, f32[3,3,128]{2,1,0:T(4,128)}, u32[]{:S(2)}) copy-start(f32[3,3,128]{2,1,0:T(4,128)} %param.18) | copy-start | bytes 13828
  11.6 6.6 %copy-start.8 = (f32[2,1,2,256,128]{4,3,2,1,0:T(8,128)S(1)}, f32[2,1,2,256,128]{4,3,2,1,0:T(8,128)}, u32[]{:S(2)}) copy-start(f32[2,1,2,256,128]{4,3,2,1,0:T(8,128)} %param.20) | copy-start | bytes 1572868
  11.9 9.6 %collective-permute-start = (bf16[2,3,128]{2,0,1:T(2,128)(2,1)S(1)}, bf16[2,3,128]{2,0,1:T(2,128)(2,1)S(1)}, u32[]{:S(2)}, u32[]{:S(2)}) collective-permute-start(bf16[2,3,128]{2,0,1:T(2,128)(2,1)S(1)} %slice.61), channel_id=1, source_target_pairs={{0,4},{4,8},{8,12},{12,16},{16,20},{20,24},{24,28},{28,32},{32,36}... | collective-permute-start | bytes 4616 | tf_op jit(solution)/shard_map/ppermute | solution.py:15
  21.6 0.7 copy-start.12
  27.5 43.6 %all-to-all-start = ((bf16[128,2,768]{2,1,0:T(2,128)(2,1)}), bf16[128,2,768]{2,1,0:T(2,128)(2,1)S(1)}, u32[]{:S(2)}, u32[]{:S(2)}) async-start(bf16[128,2,768]{2,1,0:T(2,128)(2,1)} %reshape.28), calls=%async_computation | async-start | bytes 786432 | tf_op jit(solution)/shard_map/all_to_all | solution.py:103
  45.8 0.7 copy-start.15
  72.6 0.9 copy-start.9
  72.6 1.2 %copy-start.7 = (f32[256,128]{1,0:T(8,128)S(1)}, f32[256,128]{1,0:T(8,128)}, u32[]{:S(2)}) copy-start(f32[256,128]{1,0:T(8,128)} %constant.33.clone) | copy-start | bytes 393220
  73.5 1.0 copy-start.3
  73.5 1.0 copy-start.6
  73.8 1.0 copy-start.2
  74.8 0.9 copy-start.1
  74.8 1.0 copy-start.5
  75.8 0.9 copy-start.4
  82.7 23.8 %all-to-all-start.1 = ((bf16[128,2,128]{2,1,0:T(2,128)(2,1)}), bf16[128,2,128]{2,1,0:T(2,128)(2,1)S(1)}, u32[]{:S(2)}, u32[]{:S(2)}) async-start(bf16[128,2,128]{2,1,0:T(2,128)(2,1)} %reshape.30), calls=%async_computation.1 | async-start | bytes 131072 | tf_op jit(solution)/shard_map/all_to_all | solution.py:115
  106.5 9.8 %copy-start.13 = (f32[128]{0:T(128)S(1)}, f32[128]{0:T(128)}, u32[]{:S(2)}) copy-start(f32[128]{0:T(128)} %param.23) | copy-start | bytes 1540

commit v4 on v3

--- a/solution.py
+++ b/solution.py
@@ -43,6 +43,12 @@
     )
 
 
+def gather_chan(x):
+    count = lax.axis_size("chan")
+    wide = jnp.broadcast_to(x[:, None, :], (x.shape[0], count, x.shape[1]))
+    return lax.all_to_all(wide, "chan", 1, 1, tiled=True).reshape(x.shape[0], count * x.shape[1])
+
+
 def mm(a, b):
     return jnp.dot(a, b, precision=HI, preferred_element_type=jnp.float32)
 
@@ -77,16 +83,17 @@
     tab = dft_tables(tm_count, steps_dev)
 
     flat_weight = proj_weight.reshape(model_width, 3 * channels)
-    projected = jnp.dot(
-        lax.all_gather(series, "chan", axis=1, tiled=True),
-        flat_weight,
-        preferred_element_type=jnp.float32,
-    )
-    projected = lax.reduce_precision(projected.reshape(steps_dev, 3, channels) + proj_bias, 8, 7)
-    projected = projected.astype(jnp.bfloat16)
     taps_count = short_taps.shape[0]
-    earlier = from_behind(projected[steps_dev - taps_count + 1:], "tm", 1)
-    extended = jnp.concatenate([earlier, projected], 0).astype(jnp.float32)
+    halo = taps_count - 1
+    rows = gather_chan(series)
+    earlier = from_behind(rows[steps_dev - halo:], "tm", 1)
+    projected = jnp.concatenate([
+        jnp.dot(earlier, flat_weight, preferred_element_type=jnp.float32),
+        jnp.dot(rows, flat_weight, preferred_element_type=jnp.float32)], 0)
+    projected = lax.reduce_precision(projected.reshape(steps_dev + halo, 3, channels) + proj_bias, 8, 7)
+    first = lax.axis_index("tm") == 0
+    keep = jnp.logical_not(first) | (jnp.arange(steps_dev + halo) >= halo)
+    extended = jnp.where(keep[:, None, None], projected, 0.0)
     streams = short_bias + short_taps[0] * extended[taps_count - 1:]
     for offset in range(1, taps_count):
         streams = (
@@ -113,7 +120,7 @@
     gated = ((convolved + skip * signal) * gate_own).astype(jnp.bfloat16)
 
     gated = lax.all_to_all(gated[:, :, None], "tm", 0, 2, tiled=True)
-    gated = lax.all_gather(gated[0], "chan", axis=1, tiled=True)
+    gated = gather_chan(gated[0])
     column_start = lax.axis_index("chan") * channels
     weight_cols = lax.dynamic_slice_in_dim(out_weight, column_start, channels, 1)
     mixed_out = jnp.dot(gated, weight_cols, preferred_element_type=jnp.float32) + out_bias

time: 119 us -> 119 us (level)
  waiting for transfers between devices: 42.2 us -> 36.5 us
  local copies, waits for them, and re-layouts: 10.2 us -> 14.2 us
  blocking collectives: 20.1 us -> 23.6 us
  starting transfers between devices: 33.4 us -> 31.7 us
    all_to_all x0 -> x1, blocking collectives: none -> 23.6 us  [shards(): gated = lax.all_to_all(gated[:, :, None], 'tm', 0, 2, tiled=True)]
    all_gather x2 -> x0, blocking collectives: 20.1 us -> none  [the longest x1 10.3 us: shards(): lax.all_gather(series, 'chan', axis=1, tiled=True)]
    all_to_all x1 -> x2, waiting for transfers between devices: 14.8 us -> 9.67 us  [gather_chan(): lax.all_to_all(wide, 'chan', 1, 1, tiled=True)]
    broadcast_in_dim x0 -> x3, local copies, waits for them, and re-layouts: none -> 2.52 us  [gather_chan(): wide = jnp.broadcast_to(x[:, None, :], (x.shape[0], count, x.shape[1]))]
    all_to_all x1 -> x2, starting transfers between devices: 8.93 us -> 8.23 us  [gather_chan(): lax.all_to_all(wide, 'chan', 1, 1, tiled=True)]
  transfers between devices with their start and end apart: 3 -> 4, of which waited for: 3 -> 4; matrix products, arithmetic and copies ran while one was open for 1% -> 1% of each run, Pallas kernels for 0% -> 0%
where the time goes in v4:
time: 119 us; the launch traced here: 118 us
  waiting for transfers between devices  36.5 us (31%)
  starting transfers between devices  31.7 us (27%)
  blocking collectives  23.6 us (20%)
  local copies, waits for them, and re-layouts  14.2 us (12%)
  matrix products  6.99 us (6%)
  other arithmetic  4.93 us (4%)
    all_to_all x1, waiting for transfers between devices, shards(): recv = lax.all_to_all(send[None], 'tm', 2, 0, tiled=True)[:, :, 0]  24.1 us
    all_to_all x1, blocking collectives, shards(): gated = lax.all_to_all(gated[:, :, None], 'tm', 0, 2, tiled=True)  23.6 us
    all_to_all x1, starting transfers between devices, shards(): recv = lax.all_to_all(send[None], 'tm', 2, 0, tiled=True)[:, :, 0]  18.3 us
    all_to_all x2, waiting for transfers between devices, gather_chan(): lax.all_to_all(wide, 'chan', 1, 1, tiled=True)  9.67 us
    unnamed x41, local copies, waits for them, and re-layouts  8.88 us
    all_to_all x2, starting transfers between devices, gather_chan(): lax.all_to_all(wide, 'chan', 1, 1, tiled=True)  8.23 us
    ppermute x1, starting transfers between devices, from_behind(): return lax.ppermute(array, axis, pairs)  5.19 us
    unnamed x2, other arithmetic  4.01 us
  transfers between devices with their start and end apart: 4, of which 4 were waited for; matrix products, arithmetic and copies ran while one was open for 1% of the time, Pallas kernels for 0%

profile of v4, /device:TPU:1, one launch (start us, length us, event | category | flops | bytes accessed | tf_op | source)
XLA Modules:
  0.0 118.4 jit_solution(16485873739298068994)
XLA Ops:
  0.0 1.6 %broadcast_in_dim.36 = bf16[256,4,128]{2,0,1:T(8,128)(2,1)} broadcast(bf16[256,128]{1,0:T(8,128)(2,1)} %param.15), dimensions={0,2} | broadcast | bytes 327680 | tf_op jit(solution)/shard_map/broadcast_in_dim | solution.py:48
  1.7 4.8 %all-to-all-start = ((bf16[256,4,128]{2,0,1:T(8,128)(2,1)}), bf16[256,4,128]{2,0,1:T(8,128)(2,1)S(1)}, u32[]{:S(2)}, u32[]{:S(2)}) async-start(bf16[256,4,128]{2,0,1:T(8,128)(2,1)} %broadcast_in_dim.36), calls=%async_computation | async-start | bytes 524288 | tf_op jit(solution)/shard_map/all_to_all | solution.py:49
  6.7 0.8 copy-done.8
  7.6 0.6 copy-done.11
  8.2 3.8 %all-to-all-done = bf16[256,4,128]{2,0,1:T(8,128)(2,1)S(1)} async-done(((bf16[256,4,128]{2,0,1:T(8,128)(2,1)}), bf16[256,4,128]{2,0,1:T(8,128)(2,1)S(1)}, u32[]{:S(2)}, u32[]{:S(2)}) %all-to-all-start) | async-done | bytes 262176 | tf_op jit(solution)/shard_map/all_to_all | solution.py:49
  12.0 5.2 %collective-permute-start = (bf16[2,512]{1,0:T(2,128)(2,1)S(1)}, bf16[2,512]{1,0:T(2,128)(2,1)S(1)}, u32[]{:S(2)}, u32[]{:S(2)}) collective-permute-start(bf16[2,512]{1,0:T(2,128)(2,1)S(1)} %slice_bitcast_fusion), channel_id=1, source_target_pairs={{0,4},{4,8},{8,12},{12,16},{16,20},{20,24},{24,28},{28,32},{32,36}... | collective-permute-start | bytes 6152 | tf_op jit(solution)/shard_map/ppermute | solution.py:15
  17.4 0.3 fusion.29
  17.7 2.8 %collective-permute-done = bf16[2,512]{1,0:T(2,128)(2,1)S(1)} collective-permute-done((bf16[2,512]{1,0:T(2,128)(2,1)S(1)}, bf16[2,512]{1,0:T(2,128)(2,1)S(1)}, u32[]{:S(2)}, u32[]{:S(2)}) %collective-permute-start) | collective-permute-done | bytes 2080 | tf_op jit(solution)/shard_map/ppermute | solution.py:15
  20.5 0.2 fusion.28
  21.0 0.5 copy-done.12
  21.5 0.3 reduce-precision_select_fusion
  21.8 0.7 copy-done.13
  22.5 0.2 fusion.8
  22.8 0.2 fusion.18
  23.1 0.7 copy.37
  23.8 0.5 broadcast.14
  24.4 3.0 %reduce = bf16[128,1536]{1,0:T(8,128)(2,1)S(1)} reduce(bf16[128,1,1536]{2,1,0:T(2,128)(2,1)S(1)} %bitcast.85, bf16[]{:T(256)} %broadcast.14), dimensions={1}, to_apply=%bitcast.56.reduce_sub_computation | reduce | bytes 786434
  27.4 0.8 reshape.44
  28.2 18.3 %all-to-all-start.1 = ((bf16[128,2,768]{2,1,0:T(2,128)(2,1)}), bf16[128,2,768]{2,1,0:T(2,128)(2,1)S(1)}, u32[]{:S(2)}, u32[]{:S(2)}) async-start(bf16[128,2,768]{2,1,0:T(2,128)(2,1)} %reshape.44), calls=%async_computation.1 | async-start | bytes 786432 | tf_op jit(solution)/shard_map/all_to_all | solution.py:110
  46.5 0.6 copy-done.15
  47.2 0.6 dynamic_slice.7
  47.8 24.1 %all-to-all-done.1 = bf16[128,2,768]{2,1,0:T(2,128)(2,1)S(1)} async-done(((bf16[128,2,768]{2,1,0:T(2,128)(2,1)}), bf16[128,2,768]{2,1,0:T(2,128)(2,1)S(1)}, u32[]{:S(2)}, u32[]{:S(2)}) %all-to-all-start.1) | async-done | bytes 393248 | tf_op jit(solution)/shard_map/all_to_all | solution.py:110
  71.9 0.3 reshape.45
  72.2 0.7 copy.38
  73.3 0.8 copy-done.9
  74.2 0.3 convolution_negate_fusion
  74.5 0.3 fusion.23
  74.8 0.4 copy-done.3
  75.2 0.2 copy-done.2
  75.5 0.4 fusion.20
  75.9 0.6 copy-done.1
  76.5 0.4 fusion.21
  76.9 0.6 copy-done.4
  77.4 0.4 convolution_add_fusion.1
  77.8 0.4 multiply_subtract_fusion
  78.3 0.4 fusion.31
  78.6 0.4 fusion.30
  79.0 0.4 convolution_add_fusion
  79.4 0.4 convolution_subtract_fusion
  79.8 0.6 fusion.14
  80.4 1.3 %fusion.6 = bf16[128,256,1]{0,1,2:T(8,128)(2,1)S(1)} fusion(f32[256,128]{1,0:T(8,128)S(1)} %fusion.14, f32[256,128]{1,0:T(8,128)S(1)} %copy-done.9, f32[256,256]{1,0:T(8,128)S(1)} %convolution_subtract_fusion, f32[256,256]{1,0:T(8,128)S(1)} %copy-done.1, f32[256,256]{1,0:T(8,128)S(1)} %convolution_add_fusion, f32[256,256]{1,0:T(8,128)S(1)} %copy-done.3, ...), kind=kOutput, calls=%fused_computation.13 | convolution fusion | flops 101122048 | bytes 1507332 | tf_op jit(solution)/shard_map/dot_general | solution.py:72
  81.9 1.0 reduce.1
  82.9 23.6 %all_to_all.40 = bf16[128,2,128]{2,1,0:T(2,128)(2,1)S(1)} all-to-all(bf16[128,2,128]{2,1,0:T(2,128)(2,1)S(1)} %reshape.46), channel_id=1, replica_groups=mesh['tm'=128,'chan'=4] {'tm'}, dimensions={0} | all-to-all | bytes 131072 | tf_op jit(solution)/shard_map/all_to_all | solution.py:122
  106.7 0.7 broadcast_in_dim.41
  107.4 3.4 %all-to-all-start.3 = ((bf16[256,4,128]{2,0,1:T(8,128)(2,1)}), bf16[256,4,128]{2,0,1:T(8,128)(2,1)S(1)}, u32[]{:S(2)}, u32[]{:S(2)}) async-start(bf16[256,4,128]{2,0,1:T(8,128)(2,1)} %broadcast_in_dim.41), calls=%async_computation.3 | async-start | bytes 524288 | tf_op jit(solution)/shard_map/all_to_all | solution.py:49
  110.9 5.9 %all-to-all-done.3 = bf16[256,4,128]{2,0,1:T(8,128)(2,1)S(1)} async-done(((bf16[256,4,128]{2,0,1:T(8,128)(2,1)}), bf16[256,4,128]{2,0,1:T(8,128)(2,1)S(1)}, u32[]{:S(2)}, u32[]{:S(2)}) %all-to-all-start.3) | async-done | bytes 262176 | tf_op jit(solution)/shard_map/all_to_all | solution.py:49
  116.9 0.6 copy-done.14
  117.5 0.9 fusion.5
  (43 shorter events, 1.8 us)
Async XLA Ops:
  0.0 116.9 %copy-start = (bf16[512,512]{1,0:T(8,128)(2,1)S(1)}, bf16[512,512]{1,0:T(8,128)(2,1)}, u32[]{:S(2)}) copy-start(bf16[512,512]{1,0:T(8,128)(2,1)} %param.22) | copy-start | bytes 1572868
  0.0 6.5 %copy-start.10 = (bf16[512,3,128]{2,0,1:T(8,128)(2,1)S(1)}, bf16[512,3,128]{2,0,1:T(8,128)(2,1)}, u32[]{:S(2)}) copy-start(bf16[512,3,128]{2,0,1:T(8,128)(2,1)} %param.16) | copy-start | bytes 1179652
  1.7 10.4 %all-to-all-start = ((bf16[256,4,128]{2,0,1:T(8,128)(2,1)}), bf16[256,4,128]{2,0,1:T(8,128)(2,1)S(1)}, u32[]{:S(2)}, u32[]{:S(2)}) async-start(bf16[256,4,128]{2,0,1:T(8,128)(2,1)} %broadcast_in_dim.36), calls=%async_computation | async-start | bytes 524288 | tf_op jit(solution)/shard_map/all_to_all | solution.py:49
  6.5 1.0 copy-start.8
  7.5 0.7 copy-start.11
  12.0 8.5 %collective-permute-start = (bf16[2,512]{1,0:T(2,128)(2,1)S(1)}, bf16[2,512]{1,0:T(2,128)(2,1)S(1)}, u32[]{:S(2)}, u32[]{:S(2)}) collective-permute-start(bf16[2,512]{1,0:T(2,128)(2,1)S(1)} %slice_bitcast_fusion), channel_id=1, source_target_pairs={{0,4},{4,8},{8,12},{12,16},{16,20},{20,24},{24,28},{28,32},{32,36}... | collective-permute-start | bytes 6152 | tf_op jit(solution)/shard_map/ppermute | solution.py:15
  20.8 0.7 copy-start.12
  21.8 0.7 copy-start.13
  28.2 43.7 %all-to-all-start.1 = ((bf16[128,2,768]{2,1,0:T(2,128)(2,1)}), bf16[128,2,768]{2,1,0:T(2,128)(2,1)S(1)}, u32[]{:S(2)}, u32[]{:S(2)}) async-start(bf16[128,2,768]{2,1,0:T(2,128)(2,1)} %reshape.44), calls=%async_computation.1 | async-start | bytes 786432 | tf_op jit(solution)/shard_map/all_to_all | solution.py:110
  46.5 0.7 copy-start.15
  73.3 0.9 copy-start.9
  73.3 1.2 copy-start.7
  74.2 1.0 copy-start.3
  74.2 1.0 copy-start.6
  74.5 1.0 copy-start.2
  75.5 0.9 copy-start.1
  75.5 1.0 copy-start.5
  76.5 0.9 copy-start.4
  107.4 9.3 %all-to-all-start.3 = ((bf16[256,4,128]{2,0,1:T(8,128)(2,1)}), bf16[256,4,128]{2,0,1:T(8,128)(2,1)S(1)}, u32[]{:S(2)}, u32[]{:S(2)}) async-start(bf16[256,4,128]{2,0,1:T(8,128)(2,1)} %broadcast_in_dim.41), calls=%async_computation.3 | async-start | bytes 524288 | tf_op jit(solution)/shard_map/all_to_all | solution.py:49
  116.9 0.7 copy-start.14

commit v5 on v4

--- a/solution.py
+++ b/solution.py
@@ -1,10 +1,9 @@
-import math
-
 import jax
 import jax.numpy as jnp
 import numpy as np
 from jax import lax
 from jax.sharding import PartitionSpec as P
+
 
 HI = lax.Precision.HIGHEST
 
@@ -85,7 +84,8 @@
     flat_weight = proj_weight.reshape(model_width, 3 * channels)
     taps_count = short_taps.shape[0]
     halo = taps_count - 1
-    rows = gather_chan(series)
+    h_recv = lax.all_to_all(spectrum.reshape(1, -1, channels).astype(jnp.bfloat16), "tm", 2, 0, tiled=True)
+    rows = lax.all_gather(series, "chan", axis=1, tiled=True)
     earlier = from_behind(rows[steps_dev - halo:], "tm", 1)
     projected = jnp.concatenate([
         jnp.dot(earlier, flat_weight, preferred_element_type=jnp.float32),
@@ -105,14 +105,14 @@
     gate_out = streams[:, 0].astype(jnp.bfloat16)
     mixed_in = (streams[:, 1] * streams[:, 2]).astype(jnp.bfloat16)
 
-    send = jnp.concatenate(
-        [spectrum.reshape(-1, channels).astype(jnp.bfloat16), mixed_in, gate_out], 0)
+    send = jnp.concatenate([mixed_in, gate_out], 0)
+    h_recv, send = lax.optimization_barrier((h_recv, send))
     recv = lax.all_to_all(send[None], "tm", 2, 0, tiled=True)[:, :, 0]
     spec_len = spectrum.size // channels
-    h = recv[:, :spec_len].astype(jnp.float32).reshape(tm_count, 2, spec_len // 2)
+    h = h_recv[:, :, 0].astype(jnp.float32).reshape(tm_count, 2, spec_len // 2)
     h = jnp.stack([h[:, 0].reshape(2 * tm_count, steps_dev), h[:, 1].reshape(2 * tm_count, steps_dev)])
-    signal_bf = recv[:, spec_len:spec_len + steps_dev]
-    gate_own = recv[:, spec_len + steps_dev:].astype(jnp.float32)
+    signal_bf = recv[:, :steps_dev]
+    gate_own = recv[:, steps_dev:].astype(jnp.float32)
 
     signal = signal_bf.astype(jnp.float32)
     convolved = long_conv(signal, h, tab)

time: 119 us -> 125 us (1.050)
  waiting for transfers between devices: 36.5 us -> 21.4 us
  starting transfers between devices: 31.7 us -> 45 us
  blocking collectives: 23.6 us -> 32.5 us
  local copies, waits for them, and re-layouts: 14.2 us -> 12.1 us
  other arithmetic: 4.93 us -> 6.57 us
    all_to_all x0 -> x1, starting transfers between devices: none -> 20.7 us  [shards(): lax.all_to_all(spectrum.reshape(1, -1, channels).astype(jnp.bfloat16), 't...]
    all_gather x0 -> x1, blocking collectives: none -> 10.6 us  [shards(): rows = lax.all_gather(series, 'chan', axis=1, tiled=True)]
    all_to_all x1, waiting for transfers between devices: 24.1 us -> 14.4 us  [shards(): recv = lax.all_to_all(send[None], 'tm', 2, 0, tiled=True)[:, :, 0]]
    all_to_all x2 -> x1, starting transfers between devices: 8.23 us -> 3.4 us  [gather_chan(): lax.all_to_all(wide, 'chan', 1, 1, tiled=True)]
    all_to_all x2 -> x1, waiting for transfers between devices: 9.67 us -> 5.88 us  [gather_chan(): lax.all_to_all(wide, 'chan', 1, 1, tiled=True)]
    ppermute x1, waiting for transfers between devices: 2.76 us -> 0.01 us  [from_behind(): return lax.ppermute(array, axis, pairs)]
    all_to_all x1, starting transfers between devices: 18.3 us -> 16 us  [shards(): recv = lax.all_to_all(send[None], 'tm', 2, 0, tiled=True)[:, :, 0]]
    all_to_all x1, blocking collectives: 23.6 us -> 21.9 us  [shards(): gated = lax.all_to_all(gated[:, :, None], 'tm', 0, 2, tiled=True)]
  transfers between devices with their start and end apart: 4 -> 4, of which waited for: 4 -> 3; matrix products, arithmetic and copies ran while one was open for 1% -> 2% of each run, Pallas kernels for 0% -> 0%
where the time goes in v5:
time: 125 us
  starting transfers between devices  45 us (36%)
  blocking collectives  32.5 us (26%)
  waiting for transfers between devices  21.4 us (17%)
  local copies, waits for them, and re-layouts  12.1 us (10%)
  matrix products  6.88 us (6%)
  other arithmetic  6.57 us (5%)
    all_to_all x1, blocking collectives, shards(): gated = lax.all_to_all(gated[:, :, None], 'tm', 0, 2, tiled=True)  21.9 us
    all_to_all x1, starting transfers between devices, shards(): lax.all_to_all(spectrum.reshape(1, -1, channels).astype(jnp.bfloat16), 't...  20.7 us
    all_to_all x1, starting transfers between devices, shards(): recv = lax.all_to_all(send[None], 'tm', 2, 0, tiled=True)[:, :, 0]  16 us
    all_to_all x1, waiting for transfers between devices, shards(): recv = lax.all_to_all(send[None], 'tm', 2, 0, tiled=True)[:, :, 0]  14.4 us
    all_gather x1, blocking collectives, shards(): rows = lax.all_gather(series, 'chan', axis=1, tiled=True)  10.6 us
    unnamed x41, local copies, waits for them, and re-layouts  8.43 us
    all_to_all x1, waiting for transfers between devices, gather_chan(): lax.all_to_all(wide, 'chan', 1, 1, tiled=True)  5.88 us
    ppermute x1, starting transfers between devices, from_behind(): return lax.ppermute(array, axis, pairs)  4.87 us
  transfers between devices with their start and end apart: 4, of which 3 were waited for; matrix products, arithmetic and copies ran while one was open for 2% of the time, Pallas kernels for 0%

profile of v5, /device:TPU:1, one launch (start us, length us, event | category | flops | bytes accessed | tf_op | source)
XLA Modules:
  0.0 124.8 jit_solution(6352552940130729355)
XLA Ops:
  0.0 1.1 bitcast_convert_fusion
  1.1 0.5 copy.48
  1.6 0.5 broadcast.13
  2.2 2.1 %reduce = bf16[128,1024]{1,0:T(8,128)(2,1)S(1)} reduce(bf16[128,1,1024]{2,1,0:T(2,128)(2,1)S(1)} %bitcast.92, bf16[]{:T(256)} %broadcast.13), dimensions={1}, to_apply=%bitcast.59.reduce_sub_computation | reduce | bytes 524290
  4.3 0.9 reshape.45
  5.2 20.7 %all-to-all-start = ((bf16[128,2,512]{2,1,0:T(2,128)(2,1)}), bf16[128,2,512]{2,1,0:T(2,128)(2,1)S(1)}, u32[]{:S(2)}, u32[]{:S(2)}) async-start(bf16[128,2,512]{2,1,0:T(2,128)(2,1)} %reshape.45), calls=%async_computation | async-start | bytes 524288 | tf_op jit(solution)/shard_map/all_to_all | solution.py:87
  25.9 10.6 %all_gather.3 = bf16[256,512]{1,0:T(8,128)(2,1)S(1)} all-gather(bf16[256,128]{1,0:T(8,128)(2,1)S(1)} %copy-done.10), channel_id=1, replica_groups=mesh['tm'=128,'chan'=4] {'chan'}, dimensions={1}, use_global_device_ids=true | all-gather | bytes 327680 | tf_op jit(solution)/shard_map/all_gather | solution.py:88
  36.5 4.9 %collective-permute-start = (bf16[2,512]{1,0:T(2,128)(2,1)S(1)}, bf16[2,512]{1,0:T(2,128)(2,1)S(1)}, u32[]{:S(2)}, u32[]{:S(2)}) collective-permute-start(bf16[2,512]{1,0:T(2,128)(2,1)S(1)} %slice.57), channel_id=1, source_target_pairs={{0,4},{4,8},{8,12},{12,16},{16,20},{20,24},{24,28},{28,32},{32,36}... | collective-permute-start | bytes 6152 | tf_op jit(solution)/shard_map/ppermute | solution.py:14
  41.6 0.3 fusion.29
  41.9 0.7 copy-done.11
  42.6 0.2 fusion.28
  43.1 0.5 copy-done.12
  43.6 0.3 reduce-precision_select_fusion
  43.9 0.7 copy-done.13
  44.6 0.2 fusion.8
  45.2 1.1 all-to-all-done
  46.3 0.2 reshape.46
  46.6 0.4 copy.49
  47.2 1.4 %reduce.1 = bf16[128,512]{1,0:T(8,128)(2,1)S(1)} reduce(bf16[128,1,512]{2,1,0:T(2,128)(2,1)S(1)} %bitcast.95, bf16[]{:T(256)} %broadcast.13), dimensions={1}, to_apply=%bitcast.61.reduce_sub_computation | reduce | bytes 262146
  48.6 0.7 reshape.47
  49.3 16.0 %all-to-all-start.1 = ((bf16[128,2,256]{2,1,0:T(2,128)(2,1)}), bf16[128,2,256]{2,1,0:T(2,128)(2,1)S(1)}, u32[]{:S(2)}, u32[]{:S(2)}) async-start(bf16[128,2,256]{2,1,0:T(2,128)(2,1)} %reshape.47), calls=%async_computation.1 | async-start | bytes 262144 | tf_op jit(solution)/shard_map/all_to_all | solution.py:110
  65.4 0.6 copy-done.15
  66.0 0.6 dynamic_slice.7
  67.0 14.4 %all-to-all-done.1 = bf16[128,2,256]{2,1,0:T(2,128)(2,1)S(1)} async-done(((bf16[128,2,256]{2,1,0:T(2,128)(2,1)}), bf16[128,2,256]{2,1,0:T(2,128)(2,1)S(1)}, u32[]{:S(2)}, u32[]{:S(2)}) %all-to-all-start.1) | async-done | bytes 131104 | tf_op jit(solution)/shard_map/all_to_all | solution.py:110
  81.7 0.7 copy-done.8
  82.4 0.3 convolution_negate_fusion
  82.7 0.3 fusion.23
  83.0 0.4 copy-done.3
  83.4 0.2 copy-done.2
  83.7 0.4 fusion.20
  84.1 0.5 copy-done.1
  84.7 0.4 fusion.21
  85.1 0.5 copy-done.4
  85.7 0.4 convolution_add_fusion.1
  86.1 0.4 multiply_subtract_fusion
  86.5 0.4 fusion.31
  86.9 0.4 fusion.30
  87.3 0.4 convolution_add_fusion
  87.7 0.4 convolution_subtract_fusion
  88.0 0.6 fusion.14
  88.7 1.2 fusion.6
  90.0 1.0 reduce.2
  91.0 21.9 %all_to_all.53 = bf16[128,2,128]{2,1,0:T(2,128)(2,1)S(1)} all-to-all(bf16[128,2,128]{2,1,0:T(2,128)(2,1)S(1)} %reshape.49), channel_id=1, replica_groups=mesh['tm'=128,'chan'=4] {'tm'}, dimensions={0} | all-to-all | bytes 131072 | tf_op jit(solution)/shard_map/all_to_all | solution.py:122
  113.1 0.7 broadcast_in_dim.34
  113.8 3.4 %all-to-all-start.3 = ((bf16[256,4,128]{2,0,1:T(8,128)(2,1)}), bf16[256,4,128]{2,0,1:T(8,128)(2,1)S(1)}, u32[]{:S(2)}, u32[]{:S(2)}) async-start(bf16[256,4,128]{2,0,1:T(8,128)(2,1)} %broadcast_in_dim.34), calls=%async_computation.3 | async-start | bytes 524288 | tf_op jit(solution)/shard_map/all_to_all | solution.py:48
  117.2 5.9 %all-to-all-done.3 = bf16[256,4,128]{2,0,1:T(8,128)(2,1)S(1)} async-done(((bf16[256,4,128]{2,0,1:T(8,128)(2,1)}), bf16[256,4,128]{2,0,1:T(8,128)(2,1)S(1)}, u32[]{:S(2)}, u32[]{:S(2)}) %all-to-all-start.3) | async-done | bytes 262176 | tf_op jit(solution)/shard_map/all_to_all | solution.py:48
  123.3 0.6 copy-done.14
  123.9 0.9 fusion.5
  (46 shorter events, 2.3 us)
Async XLA Ops:
  0.0 123.3 %copy-start = (bf16[512,512]{1,0:T(8,128)(2,1)S(1)}, bf16[512,512]{1,0:T(8,128)(2,1)}, u32[]{:S(2)}) copy-start(bf16[512,512]{1,0:T(8,128)(2,1)} %param.22) | copy-start | bytes 1572868
  5.2 20.7 %copy-start.10 = (bf16[256,128]{1,0:T(8,128)(2,1)S(1)}, bf16[256,128]{1,0:T(8,128)(2,1)}, u32[]{:S(2)}) copy-start(bf16[256,128]{1,0:T(8,128)(2,1)} %param.15) | copy-start | bytes 196612
  5.2 36.2 %copy-start.9 = (bf16[512,3,128]{2,0,1:T(8,128)(2,1)S(1)}, bf16[512,3,128]{2,0,1:T(8,128)(2,1)}, u32[]{:S(2)}) copy-start(bf16[512,3,128]{2,0,1:T(8,128)(2,1)} %param.16) | copy-start | bytes 1179652
  5.2 41.1 %all-to-all-start = ((bf16[128,2,512]{2,1,0:T(2,128)(2,1)}), bf16[128,2,512]{2,1,0:T(2,128)(2,1)S(1)}, u32[]{:S(2)}, u32[]{:S(2)}) async-start(bf16[128,2,512]{2,1,0:T(2,128)(2,1)} %reshape.45), calls=%async_computation | async-start | bytes 524288 | tf_op jit(solution)/shard_map/all_to_all | solution.py:87
  36.5 6.1 %collective-permute-start = (bf16[2,512]{1,0:T(2,128)(2,1)S(1)}, bf16[2,512]{1,0:T(2,128)(2,1)S(1)}, u32[]{:S(2)}, u32[]{:S(2)}) collective-permute-start(bf16[2,512]{1,0:T(2,128)(2,1)S(1)} %slice.57), channel_id=1, source_target_pairs={{0,4},{4,8},{8,12},{12,16},{16,20},{20,24},{24,28},{28,32},{32,36}... | collective-permute-start | bytes 6152 | tf_op jit(solution)/shard_map/ppermute | solution.py:14
  41.9 0.7 copy-start.11
  42.9 0.7 copy-start.12
  43.9 0.7 copy-start.13
  49.3 32.1 %all-to-all-start.1 = ((bf16[128,2,256]{2,1,0:T(2,128)(2,1)}), bf16[128,2,256]{2,1,0:T(2,128)(2,1)S(1)}, u32[]{:S(2)}, u32[]{:S(2)}) async-start(bf16[128,2,256]{2,1,0:T(2,128)(2,1)} %reshape.47), calls=%async_computation.1 | async-start | bytes 262144 | tf_op jit(solution)/shard_map/all_to_all | solution.py:110
  65.4 0.7 copy-start.15
  81.5 0.9 copy-start.8
  81.5 1.2 copy-start.7
  82.4 1.0 copy-start.3
  82.4 1.0 copy-start.6
  82.7 1.0 copy-start.2
  83.7 0.9 copy-start.1
  83.7 1.0 copy-start.5
  84.7 0.9 copy-start.4
  113.8 9.3 %all-to-all-start.3 = ((bf16[256,4,128]{2,0,1:T(8,128)(2,1)}), bf16[256,4,128]{2,0,1:T(8,128)(2,1)S(1)}, u32[]{:S(2)}, u32[]{:S(2)}) async-start(bf16[256,4,128]{2,0,1:T(8,128)(2,1)} %broadcast_in_dim.34), calls=%async_computation.3 | async-start | bytes 524288 | tf_op jit(solution)/shard_map/all_to_all | solution.py:48
  123.3 0.7 copy-start.14

commit v6 on v4

--- a/solution.py
+++ b/solution.py
@@ -107,7 +107,7 @@
 
     send = jnp.concatenate(
         [spectrum.reshape(-1, channels).astype(jnp.bfloat16), mixed_in, gate_out], 0)
-    recv = lax.all_to_all(send[None], "tm", 2, 0, tiled=True)[:, :, 0]
+    recv = lax.all_to_all(send.T, "tm", 0, 0, tiled=True)
     spec_len = spectrum.size // channels
     h = recv[:, :spec_len].astype(jnp.float32).reshape(tm_count, 2, spec_len // 2)
     h = jnp.stack([h[:, 0].reshape(2 * tm_count, steps_dev), h[:, 1].reshape(2 * tm_count, steps_dev)])
@@ -119,8 +119,8 @@
     skip = lax.dynamic_index_in_dim(skip_gain, lax.axis_index("tm"), 0, keepdims=False)
     gated = ((convolved + skip * signal) * gate_own).astype(jnp.bfloat16)
 
-    gated = lax.all_to_all(gated[:, :, None], "tm", 0, 2, tiled=True)
-    gated = gather_chan(gated[0])
+    gated = lax.all_to_all(gated, "tm", 0, 0, tiled=True).T
+    gated = gather_chan(gated)
     column_start = lax.axis_index("chan") * channels
     weight_cols = lax.dynamic_slice_in_dim(out_weight, column_start, channels, 1)
     mixed_out = jnp.dot(gated, weight_cols, preferred_element_type=jnp.float32) + out_bias

time: 119 us -> 116 us (0.975)
  other arithmetic: 4.93 us -> 2.48 us
    unnamed x2 -> x0, other arithmetic: 4.01 us -> none
    all_to_all x0 -> x3, other arithmetic: none -> 1.59 us  [the longest x2 0.92 us: shards(): recv = lax.all_to_all(send.T, 'tm', 0, 0, tiled=True)]
    unnamed x41 -> x40, local copies, waits for them, and re-layouts: 8.88 us -> 8.34 us
    broadcast_in_dim x3 -> x2, local copies, waits for them, and re-layouts: 2.52 us -> 2.4 us  [gather_chan(): wide = jnp.broadcast_to(x[:, None, :], (x.shape[0], count, x.shape[1]))]
where the time goes in v6:
time: 116 us; the launch traced here: 115 us
  waiting for transfers between devices  36.5 us (31%)
  starting transfers between devices  31.7 us (27%)
  blocking collectives  23.6 us (20%)
  local copies, waits for them, and re-layouts  13.7 us (12%)
  matrix products  6.94 us (6%)
  other arithmetic  2.48 us (2%)
    all_to_all x1, waiting for transfers between devices, shards(): recv = lax.all_to_all(send.T, 'tm', 0, 0, tiled=True)  24.1 us
    all_to_all x1, blocking collectives, shards(): gated = lax.all_to_all(gated, 'tm', 0, 0, tiled=True).T  23.6 us
    all_to_all x1, starting transfers between devices, shards(): recv = lax.all_to_all(send.T, 'tm', 0, 0, tiled=True)  18.3 us
    all_to_all x2, waiting for transfers between devices, gather_chan(): lax.all_to_all(wide, 'chan', 1, 1, tiled=True)  9.63 us
    unnamed x40, local copies, waits for them, and re-layouts  8.34 us
    all_to_all x2, starting transfers between devices, gather_chan(): lax.all_to_all(wide, 'chan', 1, 1, tiled=True)  8.23 us
    ppermute x1, starting transfers between devices, from_behind(): return lax.ppermute(array, axis, pairs)  5.19 us
    dot_general x10, matrix products, mm(): return jnp.dot(a, b, precision=HI, preferred_element_type=jnp.float32)  3.64 us
  transfers between devices with their start and end apart: 4, of which 4 were waited for; matrix products, arithmetic and copies ran while one was open for 1% of the time, Pallas kernels for 0%

profile of v6, /device:TPU:1, one launch (start us, length us, event | category | flops | bytes accessed | tf_op | source)
XLA Modules:
  0.0 115.4 jit_solution(1161638738718470573)
XLA Ops:
  0.0 1.7 %broadcast_in_dim.17 = bf16[256,4,128]{2,0,1:T(8,128)(2,1)} broadcast(bf16[256,128]{1,0:T(8,128)(2,1)} %param.15), dimensions={0,2} | broadcast | bytes 327680 | tf_op jit(solution)/shard_map/broadcast_in_dim | solution.py:48
  1.7 4.8 %all-to-all-start = ((bf16[256,4,128]{2,0,1:T(8,128)(2,1)}), bf16[256,4,128]{2,0,1:T(8,128)(2,1)S(1)}, u32[]{:S(2)}, u32[]{:S(2)}) async-start(bf16[256,4,128]{2,0,1:T(8,128)(2,1)} %broadcast_in_dim.17), calls=%async_computation | async-start | bytes 524288 | tf_op jit(solution)/shard_map/all_to_all | solution.py:49
  6.5 0.2 copy.36
  6.7 0.8 copy-done.8
  7.7 0.5 copy-done.11
  8.3 3.7 %all-to-all-done = bf16[256,4,128]{2,0,1:T(8,128)(2,1)S(1)} async-done(((bf16[256,4,128]{2,0,1:T(8,128)(2,1)}), bf16[256,4,128]{2,0,1:T(8,128)(2,1)S(1)}, u32[]{:S(2)}, u32[]{:S(2)}) %all-to-all-start) | async-done | bytes 262176 | tf_op jit(solution)/shard_map/all_to_all | solution.py:49
  12.0 5.2 %collective-permute-start = (bf16[2,512]{1,0:T(2,128)(2,1)S(1)}, bf16[2,512]{1,0:T(2,128)(2,1)S(1)}, u32[]{:S(2)}, u32[]{:S(2)}) collective-permute-start(bf16[2,512]{1,0:T(2,128)(2,1)S(1)} %slice_bitcast_fusion), channel_id=1, source_target_pairs={{0,4},{4,8},{8,12},{12,16},{16,20},{20,24},{24,28},{28,32},{32,36}... | collective-permute-start | bytes 6152 | tf_op jit(solution)/shard_map/ppermute | solution.py:15
  17.4 0.3 fusion.29
  17.7 2.8 %collective-permute-done = bf16[2,512]{1,0:T(2,128)(2,1)S(1)} collective-permute-done((bf16[2,512]{1,0:T(2,128)(2,1)S(1)}, bf16[2,512]{1,0:T(2,128)(2,1)S(1)}, u32[]{:S(2)}, u32[]{:S(2)}) %collective-permute-start) | collective-permute-done | bytes 2080 | tf_op jit(solution)/shard_map/ppermute | solution.py:15
  20.5 0.2 fusion.28
  21.0 0.5 copy-done.12
  21.5 0.3 reduce-precision_select_fusion
  21.8 0.7 copy-done.13
  22.5 0.2 fusion.8
  22.8 0.2 fusion.18
  23.3 0.5 broadcast.15
  23.8 0.9 reduce
  24.7 0.8 reshape.46
  25.6 18.3 %all-to-all-start.1 = ((bf16[128,2,768]{2,1,0:T(2,128)(2,1)}), bf16[128,2,768]{2,1,0:T(2,128)(2,1)S(1)}, u32[]{:S(2)}, u32[]{:S(2)}) async-start(bf16[128,2,768]{2,1,0:T(2,128)(2,1)} %reshape.46), calls=%async_computation.1 | async-start | bytes 786432 | tf_op jit(solution)/shard_map/all_to_all | solution.py:110
  43.9 0.6 copy-done.15
  44.5 0.6 dynamic_slice.7
  45.1 24.1 %all-to-all-done.1 = bf16[128,2,768]{2,1,0:T(2,128)(2,1)S(1)} async-done(((bf16[128,2,768]{2,1,0:T(2,128)(2,1)}), bf16[128,2,768]{2,1,0:T(2,128)(2,1)S(1)}, u32[]{:S(2)}, u32[]{:S(2)}) %all-to-all-start.1) | async-done | bytes 393248 | tf_op jit(solution)/shard_map/all_to_all | solution.py:110
  69.3 0.3 reshape.47
  69.6 0.7 copy.41
  70.7 0.8 copy-done.9
  71.6 0.3 convolution_negate_fusion
  71.9 0.3 fusion.23
  72.1 0.4 copy-done.3
  72.6 0.2 copy-done.2
  72.9 0.4 fusion.20
  73.2 0.5 copy-done.1
  73.9 0.4 fusion.21
  74.3 0.6 copy-done.4
  74.8 0.4 convolution_add_fusion.1
  75.2 0.4 multiply_subtract_fusion
  75.6 0.4 fusion.31
  76.0 0.4 fusion.30
  76.4 0.4 convolution_add_fusion
  76.8 0.4 convolution_subtract_fusion
  77.2 0.6 fusion.14
  77.8 1.2 %fusion.6 = bf16[128,1,256]{0,2,1:T(8,128)(2,1)S(1)} fusion(f32[256,128]{1,0:T(8,128)S(1)} %fusion.14, f32[256,128]{1,0:T(8,128)S(1)} %copy-done.9, f32[256,256]{1,0:T(8,128)S(1)} %convolution_subtract_fusion, f32[256,256]{1,0:T(8,128)S(1)} %copy-done.1, f32[256,256]{1,0:T(8,128)S(1)} %convolution_add_fusion, f32[256,256]{1,0:T(8,128)S(1)} %copy-done.3, ...), kind=kOutput, calls=%fused_computation.13 | convolution fusion | flops 101122048 | bytes 1507332 | tf_op jit(solution)/shard_map/dot_general | solution.py:72
  79.0 0.7 reduce.1
  79.9 23.6 %all_to_all.34 = bf16[128,2,128]{2,1,0:T(2,128)(2,1)S(1)} all-to-all(bf16[128,2,128]{2,1,0:T(2,128)(2,1)S(1)} %reshape.48), channel_id=1, replica_groups=mesh['tm'=128,'chan'=4] {'tm'}, dimensions={0} | all-to-all | bytes 131072 | tf_op jit(solution)/shard_map/all_to_all | solution.py:122
  103.7 0.7 broadcast_in_dim.19
  104.4 3.4 %all-to-all-start.3 = ((bf16[256,4,128]{2,0,1:T(8,128)(2,1)}), bf16[256,4,128]{2,0,1:T(8,128)(2,1)S(1)}, u32[]{:S(2)}, u32[]{:S(2)}) async-start(bf16[256,4,128]{2,0,1:T(8,128)(2,1)} %broadcast_in_dim.19), calls=%async_computation.3 | async-start | bytes 524288 | tf_op jit(solution)/shard_map/all_to_all | solution.py:49
  107.8 5.9 %all-to-all-done.3 = bf16[256,4,128]{2,0,1:T(8,128)(2,1)S(1)} async-done(((bf16[256,4,128]{2,0,1:T(8,128)(2,1)}), bf16[256,4,128]{2,0,1:T(8,128)(2,1)S(1)}, u32[]{:S(2)}, u32[]{:S(2)}) %all-to-all-start.3) | async-done | bytes 262176 | tf_op jit(solution)/shard_map/all_to_all | solution.py:49
  113.9 0.6 copy-done.14
  114.5 0.9 fusion.5
  (44 shorter events, 1.9 us)
Async XLA Ops:
  0.0 113.9 %copy-start = (bf16[512,512]{1,0:T(8,128)(2,1)S(1)}, bf16[512,512]{1,0:T(8,128)(2,1)}, u32[]{:S(2)}) copy-start(bf16[512,512]{1,0:T(8,128)(2,1)} %param.22) | copy-start | bytes 1572868
  0.0 6.5 %copy-start.10 = (bf16[512,3,128]{2,0,1:T(8,128)(2,1)S(1)}, bf16[512,3,128]{2,0,1:T(8,128)(2,1)}, u32[]{:S(2)}) copy-start(bf16[512,3,128]{2,0,1:T(8,128)(2,1)} %param.16) | copy-start | bytes 1179652
  1.7 10.4 %all-to-all-start = ((bf16[256,4,128]{2,0,1:T(8,128)(2,1)}), bf16[256,4,128]{2,0,1:T(8,128)(2,1)S(1)}, u32[]{:S(2)}, u32[]{:S(2)}) async-start(bf16[256,4,128]{2,0,1:T(8,128)(2,1)} %broadcast_in_dim.17), calls=%async_computation | async-start | bytes 524288 | tf_op jit(solution)/shard_map/all_to_all | solution.py:49
  6.5 1.0 copy-start.8
  7.6 0.7 copy-start.11
  12.0 8.5 %collective-permute-start = (bf16[2,512]{1,0:T(2,128)(2,1)S(1)}, bf16[2,512]{1,0:T(2,128)(2,1)S(1)}, u32[]{:S(2)}, u32[]{:S(2)}) collective-permute-start(bf16[2,512]{1,0:T(2,128)(2,1)S(1)} %slice_bitcast_fusion), channel_id=1, source_target_pairs={{0,4},{4,8},{8,12},{12,16},{16,20},{20,24},{24,28},{28,32},{32,36}... | collective-permute-start | bytes 6152 | tf_op jit(solution)/shard_map/ppermute | solution.py:15
  20.8 0.7 copy-start.12
  21.8 0.7 copy-start.13
  25.6 43.7 %all-to-all-start.1 = ((bf16[128,2,768]{2,1,0:T(2,128)(2,1)}), bf16[128,2,768]{2,1,0:T(2,128)(2,1)S(1)}, u32[]{:S(2)}, u32[]{:S(2)}) async-start(bf16[128,2,768]{2,1,0:T(2,128)(2,1)} %reshape.46), calls=%async_computation.1 | async-start | bytes 786432 | tf_op jit(solution)/shard_map/all_to_all | solution.py:110
  43.9 0.7 copy-start.15
  70.7 0.9 copy-start.9
  70.7 1.2 %copy-start.7 = (f32[256,128]{1,0:T(8,128)S(1)}, f32[256,128]{1,0:T(8,128)}, u32[]{:S(2)}) copy-start(f32[256,128]{1,0:T(8,128)} %constant.37.clone) | copy-start | bytes 393220
  71.6 1.0 copy-start.3
  71.6 1.0 copy-start.6
  71.9 1.0 copy-start.2
  72.8 0.9 copy-start.1
  72.8 1.0 copy-start.5
  73.9 0.9 copy-start.4
  104.4 9.3 %all-to-all-start.3 = ((bf16[256,4,128]{2,0,1:T(8,128)(2,1)}), bf16[256,4,128]{2,0,1:T(8,128)(2,1)S(1)}, u32[]{:S(2)}, u32[]{:S(2)}) async-start(bf16[256,4,128]{2,0,1:T(8,128)(2,1)} %broadcast_in_dim.19), calls=%async_computation.3 | async-start | bytes 524288 | tf_op jit(solution)/shard_map/all_to_all | solution.py:49
  113.8 0.7 copy-start.14

commit v7 on v6

--- a/solution.py
+++ b/solution.py
@@ -6,7 +6,7 @@
 from jax import lax
 from jax.sharding import PartitionSpec as P
 
-HI = lax.Precision.HIGHEST
+HI = lax.Precision.HIGH
 
 
 def from_behind(array, axis, by):

time: 116 us -> 115 us (level)
  matrix products: 6.94 us -> 5.57 us
where the time goes in v7:
time: 115 us; the launch traced here: 114 us
  waiting for transfers between devices  36.5 us (32%)
  starting transfers between devices  31.7 us (28%)
  blocking collectives  23.6 us (21%)
  local copies, waits for them, and re-layouts  13.9 us (12%)
  matrix products  5.57 us (5%)
  other arithmetic  2.48 us (2%)
    all_to_all x1, waiting for transfers between devices, shards(): recv = lax.all_to_all(send.T, 'tm', 0, 0, tiled=True)  24.1 us
    all_to_all x1, blocking collectives, shards(): gated = lax.all_to_all(gated, 'tm', 0, 0, tiled=True).T  23.6 us
    all_to_all x1, starting transfers between devices, shards(): recv = lax.all_to_all(send.T, 'tm', 0, 0, tiled=True)  18.3 us
    all_to_all x2, waiting for transfers between devices, gather_chan(): lax.all_to_all(wide, 'chan', 1, 1, tiled=True)  9.63 us
    unnamed x40, local copies, waits for them, and re-layouts  8.58 us
    all_to_all x2, starting transfers between devices, gather_chan(): lax.all_to_all(wide, 'chan', 1, 1, tiled=True)  8.23 us
    ppermute x1, starting transfers between devices, from_behind(): return lax.ppermute(array, axis, pairs)  5.19 us
    ppermute x1, waiting for transfers between devices, from_behind(): return lax.ppermute(array, axis, pairs)  2.76 us
  transfers between devices with their start and end apart: 4, of which 4 were waited for; matrix products, arithmetic and copies ran while one was open for 1% of the time, Pallas kernels for 0%

profile of v7, /device:TPU:1, one launch (start us, length us, event | category | flops | bytes accessed | tf_op | source)
XLA Modules:
  0.0 114.3 jit_solution(7598458389436218368)
XLA Ops:
  0.0 1.7 %broadcast_in_dim.17 = bf16[256,4,128]{2,0,1:T(8,128)(2,1)} broadcast(bf16[256,128]{1,0:T(8,128)(2,1)} %param.15), dimensions={0,2} | broadcast | bytes 327680 | tf_op jit(solution)/shard_map/broadcast_in_dim | solution.py:48
  1.7 4.8 %all-to-all-start = ((bf16[256,4,128]{2,0,1:T(8,128)(2,1)}), bf16[256,4,128]{2,0,1:T(8,128)(2,1)S(1)}, u32[]{:S(2)}, u32[]{:S(2)}) async-start(bf16[256,4,128]{2,0,1:T(8,128)(2,1)} %broadcast_in_dim.17), calls=%async_computation | async-start | bytes 524288 | tf_op jit(solution)/shard_map/all_to_all | solution.py:49
  6.5 0.2 copy.36
  6.7 0.8 copy-done.8
  7.7 0.5 copy-done.11
  8.3 3.7 %all-to-all-done = bf16[256,4,128]{2,0,1:T(8,128)(2,1)S(1)} async-done(((bf16[256,4,128]{2,0,1:T(8,128)(2,1)}), bf16[256,4,128]{2,0,1:T(8,128)(2,1)S(1)}, u32[]{:S(2)}, u32[]{:S(2)}) %all-to-all-start) | async-done | bytes 262176 | tf_op jit(solution)/shard_map/all_to_all | solution.py:49
  12.0 5.2 %collective-permute-start = (bf16[2,512]{1,0:T(2,128)(2,1)S(1)}, bf16[2,512]{1,0:T(2,128)(2,1)S(1)}, u32[]{:S(2)}, u32[]{:S(2)}) collective-permute-start(bf16[2,512]{1,0:T(2,128)(2,1)S(1)} %slice_bitcast_fusion), channel_id=1, source_target_pairs={{0,4},{4,8},{8,12},{12,16},{16,20},{20,24},{24,28},{28,32},{32,36}... | collective-permute-start | bytes 6152 | tf_op jit(solution)/shard_map/ppermute | solution.py:15
  17.4 0.3 fusion.29
  17.7 2.8 %collective-permute-done = bf16[2,512]{1,0:T(2,128)(2,1)S(1)} collective-permute-done((bf16[2,512]{1,0:T(2,128)(2,1)S(1)}, bf16[2,512]{1,0:T(2,128)(2,1)S(1)}, u32[]{:S(2)}, u32[]{:S(2)}) %collective-permute-start) | collective-permute-done | bytes 2080 | tf_op jit(solution)/shard_map/ppermute | solution.py:15
  20.5 0.2 fusion.28
  21.0 0.5 copy-done.12
  21.5 0.3 reduce-precision_select_fusion
  21.8 0.7 copy-done.13
  22.5 0.2 fusion.8
  22.8 0.2 fusion.18
  23.3 0.5 broadcast.15
  23.8 0.9 reduce
  24.7 0.8 reshape.46
  25.6 18.3 %all-to-all-start.1 = ((bf16[128,2,768]{2,1,0:T(2,128)(2,1)}), bf16[128,2,768]{2,1,0:T(2,128)(2,1)S(1)}, u32[]{:S(2)}, u32[]{:S(2)}) async-start(bf16[128,2,768]{2,1,0:T(2,128)(2,1)} %reshape.46), calls=%async_computation.1 | async-start | bytes 786432 | tf_op jit(solution)/shard_map/all_to_all | solution.py:110
  43.9 0.6 copy-done.15
  44.5 0.6 dynamic_slice.7
  45.1 24.1 %all-to-all-done.1 = bf16[128,2,768]{2,1,0:T(2,128)(2,1)S(1)} async-done(((bf16[128,2,768]{2,1,0:T(2,128)(2,1)}), bf16[128,2,768]{2,1,0:T(2,128)(2,1)S(1)}, u32[]{:S(2)}, u32[]{:S(2)}) %all-to-all-start.1) | async-done | bytes 393248 | tf_op jit(solution)/shard_map/all_to_all | solution.py:110
  69.3 0.3 reshape.47
  69.6 0.7 copy.41
  70.7 0.8 copy-done.9
  71.6 0.2 convolution_negate_fusion
  71.8 0.2 fusion.23
  72.1 0.5 copy-done.3
  72.6 0.2 copy-done.2
  72.8 0.3 fusion.20
  73.1 0.7 copy-done.1
  73.8 0.3 fusion.21
  74.1 0.7 copy-done.4
  74.8 0.3 convolution_add_fusion.1
  75.1 0.3 multiply_subtract_fusion
  75.4 0.3 fusion.31
  75.7 0.3 fusion.30
  75.9 0.3 convolution_add_fusion
  76.2 0.3 convolution_subtract_fusion
  76.5 0.4 fusion.14
  76.9 1.0 fusion.6
  77.9 0.7 reduce.1
  78.7 23.6 %all_to_all.34 = bf16[128,2,128]{2,1,0:T(2,128)(2,1)S(1)} all-to-all(bf16[128,2,128]{2,1,0:T(2,128)(2,1)S(1)} %reshape.48), channel_id=1, replica_groups=mesh['tm'=128,'chan'=4] {'tm'}, dimensions={0} | all-to-all | bytes 131072 | tf_op jit(solution)/shard_map/all_to_all | solution.py:122
  102.5 0.7 broadcast_in_dim.19
  103.3 3.4 %all-to-all-start.3 = ((bf16[256,4,128]{2,0,1:T(8,128)(2,1)}), bf16[256,4,128]{2,0,1:T(8,128)(2,1)S(1)}, u32[]{:S(2)}, u32[]{:S(2)}) async-start(bf16[256,4,128]{2,0,1:T(8,128)(2,1)} %broadcast_in_dim.19), calls=%async_computation.3 | async-start | bytes 524288 | tf_op jit(solution)/shard_map/all_to_all | solution.py:49
  106.7 5.9 %all-to-all-done.3 = bf16[256,4,128]{2,0,1:T(8,128)(2,1)S(1)} async-done(((bf16[256,4,128]{2,0,1:T(8,128)(2,1)}), bf16[256,4,128]{2,0,1:T(8,128)(2,1)S(1)}, u32[]{:S(2)}, u32[]{:S(2)}) %all-to-all-start.3) | async-done | bytes 262176 | tf_op jit(solution)/shard_map/all_to_all | solution.py:49
  112.7 0.6 copy-done.14
  113.4 0.9 fusion.5
  (44 shorter events, 1.9 us)
Async XLA Ops:
  0.0 112.7 %copy-start = (bf16[512,512]{1,0:T(8,128)(2,1)S(1)}, bf16[512,512]{1,0:T(8,128)(2,1)}, u32[]{:S(2)}) copy-start(bf16[512,512]{1,0:T(8,128)(2,1)} %param.22) | copy-start | bytes 1572868
  0.0 6.5 %copy-start.10 = (bf16[512,3,128]{2,0,1:T(8,128)(2,1)S(1)}, bf16[512,3,128]{2,0,1:T(8,128)(2,1)}, u32[]{:S(2)}) copy-start(bf16[512,3,128]{2,0,1:T(8,128)(2,1)} %param.16) | copy-start | bytes 1179652
  1.7 10.4 %all-to-all-start = ((bf16[256,4,128]{2,0,1:T(8,128)(2,1)}), bf16[256,4,128]{2,0,1:T(8,128)(2,1)S(1)}, u32[]{:S(2)}, u32[]{:S(2)}) async-start(bf16[256,4,128]{2,0,1:T(8,128)(2,1)} %broadcast_in_dim.17), calls=%async_computation | async-start | bytes 524288 | tf_op jit(solution)/shard_map/all_to_all | solution.py:49
  6.5 1.0 copy-start.8
  7.6 0.7 copy-start.11
  12.0 8.5 %collective-permute-start = (bf16[2,512]{1,0:T(2,128)(2,1)S(1)}, bf16[2,512]{1,0:T(2,128)(2,1)S(1)}, u32[]{:S(2)}, u32[]{:S(2)}) collective-permute-start(bf16[2,512]{1,0:T(2,128)(2,1)S(1)} %slice_bitcast_fusion), channel_id=1, source_target_pairs={{0,4},{4,8},{8,12},{12,16},{16,20},{20,24},{24,28},{28,32},{32,36}... | collective-permute-start | bytes 6152 | tf_op jit(solution)/shard_map/ppermute | solution.py:15
  20.8 0.7 copy-start.12
  21.8 0.7 copy-start.13
  25.6 43.7 %all-to-all-start.1 = ((bf16[128,2,768]{2,1,0:T(2,128)(2,1)}), bf16[128,2,768]{2,1,0:T(2,128)(2,1)S(1)}, u32[]{:S(2)}, u32[]{:S(2)}) async-start(bf16[128,2,768]{2,1,0:T(2,128)(2,1)} %reshape.46), calls=%async_computation.1 | async-start | bytes 786432 | tf_op jit(solution)/shard_map/all_to_all | solution.py:110
  43.9 0.7 copy-start.15
  70.7 0.9 copy-start.9
  70.7 1.1 copy-start.7
  71.6 1.0 copy-start.3
  71.6 1.0 copy-start.6
  71.8 1.0 copy-start.2
  72.8 0.9 copy-start.1
  72.8 1.0 copy-start.5
  73.8 0.9 copy-start.4
  103.3 9.3 %all-to-all-start.3 = ((bf16[256,4,128]{2,0,1:T(8,128)(2,1)}), bf16[256,4,128]{2,0,1:T(8,128)(2,1)S(1)}, u32[]{:S(2)}, u32[]{:S(2)}) async-start(bf16[256,4,128]{2,0,1:T(8,128)(2,1)} %broadcast_in_dim.19), calls=%async_computation.3 | async-start | bytes 524288 | tf_op jit(solution)/shard_map/all_to_all | solution.py:49
  112.7 0.7 copy-start.14

commit v8 on v7

--- a/solution.py
+++ b/solution.py
@@ -86,35 +86,29 @@
     taps_count = short_taps.shape[0]
     halo = taps_count - 1
     rows = gather_chan(series)
-    earlier = from_behind(rows[steps_dev - halo:], "tm", 1)
-    projected = jnp.concatenate([
-        jnp.dot(earlier, flat_weight, preferred_element_type=jnp.float32),
-        jnp.dot(rows, flat_weight, preferred_element_type=jnp.float32)], 0)
-    projected = lax.reduce_precision(projected.reshape(steps_dev + halo, 3, channels) + proj_bias, 8, 7)
-    first = lax.axis_index("tm") == 0
-    keep = jnp.logical_not(first) | (jnp.arange(steps_dev + halo) >= halo)
-    extended = jnp.where(keep[:, None, None], projected, 0.0)
-    streams = short_bias + short_taps[0] * extended[taps_count - 1:]
-    for offset in range(1, taps_count):
-        streams = (
-            streams
-            + short_taps[offset]
-            * extended[taps_count - 1 - offset: taps_count - 1 - offset + steps_dev]
-        )
-    streams = lax.reduce_precision(streams, 8, 7)
-    gate_out = streams[:, 0].astype(jnp.bfloat16)
-    mixed_in = (streams[:, 1] * streams[:, 2]).astype(jnp.bfloat16)
+    projected = jnp.dot(rows, flat_weight, preferred_element_type=jnp.float32)
+    projected = (projected.reshape(steps_dev, 3, channels) + proj_bias).astype(jnp.bfloat16)
 
     send = jnp.concatenate(
-        [spectrum.reshape(-1, channels).astype(jnp.bfloat16), mixed_in, gate_out], 0)
+        [spectrum.reshape(-1, channels).astype(jnp.bfloat16),
+         projected.transpose(1, 0, 2).reshape(3 * steps_dev, channels)], 0)
     recv = lax.all_to_all(send.T, "tm", 0, 0, tiled=True)
     spec_len = spectrum.size // channels
     h = recv[:, :spec_len].astype(jnp.float32).reshape(tm_count, 2, spec_len // 2)
     h = jnp.stack([h[:, 0].reshape(2 * tm_count, steps_dev), h[:, 1].reshape(2 * tm_count, steps_dev)])
-    signal_bf = recv[:, spec_len:spec_len + steps_dev]
-    gate_own = recv[:, spec_len + steps_dev:].astype(jnp.float32)
-
-    signal = signal_bf.astype(jnp.float32)
+    own = lax.axis_index("tm")
+    taps = lax.dynamic_index_in_dim(short_taps, own, 2, keepdims=False)
+    bias = lax.dynamic_index_in_dim(short_bias, own, 1, keepdims=False)
+    length = tm_count * steps_dev
+    flat = recv[:, spec_len:].reshape(tm_count, 3, steps_dev).transpose(1, 0, 2).reshape(3, length)
+    flat = flat.astype(jnp.float32)
+    padded = jnp.concatenate([jnp.zeros((3, halo), jnp.float32), flat], 1)
+    streams = bias[:, None] + taps[0][:, None] * padded[:, halo:]
+    for offset in range(1, taps_count):
+        streams = streams + taps[offset][:, None] * padded[:, halo - offset: halo - offset + length]
+    streams = lax.reduce_precision(streams, 8, 7)
+    gate_own = streams[0].reshape(tm_count, steps_dev)
+    signal = lax.reduce_precision(streams[1] * streams[2], 8, 7).reshape(tm_count, steps_dev)
     convolved = long_conv(signal, h, tab)
     skip = lax.dynamic_index_in_dim(skip_gain, lax.axis_index("tm"), 0, keepdims=False)
     gated = ((convolved + skip * signal) * gate_own).astype(jnp.bfloat16)

time: 115 us -> 114 us (level)
  starting transfers between devices: 31.7 us -> 29.7 us
    ppermute x1 -> x0, starting transfers between devices: 5.19 us -> none  [from_behind(): return lax.ppermute(array, axis, pairs)]
    all_to_all x1, starting transfers between devices: 18.3 us -> 21.3 us  [shards(): recv = lax.all_to_all(send.T, 'tm', 0, 0, tiled=True)]
    ppermute x1 -> x0, waiting for transfers between devices: 2.76 us -> none  [from_behind(): return lax.ppermute(array, axis, pairs)]
    all_to_all x1, waiting for transfers between devices: 24.1 us -> 26.6 us  [shards(): recv = lax.all_to_all(send.T, 'tm', 0, 0, tiled=True)]
    unnamed x40 -> x39, local copies, waits for them, and re-layouts: 8.58 us -> 7.13 us
    all_to_all x2, waiting for transfers between devices: 9.63 us -> 11 us  [gather_chan(): lax.all_to_all(wide, 'chan', 1, 1, tiled=True)]
  transfers between devices with their start and end apart: 4 -> 3, of which waited for: 4 -> 3; matrix products, arithmetic and copies ran while one was open for 1% -> 1% of each run, Pallas kernels for 0% -> 0%
where the time goes in v8:
time: 114 us
  waiting for transfers between devices  37.6 us (33%)
  starting transfers between devices  29.7 us (26%)
  blocking collectives  23.7 us (21%)
  local copies, waits for them, and re-layouts  13.8 us (12%)
  matrix products  5.42 us (5%)
  other arithmetic  3.09 us (3%)
    all_to_all x1, waiting for transfers between devices, shards(): recv = lax.all_to_all(send.T, 'tm', 0, 0, tiled=True)  26.6 us
    all_to_all x1, blocking collectives, shards(): gated = lax.all_to_all(gated, 'tm', 0, 0, tiled=True).T  23.7 us
    all_to_all x1, starting transfers between devices, shards(): recv = lax.all_to_all(send.T, 'tm', 0, 0, tiled=True)  21.3 us
    all_to_all x2, waiting for transfers between devices, gather_chan(): lax.all_to_all(wide, 'chan', 1, 1, tiled=True)  11 us
    all_to_all x2, starting transfers between devices, gather_chan(): lax.all_to_all(wide, 'chan', 1, 1, tiled=True)  8.37 us
    unnamed x39, local copies, waits for them, and re-layouts  7.13 us
    dot_general x10, matrix products, mm(): return jnp.dot(a, b, precision=HI, preferred_element_type=jnp.float32)  2.8 us
    broadcast_in_dim x2, local copies, waits for them, and re-layouts, gather_chan(): wide = jnp.broadcast_to(x[:, None, :], (x.shape[0], count, x.shape[1]))  2.37 us
  transfers between devices with their start and end apart: 3, of which 3 were waited for; matrix products, arithmetic and copies ran while one was open for 1% of the time, Pallas kernels for 0%

profile of v8, /device:TPU:1, one launch (start us, length us, event | category | flops | bytes accessed | tf_op | source)
XLA Modules:
  0.0 113.7 jit_solution(15440765857510825409)
XLA Ops:
  0.0 1.6 %broadcast_in_dim.4 = bf16[256,4,128]{2,0,1:T(8,128)(2,1)} broadcast(bf16[256,128]{1,0:T(8,128)(2,1)} %param.15), dimensions={0,2} | broadcast | bytes 327680 | tf_op jit(solution)/shard_map/broadcast_in_dim | solution.py:48
  1.6 5.0 %all-to-all-start = ((bf16[256,4,128]{2,0,1:T(8,128)(2,1)}), bf16[256,4,128]{2,0,1:T(8,128)(2,1)S(1)}, u32[]{:S(2)}, u32[]{:S(2)}) async-start(bf16[256,4,128]{2,0,1:T(8,128)(2,1)} %broadcast_in_dim.4), calls=%async_computation | async-start | bytes 524288 | tf_op jit(solution)/shard_map/all_to_all | solution.py:49
  6.6 0.2 copy.39
  6.9 0.1 copy.53
  7.0 5.1 %all-to-all-done = bf16[256,4,128]{2,0,1:T(8,128)(2,1)S(1)} async-done(((bf16[256,4,128]{2,0,1:T(8,128)(2,1)}), bf16[256,4,128]{2,0,1:T(8,128)(2,1)S(1)}, u32[]{:S(2)}, u32[]{:S(2)}) %all-to-all-start) | async-done | bytes 262176 | tf_op jit(solution)/shard_map/all_to_all | solution.py:49
  12.1 0.2 copy.38
  12.5 0.6 copy-done.12
  13.0 0.3 fusion
  13.4 0.1 copy.40
  13.6 0.5 broadcast.21
  14.1 0.9 reduce.16
  15.0 0.9 reshape.78
  15.9 21.3 %all-to-all-start.1 = ((bf16[128,2,896]{2,1,0:T(2,128)(2,1)}), bf16[128,2,896]{2,1,0:T(2,128)(2,1)S(1)}, u32[]{:S(2)}, u32[]{:S(2)}) async-start(bf16[128,2,896]{2,1,0:T(2,128)(2,1)} %reshape.78), calls=%async_computation.1 | async-start | bytes 917504 | tf_op jit(solution)/shard_map/all_to_all | solution.py:95
  37.2 0.2 dynamic-slice_reduce_fusion.3
  37.4 0.5 copy-done.15
  37.9 0.6 dynamic_slice.17
  38.5 0.2 dynamic-slice_reduce_fusion.2
  38.7 26.6 %all-to-all-done.1 = bf16[128,2,896]{2,1,0:T(2,128)(2,1)S(1)} async-done(((bf16[128,2,896]{2,1,0:T(2,128)(2,1)}), bf16[128,2,896]{2,1,0:T(2,128)(2,1)S(1)}, u32[]{:S(2)}, u32[]{:S(2)}) %all-to-all-start.1) | async-done | bytes 458784 | tf_op jit(solution)/shard_map/all_to_all | solution.py:95
  65.3 0.4 reshape.79
  65.7 1.0 copy.42
  66.8 0.1 copy.44
  66.9 0.3 copy.56
  67.2 0.6 add_reduce-precision_fusion
  67.8 0.8 fusion.18
  69.3 0.8 copy-done.8
  70.1 0.3 convolution_negate_fusion
  70.4 0.6 copy-done.9
  71.0 0.3 fusion.23
  71.3 0.7 copy-done.2
  72.1 0.3 fusion.19
  72.4 0.7 copy-done.1
  73.1 0.3 fusion.20
  73.4 0.6 copy-done.4
  74.1 0.3 convolution_add_fusion.2
  74.4 0.3 multiply_subtract_fusion
  74.7 0.3 fusion.25
  75.0 0.3 fusion.24
  75.3 0.3 convolution_add_fusion.1
  75.5 0.3 convolution_subtract_fusion
  75.8 0.4 fusion.12
  76.2 1.0 fusion.7
  77.2 0.7 reduce.17
  78.0 23.7 %all_to_all.34 = bf16[128,2,128]{2,1,0:T(2,128)(2,1)S(1)} all-to-all(bf16[128,2,128]{2,1,0:T(2,128)(2,1)S(1)} %reshape.80), channel_id=1, replica_groups=mesh['tm'=128,'chan'=4] {'tm'}, dimensions={0} | all-to-all | bytes 131072 | tf_op jit(solution)/shard_map/all_to_all | solution.py:116
  101.9 0.7 broadcast_in_dim.5
  102.7 3.4 %all-to-all-start.3 = ((bf16[256,4,128]{2,0,1:T(8,128)(2,1)}), bf16[256,4,128]{2,0,1:T(8,128)(2,1)S(1)}, u32[]{:S(2)}, u32[]{:S(2)}) async-start(bf16[256,4,128]{2,0,1:T(8,128)(2,1)} %broadcast_in_dim.5), calls=%async_computation.3 | async-start | bytes 524288 | tf_op jit(solution)/shard_map/all_to_all | solution.py:49
  106.1 5.9 %all-to-all-done.3 = bf16[256,4,128]{2,0,1:T(8,128)(2,1)S(1)} async-done(((bf16[256,4,128]{2,0,1:T(8,128)(2,1)}), bf16[256,4,128]{2,0,1:T(8,128)(2,1)S(1)}, u32[]{:S(2)}, u32[]{:S(2)}) %all-to-all-start.3) | async-done | bytes 262176 | tf_op jit(solution)/shard_map/all_to_all | solution.py:49
  112.1 0.6 copy-done.14
  112.8 0.9 fusion.6
  (43 shorter events, 1.5 us)
Async XLA Ops:
  0.0 112.1 %copy-start = (bf16[512,512]{1,0:T(8,128)(2,1)S(1)}, bf16[512,512]{1,0:T(8,128)(2,1)}, u32[]{:S(2)}) copy-start(bf16[512,512]{1,0:T(8,128)(2,1)} %param.22) | copy-start | bytes 1572868
  0.0 6.6 %copy-start.10 = (bf16[512,3,128]{2,0,1:T(8,128)(2,1)S(1)}, bf16[512,3,128]{2,0,1:T(8,128)(2,1)}, u32[]{:S(2)}) copy-start(bf16[512,3,128]{2,0,1:T(8,128)(2,1)} %param.16) | copy-start | bytes 1179652
  1.6 5.2 %copy-start.7 = (f32[2,1,2,256,128]{4,3,2,1,0:T(8,128)S(1)}, f32[2,1,2,256,128]{4,3,2,1,0:T(8,128)}, u32[]{:S(2)}) copy-start(f32[2,1,2,256,128]{4,3,2,1,0:T(8,128)} %param.20) | copy-start | bytes 1572868
  1.6 10.5 %all-to-all-start = ((bf16[256,4,128]{2,0,1:T(8,128)(2,1)}), bf16[256,4,128]{2,0,1:T(8,128)(2,1)S(1)}, u32[]{:S(2)}, u32[]{:S(2)}) async-start(bf16[256,4,128]{2,0,1:T(8,128)(2,1)} %broadcast_in_dim.4), calls=%async_computation | async-start | bytes 524288 | tf_op jit(solution)/shard_map/all_to_all | solution.py:49
  12.3 0.7 copy-start.12
  15.9 21.3 %copy-start.13 = (f32[3,128]{1,0:T(4,128)S(1)}, f32[3,128]{1,0:T(4,128)}, u32[]{:S(2)}) copy-start(f32[3,128]{1,0:T(4,128)} %param.19) | copy-start | bytes 4612
  15.9 49.4 %all-to-all-start.1 = ((bf16[128,2,896]{2,1,0:T(2,128)(2,1)}), bf16[128,2,896]{2,1,0:T(2,128)(2,1)S(1)}, u32[]{:S(2)}, u32[]{:S(2)}) async-start(bf16[128,2,896]{2,1,0:T(2,128)(2,1)} %reshape.78), calls=%async_computation.1 | async-start | bytes 917504 | tf_op jit(solution)/shard_map/all_to_all | solution.py:95
  37.2 1.3 %copy-start.11 = (f32[3,3,128]{2,1,0:T(4,128)S(1)}, f32[3,3,128]{2,1,0:T(4,128)}, u32[]{:S(2)}) copy-start(f32[3,3,128]{2,1,0:T(4,128)} %param.18) | copy-start | bytes 13828
  37.2 0.7 copy-start.15
  69.2 0.9 copy-start.8
  70.1 0.9 copy-start.9
  70.1 1.2 %copy-start.6 = (f32[256,256]{0,1:T(8,128)S(1)}, f32[256,256]{0,1:T(8,128)}, u32[]{:S(2)}) copy-start(f32[256,256]{0,1:T(8,128)} %constant.52) | copy-start | bytes 786436
  71.0 1.0 copy-start.2
  71.0 1.0 copy-start.3
  72.1 0.9 copy-start.1
  72.1 1.0 copy-start.5
  73.1 0.9 copy-start.4
  102.7 9.3 %all-to-all-start.3 = ((bf16[256,4,128]{2,0,1:T(8,128)(2,1)}), bf16[256,4,128]{2,0,1:T(8,128)(2,1)S(1)}, u32[]{:S(2)}, u32[]{:S(2)}) async-start(bf16[256,4,128]{2,0,1:T(8,128)(2,1)} %broadcast_in_dim.5), calls=%async_computation.3 | async-start | bytes 524288 | tf_op jit(solution)/shard_map/all_to_all | solution.py:49
  112.1 0.7 copy-start.14

commit v9 on v8

--- a/solution.py
+++ b/solution.py
@@ -15,32 +15,31 @@
     return lax.ppermute(array, axis, pairs)
 
 
-def reverse_bits_np(values, digits):
-    result = np.zeros_like(values)
+def reverse_bits(values, digits):
+    result = jnp.zeros_like(values)
     for bit_level in range(digits):
-        result = result | (((values >> bit_level) & 1) << (digits - 1 - bit_level))
+        result = result | (values >> bit_level & 1) << digits - 1 - bit_level
     return result
 
 
 def dft_tables(tm_count, steps_dev):
     rows = 2 * tm_count
     digits = tm_count.bit_length() - 1
-    r = np.arange(rows)
-    k1 = 2 * reverse_bits_np(r // 2, digits) + (r % 2)
-    m = np.arange(tm_count)
-    t = np.arange(steps_dev)
-    b = np.arange(steps_dev)
+    r = lax.iota(jnp.int32, rows)
+    k1 = 2 * reverse_bits(r // 2, digits) + r % 2
+    m = lax.iota(jnp.int32, tm_count)
+    t = lax.iota(jnp.int32, steps_dev)
     period = rows * steps_dev
-    ang1 = 2 * np.pi * ((k1[:, None] * m[None, :]) % rows) / rows
-    ang2 = 2 * np.pi * ((t[:, None] * b[None, :]) % steps_dev) / steps_dev
-    angt = 2 * np.pi * ((k1[:, None] * t[None, :]) % period) / period
-    f32 = lambda a: jnp.asarray(a.astype(np.float32))
-    return dict(
-        c1=f32(np.cos(ang1)), s1=f32(np.sin(ang1)),
-        c2=f32(np.cos(ang2)), s2=f32(np.sin(ang2)),
-        ct=f32(np.cos(angt)), st=f32(np.sin(angt)),
-        period=period,
-    )
+
+    def turn(index, count):
+        angle = (index % count).astype(jnp.float32) * (2 * math.pi / count)
+        return jnp.cos(angle), jnp.sin(angle)
+
+    c1, s1 = turn(k1[:, None] * m[None, :], rows)
+    c2, s2 = turn(t[:, None] * t[None, :], steps_dev)
+    ct, st = turn(k1[:, None] * t[None, :], period)
+    c1, s1, c2, s2, ct, st = lax.optimization_barrier((c1, s1, c2, s2, ct, st))
+    return dict(c1=c1, s1=s1, c2=c2, s2=s2, ct=ct, st=st, period=period)
 
 
 def gather_chan(x):

time: 114 us -> 110 us (0.965)
  waiting for transfers between devices: 37.6 us -> 33.7 us
  local copies, waits for them, and re-layouts: 13.8 us -> 11 us
  other arithmetic: 3.09 us -> 5.85 us
    all_to_all x1, waiting for transfers between devices: 26.6 us -> 23.6 us  [shards(): recv = lax.all_to_all(send.T, 'tm', 0, 0, tiled=True)]
    sin x0 -> x3, other arithmetic: none -> 2.72 us  [turn(): return (jnp.cos(angle), jnp.sin(angle))]
    unnamed x39 -> x22, local copies, waits for them, and re-layouts: 7.13 us -> 4.5 us
  transfers between devices with their start and end apart: 3 -> 3, of which waited for: 3 -> 3; matrix products, arithmetic and copies ran while one was open for 1% -> 4% of each run, Pallas kernels for 0% -> 0%
where the time goes in v9:
time: 110 us; the launch traced here: 109 us
  waiting for transfers between devices  33.7 us (31%)
  starting transfers between devices  29.5 us (27%)
  blocking collectives  23.7 us (22%)
  local copies, waits for them, and re-layouts  11 us (10%)
  other arithmetic  5.85 us (5%)
  matrix products  5.23 us (5%)
    all_to_all x1, blocking collectives, shards(): gated = lax.all_to_all(gated, 'tm', 0, 0, tiled=True).T  23.7 us
    all_to_all x1, waiting for transfers between devices, shards(): recv = lax.all_to_all(send.T, 'tm', 0, 0, tiled=True)  23.6 us
    all_to_all x1, starting transfers between devices, shards(): recv = lax.all_to_all(send.T, 'tm', 0, 0, tiled=True)  21.3 us
    all_to_all x2, waiting for transfers between devices, gather_chan(): lax.all_to_all(wide, 'chan', 1, 1, tiled=True)  10.2 us
    all_to_all x2, starting transfers between devices, gather_chan(): lax.all_to_all(wide, 'chan', 1, 1, tiled=True)  8.23 us
    unnamed x22, local copies, waits for them, and re-layouts  4.5 us
    sin x3, other arithmetic, turn(): return (jnp.cos(angle), jnp.sin(angle))  2.72 us
    dot_general x10, matrix products, mm(): return jnp.dot(a, b, precision=HI, preferred_element_type=jnp.float32)  2.72 us
  transfers between devices with their start and end apart: 3, of which 3 were waited for; matrix products, arithmetic and copies ran while one was open for 4% of the time, Pallas kernels for 0%

profile of v9, /device:TPU:1, one launch (start us, length us, event | category | flops | bytes accessed | tf_op | source)
XLA Modules:
  0.0 109.5 jit_solution(4069924554441275985)
XLA Ops:
  0.0 1.7 %broadcast_in_dim.4 = bf16[256,4,128]{2,0,1:T(8,128)(2,1)} broadcast(bf16[256,128]{1,0:T(8,128)(2,1)} %param.9), dimensions={0,2} | broadcast | bytes 327680 | tf_op jit(solution)/shard_map/broadcast_in_dim | solution.py:47
  1.7 4.8 %all-to-all-start = ((bf16[256,4,128]{2,0,1:T(8,128)(2,1)}), bf16[256,4,128]{2,0,1:T(8,128)(2,1)S(1)}, u32[]{:S(2)}, u32[]{:S(2)}) async-start(bf16[256,4,128]{2,0,1:T(8,128)(2,1)} %broadcast_in_dim.4), calls=%async_computation | async-start | bytes 524288 | tf_op jit(solution)/shard_map/all_to_all | solution.py:48
  6.5 0.1 copy.39
  6.7 0.8 copy-done.2
  7.5 0.2 copy.29
  7.7 4.3 %all-to-all-done = bf16[256,4,128]{2,0,1:T(8,128)(2,1)S(1)} async-done(((bf16[256,4,128]{2,0,1:T(8,128)(2,1)}), bf16[256,4,128]{2,0,1:T(8,128)(2,1)S(1)}, u32[]{:S(2)}, u32[]{:S(2)}) %all-to-all-start) | async-done | bytes 262176 | tf_op jit(solution)/shard_map/all_to_all | solution.py:48
  12.0 0.2 copy.28
  12.3 0.6 copy-done.4
  12.9 0.3 fusion
  13.2 0.1 copy.30
  13.4 0.5 broadcast.216
  13.9 0.9 reduce.16
  14.9 0.9 reshape.127
  15.8 21.3 %all-to-all-start.1 = ((bf16[128,2,896]{2,1,0:T(2,128)(2,1)}), bf16[128,2,896]{2,1,0:T(2,128)(2,1)S(1)}, u32[]{:S(2)}, u32[]{:S(2)}) async-start(bf16[128,2,896]{2,1,0:T(2,128)(2,1)} %reshape.127), calls=%async_computation.1 | async-start | bytes 917504 | tf_op jit(solution)/shard_map/all_to_all | solution.py:94
  37.1 0.7 dynamic_slice.17
  37.8 0.2 dynamic-slice_reduce_fusion.3
  38.0 1.0 fusion.32
  39.0 0.6 fusion.40
  39.6 1.1 %fusion.34 = (f32[256,256]{1,0:T(8,128)S(1)}, f32[256,256]{1,0:T(8,128)S(1)}) fusion(s32[256]{0:T(256)S(1)} %fusion.45), kind=kLoop, calls=%fused_computation.60 | loop fusion | flops 917504 | bytes 525312 | tf_op jit(solution)/shard_map/sin | solution.py:36
  40.7 0.7 copy-done.3
  41.4 0.2 dynamic-slice_reduce_fusion.2
  41.6 23.6 %all-to-all-done.1 = bf16[128,2,896]{2,1,0:T(2,128)(2,1)S(1)} async-done(((bf16[128,2,896]{2,1,0:T(2,128)(2,1)}), bf16[128,2,896]{2,1,0:T(2,128)(2,1)S(1)}, u32[]{:S(2)}, u32[]{:S(2)}) %all-to-all-start.1) | async-done | bytes 458784 | tf_op jit(solution)/shard_map/all_to_all | solution.py:94
  65.2 0.4 reshape.128
  65.5 1.0 copy.32
  66.7 0.2 copy.34
  66.9 0.3 copy.42
  67.1 0.6 add_reduce-precision_fusion
  67.8 0.8 fusion.39
  69.1 0.3 convolution_negate_fusion
  69.3 0.3 multiply_subtract_fusion.1
  69.6 0.3 fusion.48
  69.9 0.3 fusion.47
  70.2 0.3 convolution_add_fusion.2
  70.4 0.3 multiply_subtract_fusion
  70.7 0.3 fusion.49
  71.0 0.3 fusion.50
  71.3 0.3 convolution_subtract_fusion
  71.6 0.3 convolution_add_fusion.1
  71.9 0.3 fusion.17
  72.2 1.0 fusion.6
  73.2 0.7 reduce.17
  73.9 23.7 %all_to_all.34 = bf16[128,2,128]{2,1,0:T(2,128)(2,1)S(1)} all-to-all(bf16[128,2,128]{2,1,0:T(2,128)(2,1)S(1)} %reshape.129), channel_id=1, replica_groups=mesh['tm'=128,'chan'=4] {'tm'}, dimensions={0} | all-to-all | bytes 131072 | tf_op jit(solution)/shard_map/all_to_all | solution.py:115
  97.8 0.7 broadcast_in_dim.5
  98.5 3.4 %all-to-all-start.3 = ((bf16[256,4,128]{2,0,1:T(8,128)(2,1)}), bf16[256,4,128]{2,0,1:T(8,128)(2,1)S(1)}, u32[]{:S(2)}, u32[]{:S(2)}) async-start(bf16[256,4,128]{2,0,1:T(8,128)(2,1)} %broadcast_in_dim.5), calls=%async_computation.3 | async-start | bytes 524288 | tf_op jit(solution)/shard_map/all_to_all | solution.py:48
  101.9 5.9 %all-to-all-done.3 = bf16[256,4,128]{2,0,1:T(8,128)(2,1)S(1)} async-done(((bf16[256,4,128]{2,0,1:T(8,128)(2,1)}), bf16[256,4,128]{2,0,1:T(8,128)(2,1)S(1)}, u32[]{:S(2)}, u32[]{:S(2)}) %all-to-all-start.3) | async-done | bytes 262176 | tf_op jit(solution)/shard_map/all_to_all | solution.py:48
  107.8 0.1 copy.38
  108.0 0.6 copy-done.6
  108.6 0.9 fusion.5
  (29 shorter events, 0.9 us)
Async XLA Ops:
  0.0 107.9 %copy-start = (bf16[512,512]{1,0:T(8,128)(2,1)S(1)}, bf16[512,512]{1,0:T(8,128)(2,1)}, u32[]{:S(2)}) copy-start(bf16[512,512]{1,0:T(8,128)(2,1)} %param.16) | copy-start | bytes 1572868
  0.0 6.5 %copy-start.1 = (f32[2,1,2,256,128]{4,3,2,1,0:T(8,128)S(1)}, f32[2,1,2,256,128]{4,3,2,1,0:T(8,128)}, u32[]{:S(2)}) copy-start(f32[2,1,2,256,128]{4,3,2,1,0:T(8,128)} %param.14) | copy-start | bytes 1572868
  1.7 10.4 %all-to-all-start = ((bf16[256,4,128]{2,0,1:T(8,128)(2,1)}), bf16[256,4,128]{2,0,1:T(8,128)(2,1)S(1)}, u32[]{:S(2)}, u32[]{:S(2)}) async-start(bf16[256,4,128]{2,0,1:T(8,128)(2,1)} %broadcast_in_dim.4), calls=%async_computation | async-start | bytes 524288 | tf_op jit(solution)/shard_map/all_to_all | solution.py:48
  6.5 1.0 copy-start.2
  12.2 0.7 copy-start.4
  15.8 21.3 %copy-start.7 = (f32[128]{0:T(128)S(1)}, f32[128]{0:T(128)}, u32[]{:S(2)}) copy-start(f32[128]{0:T(128)} %param.15) | copy-start | bytes 1540
  15.8 49.4 %all-to-all-start.1 = ((bf16[128,2,896]{2,1,0:T(2,128)(2,1)}), bf16[128,2,896]{2,1,0:T(2,128)(2,1)S(1)}, u32[]{:S(2)}, u32[]{:S(2)}) async-start(bf16[128,2,896]{2,1,0:T(2,128)(2,1)} %reshape.127), calls=%async_computation.1 | async-start | bytes 917504 | tf_op jit(solution)/shard_map/all_to_all | solution.py:94
  37.1 0.7 copy-start.5
  40.7 0.7 copy-start.3
  98.5 9.3 %all-to-all-start.3 = ((bf16[256,4,128]{2,0,1:T(8,128)(2,1)}), bf16[256,4,128]{2,0,1:T(8,128)(2,1)S(1)}, u32[]{:S(2)}, u32[]{:S(2)}) async-start(bf16[256,4,128]{2,0,1:T(8,128)(2,1)} %broadcast_in_dim.5), calls=%async_computation.3 | async-start | bytes 524288 | tf_op jit(solution)/shard_map/all_to_all | solution.py:48
  107.9 0.7 copy-start.6

commit v10 on v9

--- a/solution.py
+++ b/solution.py
@@ -91,7 +91,8 @@
     send = jnp.concatenate(
         [spectrum.reshape(-1, channels).astype(jnp.bfloat16),
          projected.transpose(1, 0, 2).reshape(3 * steps_dev, channels)], 0)
-    recv = lax.all_to_all(send.T, "tm", 0, 0, tiled=True)
+    send = send.T.reshape(channels, 2, -1)
+    recv = lax.all_to_all(send, "tm", 0, 0, tiled=True).reshape(tm_count, -1)
     spec_len = spectrum.size // channels
     h = recv[:, :spec_len].astype(jnp.float32).reshape(tm_count, 2, spec_len // 2)
     h = jnp.stack([h[:, 0].reshape(2 * tm_count, steps_dev), h[:, 1].reshape(2 * tm_count, steps_dev)])

time: 110 us -> 108 us (0.982)
  local copies, waits for them, and re-layouts: 11 us -> 9.16 us
  waiting for transfers between devices: 33.7 us -> 34.9 us
    unnamed x22 -> x20, local copies, waits for them, and re-layouts: 4.5 us -> 2.2 us
where the time goes in v10:
time: 108 us
  waiting for transfers between devices  34.9 us (32%)
  starting transfers between devices  29.5 us (27%)
  blocking collectives  23.9 us (22%)
  local copies, waits for them, and re-layouts  9.16 us (8%)
  matrix products  5.2 us (5%)
  other arithmetic  4.91 us (5%)
    all_to_all x1, blocking collectives, shards(): gated = lax.all_to_all(gated, 'tm', 0, 0, tiled=True).T  23.9 us
    all_to_all x1, waiting for transfers between devices, shards(): recv = lax.all_to_all(send, 'tm', 0, 0, tiled=True).reshape(tm_count, -1)  23.8 us
    all_to_all x1, starting transfers between devices, shards(): recv = lax.all_to_all(send, 'tm', 0, 0, tiled=True).reshape(tm_count, -1)  21.2 us
    all_to_all x2, waiting for transfers between devices, gather_chan(): lax.all_to_all(wide, 'chan', 1, 1, tiled=True)  11 us
    all_to_all x2, starting transfers between devices, gather_chan(): lax.all_to_all(wide, 'chan', 1, 1, tiled=True)  8.37 us
    sin x3, other arithmetic, turn(): return (jnp.cos(angle), jnp.sin(angle))  2.72 us
    dot_general x10, matrix products, mm(): return jnp.dot(a, b, precision=HI, preferred_element_type=jnp.float32)  2.72 us
    broadcast_in_dim x2, local copies, waits for them, and re-layouts, gather_chan(): wide = jnp.broadcast_to(x[:, None, :], (x.shape[0], count, x.shape[1]))  2.37 us
  transfers between devices with their start and end apart: 3, of which 3 were waited for; matrix products, arithmetic and copies ran while one was open for 4% of the time, Pallas kernels for 0%

profile of v10, /device:TPU:1, one launch (start us, length us, event | category | flops | bytes accessed | tf_op | source)
XLA Modules:
  0.0 108.0 jit_solution(3881756695433953859)
XLA Ops:
  0.0 1.6 %broadcast_in_dim.4 = bf16[256,4,128]{2,0,1:T(8,128)(2,1)} broadcast(bf16[256,128]{1,0:T(8,128)(2,1)} %param.9), dimensions={0,2} | broadcast | bytes 327680 | tf_op jit(solution)/shard_map/broadcast_in_dim | solution.py:47
  1.6 5.0 %all-to-all-start = ((bf16[256,4,128]{2,0,1:T(8,128)(2,1)}), bf16[256,4,128]{2,0,1:T(8,128)(2,1)S(1)}, u32[]{:S(2)}, u32[]{:S(2)}) async-start(bf16[256,4,128]{2,0,1:T(8,128)(2,1)} %broadcast_in_dim.4), calls=%async_computation | async-start | bytes 524288 | tf_op jit(solution)/shard_map/all_to_all | solution.py:48
  6.6 0.2 copy.31
  6.9 0.1 copy.32
  7.0 5.1 %all-to-all-done = bf16[256,4,128]{2,0,1:T(8,128)(2,1)S(1)} async-done(((bf16[256,4,128]{2,0,1:T(8,128)(2,1)}), bf16[256,4,128]{2,0,1:T(8,128)(2,1)S(1)}, u32[]{:S(2)}, u32[]{:S(2)}) %all-to-all-start) | async-done | bytes 262176 | tf_op jit(solution)/shard_map/all_to_all | solution.py:48
  12.1 0.2 copy.30
  12.5 0.6 copy-done.4
  13.0 0.3 fusion
  13.4 0.1 copy.33
  13.5 0.9 reshape.106
  14.4 21.2 %all-to-all-start.1 = ((bf16[128,2,896]{2,1,0:T(2,128)(2,1)}), bf16[128,2,896]{2,1,0:T(2,128)(2,1)S(1)}, u32[]{:S(2)}, u32[]{:S(2)}) async-start(bf16[128,2,896]{2,1,0:T(2,128)(2,1)} %reshape.106), calls=%async_computation.1 | async-start | bytes 917504 | tf_op jit(solution)/shard_map/all_to_all | solution.py:95
  35.6 1.0 fusion.32
  36.7 0.6 fusion.40
  37.3 1.1 %fusion.34 = (f32[256,256]{1,0:T(8,128)S(1)}, f32[256,256]{1,0:T(8,128)S(1)}) fusion(s32[256]{0:T(256)S(1)} %fusion.45), kind=kLoop, calls=%fused_computation.60 | loop fusion | flops 917504 | bytes 525312 | tf_op jit(solution)/shard_map/sin | solution.py:36
  38.4 0.2 dynamic-slice_reduce_fusion.3
  38.6 0.5 copy-done.7
  39.0 0.6 dynamic_slice.17
  39.6 0.2 dynamic-slice_reduce_fusion.2
  39.9 23.8 %all-to-all-done.1 = bf16[128,2,896]{2,1,0:T(2,128)(2,1)S(1)} async-done(((bf16[128,2,896]{2,1,0:T(2,128)(2,1)}), bf16[128,2,896]{2,1,0:T(2,128)(2,1)S(1)}, u32[]{:S(2)}, u32[]{:S(2)}) %all-to-all-start.1) | async-done | bytes 458784 | tf_op jit(solution)/shard_map/all_to_all | solution.py:95
  63.7 0.7 copy.34
  64.5 0.2 copy.36
  64.7 0.3 copy.43
  64.9 0.6 add_reduce-precision_fusion
  65.6 0.8 fusion.39
  66.5 0.1 copy.37
  66.7 0.1 copy.35
  66.9 0.3 convolution_negate_fusion
  67.1 0.3 multiply_subtract_fusion.1
  67.4 0.3 fusion.47
  67.7 0.3 fusion.48
  68.0 0.3 convolution_add_fusion.2
  68.3 0.3 multiply_subtract_fusion
  68.6 0.3 fusion.50
  68.8 0.3 fusion.49
  69.1 0.3 convolution_add_fusion.1
  69.4 0.3 convolution_subtract_fusion
  69.7 0.3 fusion.17
  70.0 1.0 fusion.6
  71.0 0.5 broadcast.216
  71.5 0.7 reduce.16
  72.2 23.9 %all_to_all.27 = bf16[128,2,128]{2,1,0:T(2,128)(2,1)S(1)} all-to-all(bf16[128,2,128]{2,1,0:T(2,128)(2,1)S(1)} %reshape.133), channel_id=1, replica_groups=mesh['tm'=128,'chan'=4] {'tm'}, dimensions={0} | all-to-all | bytes 131072 | tf_op jit(solution)/shard_map/all_to_all | solution.py:116
  96.1 0.1 copy.42
  96.2 0.7 broadcast_in_dim.5
  97.0 3.4 %all-to-all-start.3 = ((bf16[256,4,128]{2,0,1:T(8,128)(2,1)}), bf16[256,4,128]{2,0,1:T(8,128)(2,1)S(1)}, u32[]{:S(2)}, u32[]{:S(2)}) async-start(bf16[256,4,128]{2,0,1:T(8,128)(2,1)} %broadcast_in_dim.5), calls=%async_computation.3 | async-start | bytes 524288 | tf_op jit(solution)/shard_map/all_to_all | solution.py:48
  100.4 5.9 %all-to-all-done.3 = bf16[256,4,128]{2,0,1:T(8,128)(2,1)S(1)} async-done(((bf16[256,4,128]{2,0,1:T(8,128)(2,1)}), bf16[256,4,128]{2,0,1:T(8,128)(2,1)S(1)}, u32[]{:S(2)}, u32[]{:S(2)}) %all-to-all-start.3) | async-done | bytes 262176 | tf_op jit(solution)/shard_map/all_to_all | solution.py:48
  106.3 0.1 copy.40
  106.4 0.6 copy-done.6
  107.1 0.9 fusion.5
  (27 shorter events, 0.5 us)
Async XLA Ops:
  0.0 106.4 %copy-start = (bf16[512,512]{1,0:T(8,128)(2,1)S(1)}, bf16[512,512]{1,0:T(8,128)(2,1)}, u32[]{:S(2)}) copy-start(bf16[512,512]{1,0:T(8,128)(2,1)} %param.16) | copy-start | bytes 1572868
  0.0 6.6 %copy-start.2 = (bf16[512,3,128]{2,0,1:T(8,128)(2,1)S(1)}, bf16[512,3,128]{2,0,1:T(8,128)(2,1)}, u32[]{:S(2)}) copy-start(bf16[512,3,128]{2,0,1:T(8,128)(2,1)} %param.10) | copy-start | bytes 1179652
  1.6 5.2 %copy-start.1 = (f32[2,1,2,256,128]{4,3,2,1,0:T(8,128)S(1)}, f32[2,1,2,256,128]{4,3,2,1,0:T(8,128)}, u32[]{:S(2)}) copy-start(f32[2,1,2,256,128]{4,3,2,1,0:T(8,128)} %param.14) | copy-start | bytes 1572868
  1.6 10.5 %all-to-all-start = ((bf16[256,4,128]{2,0,1:T(8,128)(2,1)}), bf16[256,4,128]{2,0,1:T(8,128)(2,1)S(1)}, u32[]{:S(2)}, u32[]{:S(2)}) async-start(bf16[256,4,128]{2,0,1:T(8,128)(2,1)} %broadcast_in_dim.4), calls=%async_computation | async-start | bytes 524288 | tf_op jit(solution)/shard_map/all_to_all | solution.py:48
  12.4 0.7 copy-start.4
  14.4 49.3 %all-to-all-start.1 = ((bf16[128,2,896]{2,1,0:T(2,128)(2,1)}), bf16[128,2,896]{2,1,0:T(2,128)(2,1)S(1)}, u32[]{:S(2)}, u32[]{:S(2)}) async-start(bf16[128,2,896]{2,1,0:T(2,128)(2,1)} %reshape.106), calls=%async_computation.1 | async-start | bytes 917504 | tf_op jit(solution)/shard_map/all_to_all | solution.py:95
  37.2 1.1 %copy-start.5 = (f32[3,128]{1,0:T(4,128)S(1)}, f32[3,128]{1,0:T(4,128)}, u32[]{:S(2)}) copy-start(f32[3,128]{1,0:T(4,128)} %param.13) | copy-start | bytes 4612
  38.4 1.3 %copy-start.3 = (f32[3,3,128]{2,1,0:T(4,128)S(1)}, f32[3,3,128]{2,1,0:T(4,128)}, u32[]{:S(2)}) copy-start(f32[3,3,128]{2,1,0:T(4,128)} %param.12) | copy-start | bytes 13828
  38.4 0.7 copy-start.7
  97.0 9.3 %all-to-all-start.3 = ((bf16[256,4,128]{2,0,1:T(8,128)(2,1)}), bf16[256,4,128]{2,0,1:T(8,128)(2,1)S(1)}, u32[]{:S(2)}, u32[]{:S(2)}) async-start(bf16[256,4,128]{2,0,1:T(8,128)(2,1)} %broadcast_in_dim.5), calls=%async_computation.3 | async-start | bytes 524288 | tf_op jit(solution)/shard_map/all_to_all | solution.py:48
  106.4 0.7 copy-start.6

commit v11 on v10

--- a/solution.py
+++ b/solution.py
@@ -113,7 +113,8 @@
     skip = lax.dynamic_index_in_dim(skip_gain, lax.axis_index("tm"), 0, keepdims=False)
     gated = ((convolved + skip * signal) * gate_own).astype(jnp.bfloat16)
 
-    gated = lax.all_to_all(gated, "tm", 0, 0, tiled=True).T
+    gated = lax.all_to_all(gated.reshape(tm_count, 2, -1), "tm", 0, 0, tiled=True)
+    gated = gated.reshape(tm_count, steps_dev).T
     gated = gather_chan(gated)
     column_start = lax.axis_index("chan") * channels
     weight_cols = lax.dynamic_slice_in_dim(out_weight, column_start, channels, 1)

time: 108 us -> 107 us (level)
  waiting for transfers between devices: 34.9 us -> 33.7 us
    unnamed x20 -> x18, local copies, waits for them, and re-layouts: 2.2 us -> 3.27 us
where the time goes in v11:
time: 107 us
  waiting for transfers between devices  33.7 us (31%)
  starting transfers between devices  29.5 us (28%)
  blocking collectives  23.9 us (22%)
  local copies, waits for them, and re-layouts  9.76 us (9%)
  matrix products  5.21 us (5%)
  other arithmetic  4.25 us (4%)
    all_to_all x1, blocking collectives, shards(): lax.all_to_all(gated.reshape(tm_count, 2, -1), 'tm', 0, 0, tiled=True)  23.9 us
    all_to_all x1, waiting for transfers between devices, shards(): recv = lax.all_to_all(send, 'tm', 0, 0, tiled=True).reshape(tm_count, -1)  23.6 us
    all_to_all x1, starting transfers between devices, shards(): recv = lax.all_to_all(send, 'tm', 0, 0, tiled=True).reshape(tm_count, -1)  21.3 us
    all_to_all x2, waiting for transfers between devices, gather_chan(): lax.all_to_all(wide, 'chan', 1, 1, tiled=True)  10.2 us
    all_to_all x2, starting transfers between devices, gather_chan(): lax.all_to_all(wide, 'chan', 1, 1, tiled=True)  8.23 us
    unnamed x18, local copies, waits for them, and re-layouts  3.27 us
    dot_general x10, matrix products, mm(): return jnp.dot(a, b, precision=HI, preferred_element_type=jnp.float32)  2.73 us
    sin x3, other arithmetic, turn(): return (jnp.cos(angle), jnp.sin(angle))  2.72 us
  transfers between devices with their start and end apart: 3, of which 3 were waited for; matrix products, arithmetic and copies ran while one was open for 4% of the time, Pallas kernels for 0%

profile of v11, /device:TPU:1, one launch (start us, length us, event | category | flops | bytes accessed | tf_op | source)
XLA Modules:
  0.0 106.8 jit_solution(5047422701787357687)
XLA Ops:
  0.0 1.7 %broadcast_in_dim.4 = bf16[256,4,128]{2,0,1:T(8,128)(2,1)} broadcast(bf16[256,128]{1,0:T(8,128)(2,1)} %param.9), dimensions={0,2} | broadcast | bytes 327680 | tf_op jit(solution)/shard_map/broadcast_in_dim | solution.py:47
  1.7 4.8 %all-to-all-start = ((bf16[256,4,128]{2,0,1:T(8,128)(2,1)}), bf16[256,4,128]{2,0,1:T(8,128)(2,1)S(1)}, u32[]{:S(2)}, u32[]{:S(2)}) async-start(bf16[256,4,128]{2,0,1:T(8,128)(2,1)} %broadcast_in_dim.4), calls=%async_computation | async-start | bytes 524288 | tf_op jit(solution)/shard_map/all_to_all | solution.py:48
  6.5 0.1 copy.31
  6.7 0.8 copy-done.2
  7.5 0.2 copy.30
  7.7 4.3 %all-to-all-done = bf16[256,4,128]{2,0,1:T(8,128)(2,1)S(1)} async-done(((bf16[256,4,128]{2,0,1:T(8,128)(2,1)}), bf16[256,4,128]{2,0,1:T(8,128)(2,1)S(1)}, u32[]{:S(2)}, u32[]{:S(2)}) %all-to-all-start) | async-done | bytes 262176 | tf_op jit(solution)/shard_map/all_to_all | solution.py:48
  12.0 0.2 copy.29
  12.2 0.1 reshape.121
  12.3 0.6 copy-done.4
  12.9 0.3 fusion
  13.2 0.1 copy.32
  13.4 0.9 reshape.110
  14.3 21.3 %all-to-all-start.1 = ((bf16[128,2,896]{2,1,0:T(2,128)(2,1)}), bf16[128,2,896]{2,1,0:T(2,128)(2,1)S(1)}, u32[]{:S(2)}, u32[]{:S(2)}) async-start(bf16[128,2,896]{2,1,0:T(2,128)(2,1)} %reshape.110), calls=%async_computation.1 | async-start | bytes 917504 | tf_op jit(solution)/shard_map/all_to_all | solution.py:95
  35.6 0.6 dynamic_slice.17
  36.3 0.2 dynamic-slice_reduce_fusion.3
  36.5 1.0 fusion.31
  37.5 0.6 fusion.39
  38.1 1.1 %fusion.33 = (f32[256,256]{1,0:T(8,128)S(1)}, f32[256,256]{1,0:T(8,128)S(1)}) fusion(s32[256]{0:T(256)S(1)} %fusion.44), kind=kLoop, calls=%fused_computation.59 | loop fusion | flops 917504 | bytes 525312 | tf_op jit(solution)/shard_map/sin | solution.py:36
  39.2 0.7 copy-done.3
  39.9 0.2 dynamic-slice_reduce_fusion.2
  40.1 23.6 %all-to-all-done.1 = bf16[128,2,896]{2,1,0:T(2,128)(2,1)S(1)} async-done(((bf16[128,2,896]{2,1,0:T(2,128)(2,1)}), bf16[128,2,896]{2,1,0:T(2,128)(2,1)S(1)}, u32[]{:S(2)}, u32[]{:S(2)}) %all-to-all-start.1) | async-done | bytes 458784 | tf_op jit(solution)/shard_map/all_to_all | solution.py:95
  63.7 0.7 copy.33
  64.5 0.2 copy.35
  64.7 0.3 copy.40
  65.0 0.6 add_reduce-precision_fusion
  65.6 0.8 fusion.38
  66.5 0.1 copy.34
  66.7 0.1 copy.36
  66.9 0.3 convolution_negate_fusion
  67.2 0.3 multiply_subtract_fusion.1
  67.4 0.3 fusion.47
  67.7 0.3 fusion.46
  68.0 0.3 convolution_add_fusion.2
  68.3 0.3 multiply_subtract_fusion
  68.6 0.3 fusion.48
  68.9 0.3 fusion.49
  69.1 0.3 convolution_subtract_fusion
  69.4 0.3 convolution_add_fusion.1
  69.7 0.3 fusion.16
  70.0 1.0 fusion.4
  71.0 23.9 %all_to_all.20 = bf16[128,2,128]{2,1,0:T(2,128)(2,1)S(1)} all-to-all(bf16[128,2,128]{2,1,0:T(2,128)(2,1)S(1)} %reshape.114), channel_id=1, replica_groups=mesh['tm'=128,'chan'=4] {'tm'}, dimensions={0} | all-to-all | bytes 131072 | tf_op jit(solution)/shard_map/all_to_all | solution.py:116
  94.9 0.1 copy.39
  95.0 0.7 broadcast_in_dim.5
  95.8 3.4 %all-to-all-start.3 = ((bf16[256,4,128]{2,0,1:T(8,128)(2,1)}), bf16[256,4,128]{2,0,1:T(8,128)(2,1)S(1)}, u32[]{:S(2)}, u32[]{:S(2)}) async-start(bf16[256,4,128]{2,0,1:T(8,128)(2,1)} %broadcast_in_dim.5), calls=%async_computation.3 | async-start | bytes 524288 | tf_op jit(solution)/shard_map/all_to_all | solution.py:48
  99.2 5.9 %all-to-all-done.3 = bf16[256,4,128]{2,0,1:T(8,128)(2,1)S(1)} async-done(((bf16[256,4,128]{2,0,1:T(8,128)(2,1)}), bf16[256,4,128]{2,0,1:T(8,128)(2,1)S(1)}, u32[]{:S(2)}, u32[]{:S(2)}) %all-to-all-start.3) | async-done | bytes 262176 | tf_op jit(solution)/shard_map/all_to_all | solution.py:48
  105.1 0.1 copy.38
  105.2 0.6 copy-done.6
  105.9 0.9 fusion.5
  (24 shorter events, 0.5 us)
Async XLA Ops:
  0.0 105.2 %copy-start = (bf16[512,512]{1,0:T(8,128)(2,1)S(1)}, bf16[512,512]{1,0:T(8,128)(2,1)}, u32[]{:S(2)}) copy-start(bf16[512,512]{1,0:T(8,128)(2,1)} %param.16) | copy-start | bytes 1572868
  0.0 6.5 %copy-start.1 = (f32[2,1,2,256,128]{4,3,2,1,0:T(8,128)S(1)}, f32[2,1,2,256,128]{4,3,2,1,0:T(8,128)}, u32[]{:S(2)}) copy-start(f32[2,1,2,256,128]{4,3,2,1,0:T(8,128)} %param.14) | copy-start | bytes 1572868
  1.7 10.4 %all-to-all-start = ((bf16[256,4,128]{2,0,1:T(8,128)(2,1)}), bf16[256,4,128]{2,0,1:T(8,128)(2,1)S(1)}, u32[]{:S(2)}, u32[]{:S(2)}) async-start(bf16[256,4,128]{2,0,1:T(8,128)(2,1)} %broadcast_in_dim.4), calls=%async_computation | async-start | bytes 524288 | tf_op jit(solution)/shard_map/all_to_all | solution.py:48
  6.5 1.0 copy-start.2
  12.2 0.7 copy-start.4
  14.3 21.3 %copy-start.7 = (f32[128]{0:T(128)S(1)}, f32[128]{0:T(128)}, u32[]{:S(2)}) copy-start(f32[128]{0:T(128)} %param.15) | copy-start | bytes 1540
  14.3 49.4 %all-to-all-start.1 = ((bf16[128,2,896]{2,1,0:T(2,128)(2,1)}), bf16[128,2,896]{2,1,0:T(2,128)(2,1)S(1)}, u32[]{:S(2)}, u32[]{:S(2)}) async-start(bf16[128,2,896]{2,1,0:T(2,128)(2,1)} %reshape.110), calls=%async_computation.1 | async-start | bytes 917504 | tf_op jit(solution)/shard_map/all_to_all | solution.py:95
  35.6 0.7 copy-start.5
  39.2 0.7 copy-start.3
  95.8 9.3 %all-to-all-start.3 = ((bf16[256,4,128]{2,0,1:T(8,128)(2,1)}), bf16[256,4,128]{2,0,1:T(8,128)(2,1)S(1)}, u32[]{:S(2)}, u32[]{:S(2)}) async-start(bf16[256,4,128]{2,0,1:T(8,128)(2,1)} %broadcast_in_dim.5), calls=%async_computation.3 | async-start | bytes 524288 | tf_op jit(solution)/shard_map/all_to_all | solution.py:48
  105.2 0.7 copy-start.6

commit v12 on v11

--- a/solution.py
+++ b/solution.py
@@ -99,16 +99,21 @@
     own = lax.axis_index("tm")
     taps = lax.dynamic_index_in_dim(short_taps, own, 2, keepdims=False)
     bias = lax.dynamic_index_in_dim(short_bias, own, 1, keepdims=False)
-    length = tm_count * steps_dev
-    flat = recv[:, spec_len:].reshape(tm_count, 3, steps_dev).transpose(1, 0, 2).reshape(3, length)
-    flat = flat.astype(jnp.float32)
-    padded = jnp.concatenate([jnp.zeros((3, halo), jnp.float32), flat], 1)
-    streams = bias[:, None] + taps[0][:, None] * padded[:, halo:]
-    for offset in range(1, taps_count):
-        streams = streams + taps[offset][:, None] * padded[:, halo - offset: halo - offset + length]
-    streams = lax.reduce_precision(streams, 8, 7)
-    gate_own = streams[0].reshape(tm_count, steps_dev)
-    signal = lax.reduce_precision(streams[1] * streams[2], 8, 7).reshape(tm_count, steps_dev)
+    held = recv[:, spec_len:].astype(jnp.float32).reshape(tm_count, 3, steps_dev)
+
+    def earlier(x, offset):
+        carried = jnp.concatenate([jnp.zeros((1, offset), x.dtype), x[:-1, steps_dev - offset:]], 0)
+        return jnp.concatenate([carried, x[:, :steps_dev - offset]], 1)
+
+    streams = []
+    for j in range(3):
+        x = held[:, j]
+        value = bias[j] + taps[0, j] * x
+        for offset in range(1, taps_count):
+            value = value + taps[offset, j] * earlier(x, offset)
+        streams.append(lax.reduce_precision(value, 8, 7))
+    gate_own = streams[0]
+    signal = lax.reduce_precision(streams[1] * streams[2], 8, 7)
     convolved = long_conv(signal, h, tab)
     skip = lax.dynamic_index_in_dim(skip_gain, lax.axis_index("tm"), 0, keepdims=False)
     gated = ((convolved + skip * signal) * gate_own).astype(jnp.bfloat16)

time: 107 us -> 114 us (1.065)
  other arithmetic: 4.25 us -> 8.06 us
  matrix products: 5.21 us -> 7.64 us
    reduce_precision x2 -> x1, other arithmetic: 1.41 us -> 5.26 us  [shards(): signal = lax.reduce_precision(streams[1] * streams[2], 8, 7)]
    dot_general x1, matrix products: 0.95 us -> 3.39 us  [long_conv(): lax.dot_general(s1, ui, (((0,), (0,)), ((), ())), precision=HI, preferred...]
    slice x2 -> x10, local copies, waits for them, and re-layouts: 0.23 us -> 1.76 us  [the longest x2 1.24 us: shards(): value = bias[j] + taps[0, j] * x]
    all_to_all x1, waiting for transfers between devices: 23.6 us -> 22.1 us  [shards(): recv = lax.all_to_all(send, 'tm', 0, 0, tiled=True).reshape(tm_count, -1)]
    unnamed x18 -> x20, local copies, waits for them, and re-layouts: 3.27 us -> 2.89 us
  transfers between devices with their start and end apart: 3 -> 3, of which waited for: 3 -> 3; matrix products, arithmetic and copies ran while one was open for 4% -> 5% of each run, Pallas kernels for 0% -> 0%
where the time goes in v12:
time: 114 us; the launch traced here: 113 us
  waiting for transfers between devices  33.1 us (29%)
  starting transfers between devices  29.5 us (26%)
  blocking collectives  23.7 us (21%)
  local copies, waits for them, and re-layouts  10.7 us (9%)
  other arithmetic  8.06 us (7%)
  matrix products  7.64 us (7%)
    all_to_all x1, blocking collectives, shards(): lax.all_to_all(gated.reshape(tm_count, 2, -1), 'tm', 0, 0, tiled=True)  23.7 us
    all_to_all x1, waiting for transfers between devices, shards(): recv = lax.all_to_all(send, 'tm', 0, 0, tiled=True).reshape(tm_count, -1)  22.1 us
    all_to_all x1, starting transfers between devices, shards(): recv = lax.all_to_all(send, 'tm', 0, 0, tiled=True).reshape(tm_count, -1)  21.2 us
    all_to_all x2, waiting for transfers between devices, gather_chan(): lax.all_to_all(wide, 'chan', 1, 1, tiled=True)  11 us
    all_to_all x2, starting transfers between devices, gather_chan(): lax.all_to_all(wide, 'chan', 1, 1, tiled=True)  8.37 us
    reduce_precision x1, other arithmetic, shards(): signal = lax.reduce_precision(streams[1] * streams[2], 8, 7)  5.26 us
    dot_general x1, matrix products, long_conv(): lax.dot_general(s1, ui, (((0,), (0,)), ((), ())), precision=HI, preferred...  3.39 us
    unnamed x20, local copies, waits for them, and re-layouts  2.89 us
  transfers between devices with their start and end apart: 3, of which 3 were waited for; matrix products, arithmetic and copies ran while one was open for 5% of the time, Pallas kernels for 0%

profile of v12, /device:TPU:1, one launch (start us, length us, event | category | flops | bytes accessed | tf_op | source)
XLA Modules:
  0.0 113.2 jit_solution(3054021784135492555)
XLA Ops:
  0.0 1.7 %broadcast_in_dim.4 = bf16[256,4,128]{2,0,1:T(8,128)(2,1)} broadcast(bf16[256,128]{1,0:T(8,128)(2,1)} %param.9), dimensions={0,2} | broadcast | bytes 327680 | tf_op jit(solution)/shard_map/broadcast_in_dim | solution.py:47
  1.7 5.0 %all-to-all-start = ((bf16[256,4,128]{2,0,1:T(8,128)(2,1)}), bf16[256,4,128]{2,0,1:T(8,128)(2,1)S(1)}, u32[]{:S(2)}, u32[]{:S(2)}) async-start(bf16[256,4,128]{2,0,1:T(8,128)(2,1)} %broadcast_in_dim.4), calls=%async_computation | async-start | bytes 524288 | tf_op jit(solution)/shard_map/all_to_all | solution.py:48
  6.6 0.2 copy.54
  6.9 0.1 copy.55
  7.0 5.1 %all-to-all-done = bf16[256,4,128]{2,0,1:T(8,128)(2,1)S(1)} async-done(((bf16[256,4,128]{2,0,1:T(8,128)(2,1)}), bf16[256,4,128]{2,0,1:T(8,128)(2,1)S(1)}, u32[]{:S(2)}, u32[]{:S(2)}) %all-to-all-start) | async-done | bytes 262176 | tf_op jit(solution)/shard_map/all_to_all | solution.py:48
  12.2 0.2 copy.53
  12.4 0.1 reshape.115
  12.5 0.6 copy-done.4
  13.0 0.3 fusion
  13.4 0.1 copy.56
  13.6 0.9 reshape.102
  14.4 21.2 %all-to-all-start.1 = ((bf16[128,2,896]{2,1,0:T(2,128)(2,1)}), bf16[128,2,896]{2,1,0:T(2,128)(2,1)S(1)}, u32[]{:S(2)}, u32[]{:S(2)}) async-start(bf16[128,2,896]{2,1,0:T(2,128)(2,1)} %reshape.102), calls=%async_computation.1 | async-start | bytes 917504 | tf_op jit(solution)/shard_map/all_to_all | solution.py:95
  35.6 1.0 fusion.50
  36.7 0.6 fusion.57
  37.3 1.1 fusion.52
  38.4 0.6 copy-done.7
  39.1 0.6 dynamic_slice.17
  39.6 0.2 dynamic-slice_reduce_fusion
  39.8 0.5 copy-done.5
  40.4 0.6 fusion.65
  40.9 0.7 fusion.66
  41.6 22.1 %all-to-all-done.1 = bf16[128,2,896]{2,1,0:T(2,128)(2,1)S(1)} async-done(((bf16[128,2,896]{2,1,0:T(2,128)(2,1)}), bf16[128,2,896]{2,1,0:T(2,128)(2,1)S(1)}, u32[]{:S(2)}, u32[]{:S(2)}) %all-to-all-start.1) | async-done | bytes 458784 | tf_op jit(solution)/shard_map/all_to_all | solution.py:95
  63.7 0.7 copy.57
  64.8 0.1 copy.67
  65.1 0.1 copy.68
  65.4 0.1 copy.61
  65.6 0.1 copy.58
  65.8 5.3 %fusion.35 = f32[128,256]{1,0:T(8,128)S(1)} fusion(f32[1,1]{1,0:T(1,128)} %constant.105.clone.1, f32[127,2]{1,0:T(8,128)S(1)} %slice.138, f32[127,2]{1,0:T(8,128)S(1)} %slice.133, f32[128,255]{1,0:T(8,128)S(1)} %bitcast.81, f32[127,1]{1,0:T(8,128)S(1)} %slice.131, f32[128,254]{1,0:T(8,128)S(1)} %bitcast.82, f32[128,255]{1,0:T(8,128)S(1)} %bitcast.85, ...), kind=kLoop, calls=%fused_computation.60 | loop fusion | flops 819200 | bytes 917516 | tf_op jit(solution)/shard_map/reduce_precision | solution.py:116
  71.0 0.3 convolution_negate_fusion
  71.3 0.3 multiply_subtract_fusion.1
  71.6 0.3 fusion.67
  71.8 0.3 fusion.68
  72.1 0.3 convolution_add_fusion.2
  72.4 0.3 multiply_subtract_fusion
  72.7 0.3 fusion.70
  73.0 0.3 fusion.69
  73.3 0.3 convolution_add_fusion.1
  73.5 0.3 convolution_subtract_fusion
  73.8 0.3 fusion.16
  74.1 3.4 %fusion.4 = bf16[128,256]{1,0:T(8,128)(2,1)S(1)} fusion(f32[128,256]{1,0:T(8,128)S(1)} %fusion.16, f32[256,128]{1,0:T(8,128)S(1)} %get-tuple-element.13, f32[256,256]{1,0:T(8,128)S(1)} %convolution_subtract_fusion, f32[256,256]{1,0:T(8,128)S(1)} %get-tuple-element.14, f32[256,256]{1,0:T(8,128)S(1)} %convolution_add_fusion.1, ...), kind=kOutput, calls=%fused_computation.12 | convolution fusion | flops 51118080 | bytes 1900556 | tf_op jit(solution)/shard_map/dot_general | solution.py:71
  77.5 23.7 %all_to_all.20 = bf16[128,2,128]{2,1,0:T(2,128)(2,1)S(1)} all-to-all(bf16[128,2,128]{2,1,0:T(2,128)(2,1)S(1)} %reshape.108), channel_id=1, replica_groups=mesh['tm'=128,'chan'=4] {'tm'}, dimensions={0} | all-to-all | bytes 131072 | tf_op jit(solution)/shard_map/all_to_all | solution.py:121
  101.3 0.1 copy.65
  101.4 0.7 broadcast_in_dim.5
  102.1 3.4 %all-to-all-start.3 = ((bf16[256,4,128]{2,0,1:T(8,128)(2,1)}), bf16[256,4,128]{2,0,1:T(8,128)(2,1)S(1)}, u32[]{:S(2)}, u32[]{:S(2)}) async-start(bf16[256,4,128]{2,0,1:T(8,128)(2,1)} %broadcast_in_dim.5), calls=%async_computation.3 | async-start | bytes 524288 | tf_op jit(solution)/shard_map/all_to_all | solution.py:48
  105.6 5.9 %all-to-all-done.3 = bf16[256,4,128]{2,0,1:T(8,128)(2,1)S(1)} async-done(((bf16[256,4,128]{2,0,1:T(8,128)(2,1)}), bf16[256,4,128]{2,0,1:T(8,128)(2,1)S(1)}, u32[]{:S(2)}, u32[]{:S(2)}) %all-to-all-start.3) | async-done | bytes 262176 | tf_op jit(solution)/shard_map/all_to_all | solution.py:48
  111.4 0.1 copy.64
  111.6 0.6 copy-done.6
  112.2 0.9 fusion.5
  (30 shorter events, 1.0 us)
Async XLA Ops:
  0.0 111.6 %copy-start = (bf16[512,512]{1,0:T(8,128)(2,1)S(1)}, bf16[512,512]{1,0:T(8,128)(2,1)}, u32[]{:S(2)}) copy-start(bf16[512,512]{1,0:T(8,128)(2,1)} %param.16) | copy-start | bytes 1572868
  0.0 6.6 %copy-start.2 = (bf16[512,3,128]{2,0,1:T(8,128)(2,1)S(1)}, bf16[512,3,128]{2,0,1:T(8,128)(2,1)}, u32[]{:S(2)}) copy-start(bf16[512,3,128]{2,0,1:T(8,128)(2,1)} %param.10) | copy-start | bytes 1179652
  1.7 5.2 %copy-start.1 = (f32[2,1,2,256,128]{4,3,2,1,0:T(8,128)S(1)}, f32[2,1,2,256,128]{4,3,2,1,0:T(8,128)}, u32[]{:S(2)}) copy-start(f32[2,1,2,256,128]{4,3,2,1,0:T(8,128)} %param.14) | copy-start | bytes 1572868
  1.7 10.5 %all-to-all-start = ((bf16[256,4,128]{2,0,1:T(8,128)(2,1)}), bf16[256,4,128]{2,0,1:T(8,128)(2,1)S(1)}, u32[]{:S(2)}, u32[]{:S(2)}) async-start(bf16[256,4,128]{2,0,1:T(8,128)(2,1)} %broadcast_in_dim.4), calls=%async_computation | async-start | bytes 524288 | tf_op jit(solution)/shard_map/all_to_all | solution.py:48
  12.4 0.7 copy-start.4
  14.4 49.3 %all-to-all-start.1 = ((bf16[128,2,896]{2,1,0:T(2,128)(2,1)}), bf16[128,2,896]{2,1,0:T(2,128)(2,1)S(1)}, u32[]{:S(2)}, u32[]{:S(2)}) async-start(bf16[128,2,896]{2,1,0:T(2,128)(2,1)} %reshape.102), calls=%async_computation.1 | async-start | bytes 917504 | tf_op jit(solution)/shard_map/all_to_all | solution.py:95
  38.4 1.2 %copy-start.3 = (f32[3,3,128]{2,1,0:T(4,128)S(1)}, f32[3,3,128]{2,1,0:T(4,128)}, u32[]{:S(2)}) copy-start(f32[3,3,128]{2,1,0:T(4,128)} %param.12) | copy-start | bytes 13828
  38.4 0.7 copy-start.7
  39.6 0.7 copy-start.5
  102.1 9.3 %all-to-all-start.3 = ((bf16[256,4,128]{2,0,1:T(8,128)(2,1)}), bf16[256,4,128]{2,0,1:T(8,128)(2,1)S(1)}, u32[]{:S(2)}, u32[]{:S(2)}) async-start(bf16[256,4,128]{2,0,1:T(8,128)(2,1)} %broadcast_in_dim.5), calls=%async_computation.3 | async-start | bytes 524288 | tf_op jit(solution)/shard_map/all_to_all | solution.py:48
  111.6 0.7 copy-start.6

commit v13 on v11

--- a/solution.py
+++ b/solution.py
@@ -91,7 +91,7 @@
     send = jnp.concatenate(
         [spectrum.reshape(-1, channels).astype(jnp.bfloat16),
          projected.transpose(1, 0, 2).reshape(3 * steps_dev, channels)], 0)
-    send = send.T.reshape(channels, 2, -1)
+    send = send.T.reshape(channels, -1, 128)
     recv = lax.all_to_all(send, "tm", 0, 0, tiled=True).reshape(tm_count, -1)
     spec_len = spectrum.size // channels
     h = recv[:, :spec_len].astype(jnp.float32).reshape(tm_count, 2, spec_len // 2)

time: 107 us -> 110 us (1.028)
  waiting for transfers between devices: 33.7 us -> 36.4 us
    all_to_all x1, waiting for transfers between devices: 23.6 us -> 26.1 us  [shards(): recv = lax.all_to_all(send, 'tm', 0, 0, tiled=True).reshape(tm_count, -1)]
where the time goes in v13:
time: 110 us; the launch traced here: 109 us
  waiting for transfers between devices  36.4 us (33%)
  starting transfers between devices  29.5 us (27%)
  blocking collectives  23.9 us (22%)
  local copies, waits for them, and re-layouts  9.64 us (9%)
  matrix products  5.2 us (5%)
  other arithmetic  4.25 us (4%)
    all_to_all x1, waiting for transfers between devices, shards(): recv = lax.all_to_all(send, 'tm', 0, 0, tiled=True).reshape(tm_count, -1)  26.1 us
    all_to_all x1, blocking collectives, shards(): lax.all_to_all(gated.reshape(tm_count, 2, -1), 'tm', 0, 0, tiled=True)  23.9 us
    all_to_all x1, starting transfers between devices, shards(): recv = lax.all_to_all(send, 'tm', 0, 0, tiled=True).reshape(tm_count, -1)  21.3 us
    all_to_all x2, waiting for transfers between devices, gather_chan(): lax.all_to_all(wide, 'chan', 1, 1, tiled=True)  10.2 us
    all_to_all x2, starting transfers between devices, gather_chan(): lax.all_to_all(wide, 'chan', 1, 1, tiled=True)  8.23 us
    unnamed x18, local copies, waits for them, and re-layouts  3.39 us
    sin x3, other arithmetic, turn(): return (jnp.cos(angle), jnp.sin(angle))  2.72 us
    dot_general x10, matrix products, mm(): return jnp.dot(a, b, precision=HI, preferred_element_type=jnp.float32)  2.72 us
  transfers between devices with their start and end apart: 3, of which 3 were waited for; matrix products, arithmetic and copies ran while one was open for 4% of the time, Pallas kernels for 0%

profile of v13, /device:TPU:1, one launch (start us, length us, event | category | flops | bytes accessed | tf_op | source)
XLA Modules:
  0.0 109.3 jit_solution(16342510320396330167)
XLA Ops:
  0.0 1.7 %broadcast_in_dim.4 = bf16[256,4,128]{2,0,1:T(8,128)(2,1)} broadcast(bf16[256,128]{1,0:T(8,128)(2,1)} %param.9), dimensions={0,2} | broadcast | bytes 327680 | tf_op jit(solution)/shard_map/broadcast_in_dim | solution.py:47
  1.7 4.8 %all-to-all-start = ((bf16[256,4,128]{2,0,1:T(8,128)(2,1)}), bf16[256,4,128]{2,0,1:T(8,128)(2,1)S(1)}, u32[]{:S(2)}, u32[]{:S(2)}) async-start(bf16[256,4,128]{2,0,1:T(8,128)(2,1)} %broadcast_in_dim.4), calls=%async_computation | async-start | bytes 524288 | tf_op jit(solution)/shard_map/all_to_all | solution.py:48
  6.5 1.0 copy-done.2
  7.5 0.2 copy.30
  7.7 4.3 %all-to-all-done = bf16[256,4,128]{2,0,1:T(8,128)(2,1)S(1)} async-done(((bf16[256,4,128]{2,0,1:T(8,128)(2,1)}), bf16[256,4,128]{2,0,1:T(8,128)(2,1)S(1)}, u32[]{:S(2)}, u32[]{:S(2)}) %all-to-all-start) | async-done | bytes 262176 | tf_op jit(solution)/shard_map/all_to_all | solution.py:48
  12.0 0.2 copy.29
  12.2 0.0 copy-start.4
  12.2 0.1 reshape.121
  12.3 0.6 copy-done.4
  12.9 0.3 fusion
  13.3 1.2 %copy.31 = bf16[128,14,128]{2,1,0:T(8,128)(2,1)} copy(bf16[128,14,128]{0,2,1:T(8,128)(2,1)S(1)} %bitcast.58) | data formatting | bytes 917504 | tf_op jit(solution)/shard_map/reshape | solution.py:94
  14.5 21.3 %all-to-all-start.1 = ((bf16[128,14,128]{2,1,0:T(8,128)(2,1)}), bf16[128,14,128]{2,1,0:T(8,128)(2,1)S(1)}, u32[]{:S(2)}, u32[]{:S(2)}) async-start(bf16[128,14,128]{2,1,0:T(8,128)(2,1)} %copy.31), calls=%async_computation.1 | async-start | bytes 1048576 | tf_op jit(solution)/shard_map/all_to_all | solution.py:95
  35.8 0.6 dynamic_slice.17
  36.4 0.1 copy-done.5
  36.5 0.2 dynamic-slice_reduce_fusion.3
  36.7 1.0 fusion.31
  37.7 0.6 fusion.39
  38.3 1.1 %fusion.33 = (f32[256,256]{1,0:T(8,128)S(1)}, f32[256,256]{1,0:T(8,128)S(1)}) fusion(s32[256]{0:T(256)S(1)} %fusion.44), kind=kLoop, calls=%fused_computation.59 | loop fusion | flops 917504 | bytes 525312 | tf_op jit(solution)/shard_map/sin | solution.py:36
  39.4 0.7 copy-done.3
  40.1 0.2 dynamic-slice_reduce_fusion.2
  40.3 26.1 %all-to-all-done.1 = bf16[128,14,128]{2,1,0:T(8,128)(2,1)S(1)} async-done(((bf16[128,14,128]{2,1,0:T(8,128)(2,1)}), bf16[128,14,128]{2,1,0:T(8,128)(2,1)S(1)}, u32[]{:S(2)}, u32[]{:S(2)}) %all-to-all-start.1) | async-done | bytes 458784 | tf_op jit(solution)/shard_map/all_to_all | solution.py:95
  66.5 0.4 copy.32
  67.0 0.2 copy.34
  67.2 0.3 copy.39
  67.4 0.6 add_reduce-precision_fusion
  68.1 0.8 fusion.38
  69.0 0.1 copy.33
  69.2 0.1 copy.35
  69.4 0.3 convolution_negate_fusion
  69.6 0.3 multiply_subtract_fusion.1
  69.9 0.3 fusion.47
  70.2 0.3 fusion.46
  70.5 0.3 convolution_add_fusion.2
  70.8 0.3 multiply_subtract_fusion
  71.1 0.3 fusion.48
  71.3 0.3 fusion.49
  71.6 0.3 convolution_subtract_fusion
  71.9 0.3 convolution_add_fusion.1
  72.2 0.3 fusion.16
  72.5 1.0 fusion.4
  73.5 23.9 %all_to_all.20 = bf16[128,2,128]{2,1,0:T(2,128)(2,1)S(1)} all-to-all(bf16[128,2,128]{2,1,0:T(2,128)(2,1)S(1)} %reshape.114), channel_id=1, replica_groups=mesh['tm'=128,'chan'=4] {'tm'}, dimensions={0} | all-to-all | bytes 131072 | tf_op jit(solution)/shard_map/all_to_all | solution.py:116
  97.4 0.1 copy.38
  97.5 0.7 broadcast_in_dim.5
  98.3 3.4 %all-to-all-start.3 = ((bf16[256,4,128]{2,0,1:T(8,128)(2,1)}), bf16[256,4,128]{2,0,1:T(8,128)(2,1)S(1)}, u32[]{:S(2)}, u32[]{:S(2)}) async-start(bf16[256,4,128]{2,0,1:T(8,128)(2,1)} %broadcast_in_dim.5), calls=%async_computation.3 | async-start | bytes 524288 | tf_op jit(solution)/shard_map/all_to_all | solution.py:48
  101.7 5.9 %all-to-all-done.3 = bf16[256,4,128]{2,0,1:T(8,128)(2,1)S(1)} async-done(((bf16[256,4,128]{2,0,1:T(8,128)(2,1)}), bf16[256,4,128]{2,0,1:T(8,128)(2,1)S(1)}, u32[]{:S(2)}, u32[]{:S(2)}) %all-to-all-start.3) | async-done | bytes 262176 | tf_op jit(solution)/shard_map/all_to_all | solution.py:48
  107.6 0.1 copy.37
  107.7 0.6 copy-done.6
  108.4 0.9 fusion.5
  (22 shorter events, 0.4 us)
Async XLA Ops:
  0.0 107.7 %copy-start = (bf16[512,512]{1,0:T(8,128)(2,1)S(1)}, bf16[512,512]{1,0:T(8,128)(2,1)}, u32[]{:S(2)}) copy-start(bf16[512,512]{1,0:T(8,128)(2,1)} %param.16) | copy-start | bytes 1572868
  0.0 6.5 %copy-start.1 = (f32[2,1,2,256,128]{4,3,2,1,0:T(8,128)S(1)}, f32[2,1,2,256,128]{4,3,2,1,0:T(8,128)}, u32[]{:S(2)}) copy-start(f32[2,1,2,256,128]{4,3,2,1,0:T(8,128)} %param.14) | copy-start | bytes 1572868
  1.7 10.4 %all-to-all-start = ((bf16[256,4,128]{2,0,1:T(8,128)(2,1)}), bf16[256,4,128]{2,0,1:T(8,128)(2,1)S(1)}, u32[]{:S(2)}, u32[]{:S(2)}) async-start(bf16[256,4,128]{2,0,1:T(8,128)(2,1)} %broadcast_in_dim.4), calls=%async_computation | async-start | bytes 524288 | tf_op jit(solution)/shard_map/all_to_all | solution.py:48
  6.5 1.0 copy-start.2
  12.2 0.7 copy-start.4
  14.5 21.3 %copy-start.7 = (f32[128]{0:T(128)S(1)}, f32[128]{0:T(128)}, u32[]{:S(2)}) copy-start(f32[128]{0:T(128)} %param.15) | copy-start | bytes 1540
  14.5 52.0 %all-to-all-start.1 = ((bf16[128,14,128]{2,1,0:T(8,128)(2,1)}), bf16[128,14,128]{2,1,0:T(8,128)(2,1)S(1)}, u32[]{:S(2)}, u32[]{:S(2)}) async-start(bf16[128,14,128]{2,1,0:T(8,128)(2,1)} %copy.31), calls=%async_computation.1 | async-start | bytes 1048576 | tf_op jit(solution)/shard_map/all_to_all | solution.py:95
  35.8 0.7 copy-start.5
  39.4 0.7 copy-start.3
  98.3 9.3 %all-to-all-start.3 = ((bf16[256,4,128]{2,0,1:T(8,128)(2,1)}), bf16[256,4,128]{2,0,1:T(8,128)(2,1)S(1)}, u32[]{:S(2)}, u32[]{:S(2)}) async-start(bf16[256,4,128]{2,0,1:T(8,128)(2,1)} %broadcast_in_dim.5), calls=%async_computation.3 | async-start | bytes 524288 | tf_op jit(solution)/shard_map/all_to_all | solution.py:48
  107.7 0.7 copy-start.6

commit v14 on v11

--- a/solution.py
+++ b/solution.py
@@ -94,8 +94,9 @@
     send = send.T.reshape(channels, 2, -1)
     recv = lax.all_to_all(send, "tm", 0, 0, tiled=True).reshape(tm_count, -1)
     spec_len = spectrum.size // channels
-    h = recv[:, :spec_len].astype(jnp.float32).reshape(tm_count, 2, spec_len // 2)
-    h = jnp.stack([h[:, 0].reshape(2 * tm_count, steps_dev), h[:, 1].reshape(2 * tm_count, steps_dev)])
+    half = spec_len // 2
+    h = [recv[:, part * half:(part + 1) * half].astype(jnp.float32).reshape(2 * tm_count, steps_dev)
+         for part in range(2)]
     own = lax.axis_index("tm")
     taps = lax.dynamic_index_in_dim(short_taps, own, 2, keepdims=False)
     bias = lax.dynamic_index_in_dim(short_bias, own, 1, keepdims=False)

time: 107 us -> 107 us (level)
  no operation moved by 1% of the time
where the time goes in v14:
time: 107 us
  waiting for transfers between devices  33.7 us (31%)
  starting transfers between devices  29.5 us (28%)
  blocking collectives  23.7 us (22%)
  local copies, waits for them, and re-layouts  9.7 us (9%)
  matrix products  5.2 us (5%)
  other arithmetic  4.28 us (4%)
    all_to_all x1, blocking collectives, shards(): lax.all_to_all(gated.reshape(tm_count, 2, -1), 'tm', 0, 0, tiled=True)  23.7 us
    all_to_all x1, waiting for transfers between devices, shards(): recv = lax.all_to_all(send, 'tm', 0, 0, tiled=True).reshape(tm_count, -1)  23.6 us
    all_to_all x1, starting transfers between devices, shards(): recv = lax.all_to_all(send, 'tm', 0, 0, tiled=True).reshape(tm_count, -1)  21.3 us
    all_to_all x2, waiting for transfers between devices, gather_chan(): lax.all_to_all(wide, 'chan', 1, 1, tiled=True)  10.2 us
    all_to_all x2, starting transfers between devices, gather_chan(): lax.all_to_all(wide, 'chan', 1, 1, tiled=True)  8.23 us
    unnamed x18, local copies, waits for them, and re-layouts  3.27 us
    sin x3, other arithmetic, turn(): return (jnp.cos(angle), jnp.sin(angle))  2.72 us
    dot_general x10, matrix products, mm(): return jnp.dot(a, b, precision=HI, preferred_element_type=jnp.float32)  2.72 us
  transfers between devices with their start and end apart: 3, of which 3 were waited for; matrix products, arithmetic and copies ran while one was open for 4% of the time, Pallas kernels for 0%

profile of v14, /device:TPU:1, one launch (start us, length us, event | category | flops | bytes accessed | tf_op | source)
XLA Modules:
  0.0 106.6 jit_solution(18189129630850754209)
XLA Ops:
  0.0 1.7 %broadcast_in_dim.4 = bf16[256,4,128]{2,0,1:T(8,128)(2,1)} broadcast(bf16[256,128]{1,0:T(8,128)(2,1)} %param.9), dimensions={0,2} | broadcast | bytes 327680 | tf_op jit(solution)/shard_map/broadcast_in_dim | solution.py:47
  1.7 4.8 %all-to-all-start = ((bf16[256,4,128]{2,0,1:T(8,128)(2,1)}), bf16[256,4,128]{2,0,1:T(8,128)(2,1)S(1)}, u32[]{:S(2)}, u32[]{:S(2)}) async-start(bf16[256,4,128]{2,0,1:T(8,128)(2,1)} %broadcast_in_dim.4), calls=%async_computation | async-start | bytes 524288 | tf_op jit(solution)/shard_map/all_to_all | solution.py:48
  6.5 0.1 copy.32
  6.7 0.8 copy-done.2
  7.5 0.2 copy.31
  7.7 4.3 %all-to-all-done = bf16[256,4,128]{2,0,1:T(8,128)(2,1)S(1)} async-done(((bf16[256,4,128]{2,0,1:T(8,128)(2,1)}), bf16[256,4,128]{2,0,1:T(8,128)(2,1)S(1)}, u32[]{:S(2)}, u32[]{:S(2)}) %all-to-all-start) | async-done | bytes 262176 | tf_op jit(solution)/shard_map/all_to_all | solution.py:48
  12.0 0.2 copy.30
  12.2 0.1 reshape.131
  12.3 0.6 copy-done.4
  12.9 0.3 fusion
  13.2 0.1 copy.33
  13.4 0.9 reshape.116
  14.3 21.3 %all-to-all-start.1 = ((bf16[128,2,896]{2,1,0:T(2,128)(2,1)}), bf16[128,2,896]{2,1,0:T(2,128)(2,1)S(1)}, u32[]{:S(2)}, u32[]{:S(2)}) async-start(bf16[128,2,896]{2,1,0:T(2,128)(2,1)} %reshape.116), calls=%async_computation.1 | async-start | bytes 917504 | tf_op jit(solution)/shard_map/all_to_all | solution.py:95
  35.6 0.6 dynamic_slice.17
  36.3 0.2 dynamic-slice_reduce_fusion.3
  36.5 1.0 fusion.31
  37.5 0.6 fusion.39
  38.1 1.1 %fusion.33 = (f32[256,256]{1,0:T(8,128)S(1)}, f32[256,256]{1,0:T(8,128)S(1)}) fusion(s32[256]{0:T(256)S(1)} %fusion.44), kind=kLoop, calls=%fused_computation.61 | loop fusion | flops 917504 | bytes 525312 | tf_op jit(solution)/shard_map/sin | solution.py:36
  39.3 0.7 copy-done.3
  39.9 0.2 dynamic-slice_reduce_fusion.2
  40.2 23.6 %all-to-all-done.1 = bf16[128,2,896]{2,1,0:T(2,128)(2,1)S(1)} async-done(((bf16[128,2,896]{2,1,0:T(2,128)(2,1)}), bf16[128,2,896]{2,1,0:T(2,128)(2,1)S(1)}, u32[]{:S(2)}, u32[]{:S(2)}) %all-to-all-start.1) | async-done | bytes 458784 | tf_op jit(solution)/shard_map/all_to_all | solution.py:95
  63.7 0.7 copy.34
  64.5 0.1 copy.35
  64.7 0.2 copy.36
  64.9 0.3 copy.41
  65.2 0.6 add_reduce-precision_fusion
  65.8 0.8 fusion.38
  66.7 0.1 copy.37
  66.9 0.3 convolution_negate_fusion
  67.1 0.3 multiply_subtract_fusion.1
  67.4 0.3 fusion.46
  67.7 0.3 fusion.45
  68.0 0.3 convolution_add_fusion.2
  68.3 0.3 multiply_subtract_fusion
  68.6 0.3 fusion.47
  68.8 0.3 fusion.48
  69.1 0.3 convolution_subtract_fusion
  69.4 0.3 convolution_add_fusion.1
  69.7 0.3 fusion.16
  70.0 1.0 fusion.4
  71.0 23.7 %all_to_all.20 = bf16[128,2,128]{2,1,0:T(2,128)(2,1)S(1)} all-to-all(bf16[128,2,128]{2,1,0:T(2,128)(2,1)S(1)} %reshape.122), channel_id=1, replica_groups=mesh['tm'=128,'chan'=4] {'tm'}, dimensions={0} | all-to-all | bytes 131072 | tf_op jit(solution)/shard_map/all_to_all | solution.py:117
  94.7 0.1 copy.40
  94.8 0.7 broadcast_in_dim.5
  95.6 3.4 %all-to-all-start.3 = ((bf16[256,4,128]{2,0,1:T(8,128)(2,1)}), bf16[256,4,128]{2,0,1:T(8,128)(2,1)S(1)}, u32[]{:S(2)}, u32[]{:S(2)}) async-start(bf16[256,4,128]{2,0,1:T(8,128)(2,1)} %broadcast_in_dim.5), calls=%async_computation.3 | async-start | bytes 524288 | tf_op jit(solution)/shard_map/all_to_all | solution.py:48
  99.0 5.9 %all-to-all-done.3 = bf16[256,4,128]{2,0,1:T(8,128)(2,1)S(1)} async-done(((bf16[256,4,128]{2,0,1:T(8,128)(2,1)}), bf16[256,4,128]{2,0,1:T(8,128)(2,1)S(1)}, u32[]{:S(2)}, u32[]{:S(2)}) %all-to-all-start.3) | async-done | bytes 262176 | tf_op jit(solution)/shard_map/all_to_all | solution.py:48
  104.9 0.1 copy.39
  105.0 0.6 copy-done.6
  105.7 0.9 fusion.5
  (23 shorter events, 0.5 us)
Async XLA Ops:
  0.0 105.0 %copy-start = (bf16[512,512]{1,0:T(8,128)(2,1)S(1)}, bf16[512,512]{1,0:T(8,128)(2,1)}, u32[]{:S(2)}) copy-start(bf16[512,512]{1,0:T(8,128)(2,1)} %param.16) | copy-start | bytes 1572868
  0.0 6.5 %copy-start.1 = (f32[2,1,2,256,128]{4,3,2,1,0:T(8,128)S(1)}, f32[2,1,2,256,128]{4,3,2,1,0:T(8,128)}, u32[]{:S(2)}) copy-start(f32[2,1,2,256,128]{4,3,2,1,0:T(8,128)} %param.14) | copy-start | bytes 1572868
  1.7 10.4 %all-to-all-start = ((bf16[256,4,128]{2,0,1:T(8,128)(2,1)}), bf16[256,4,128]{2,0,1:T(8,128)(2,1)S(1)}, u32[]{:S(2)}, u32[]{:S(2)}) async-start(bf16[256,4,128]{2,0,1:T(8,128)(2,1)} %broadcast_in_dim.4), calls=%async_computation | async-start | bytes 524288 | tf_op jit(solution)/shard_map/all_to_all | solution.py:48
  6.5 1.0 copy-start.2
  12.2 0.7 copy-start.4
  14.3 21.3 %copy-start.7 = (f32[128]{0:T(128)S(1)}, f32[128]{0:T(128)}, u32[]{:S(2)}) copy-start(f32[128]{0:T(128)} %param.15) | copy-start | bytes 1540
  14.3 49.4 %all-to-all-start.1 = ((bf16[128,2,896]{2,1,0:T(2,128)(2,1)}), bf16[128,2,896]{2,1,0:T(2,128)(2,1)S(1)}, u32[]{:S(2)}, u32[]{:S(2)}) async-start(bf16[128,2,896]{2,1,0:T(2,128)(2,1)} %reshape.116), calls=%async_computation.1 | async-start | bytes 917504 | tf_op jit(solution)/shard_map/all_to_all | solution.py:95
  35.6 0.7 copy-start.5
  39.2 0.7 copy-start.3
  95.6 9.3 %all-to-all-start.3 = ((bf16[256,4,128]{2,0,1:T(8,128)(2,1)}), bf16[256,4,128]{2,0,1:T(8,128)(2,1)S(1)}, u32[]{:S(2)}, u32[]{:S(2)}) async-start(bf16[256,4,128]{2,0,1:T(8,128)(2,1)} %broadcast_in_dim.5), calls=%async_computation.3 | async-start | bytes 524288 | tf_op jit(solution)/shard_map/all_to_all | solution.py:48
  105.0 0.7 copy-start.6

commit v15 on v14

--- a/solution.py
+++ b/solution.py
@@ -54,8 +54,16 @@
 
 def long_conv(x, h, tab):
     c1, s1, c2, s2, ct, st = (tab[k] for k in ("c1", "s1", "c2", "s2", "ct", "st"))
-    ar = mm(c1, x)
-    ai = -mm(s1, x)
+    xb = x.astype(jnp.bfloat16)
+
+    def mm_exact_rhs(a):
+        high = a.astype(jnp.bfloat16)
+        low = (a - high.astype(jnp.float32)).astype(jnp.bfloat16)
+        return (jnp.dot(high, xb, preferred_element_type=jnp.float32)
+                + jnp.dot(low, xb, preferred_element_type=jnp.float32))
+
+    ar = mm_exact_rhs(c1)
+    ai = -mm_exact_rhs(s1)
     tr = ar * ct + ai * st
     ti = ai * ct - ar * st
     zr = mm(tr, c2) + mm(ti, s2)

time: 107 us -> 108 us (level)
    slice x0 -> x1, other arithmetic: none -> 1.31 us  [shards(): gate_own = streams[0].reshape(tm_count, steps_dev)]
    dot_general x10 -> x8, matrix products: 2.72 us -> 2.2 us  [mm(): return jnp.dot(a, b, precision=HI, preferred_element_type=jnp.float32)]
where the time goes in v15:
time: 108 us; the launch traced here: 107 us
  waiting for transfers between devices  33.7 us (31%)
  starting transfers between devices  29.5 us (27%)
  blocking collectives  23.7 us (22%)
  local copies, waits for them, and re-layouts  9.73 us (9%)
  other arithmetic  5.31 us (5%)
  matrix products  4.75 us (4%)
    all_to_all x1, blocking collectives, shards(): lax.all_to_all(gated.reshape(tm_count, 2, -1), 'tm', 0, 0, tiled=True)  23.7 us
    all_to_all x1, waiting for transfers between devices, shards(): recv = lax.all_to_all(send, 'tm', 0, 0, tiled=True).reshape(tm_count, -1)  23.6 us
    all_to_all x1, starting transfers between devices, shards(): recv = lax.all_to_all(send, 'tm', 0, 0, tiled=True).reshape(tm_count, -1)  21.3 us
    all_to_all x2, waiting for transfers between devices, gather_chan(): lax.all_to_all(wide, 'chan', 1, 1, tiled=True)  10.2 us
    all_to_all x2, starting transfers between devices, gather_chan(): lax.all_to_all(wide, 'chan', 1, 1, tiled=True)  8.23 us
    unnamed x18, local copies, waits for them, and re-layouts  3.27 us
    sin x3, other arithmetic, turn(): return (jnp.cos(angle), jnp.sin(angle))  2.72 us
    broadcast_in_dim x2, local copies, waits for them, and re-layouts, gather_chan(): wide = jnp.broadcast_to(x[:, None, :], (x.shape[0], count, x.shape[1]))  2.38 us
  transfers between devices with their start and end apart: 3, of which 3 were waited for; matrix products, arithmetic and copies ran while one was open for 4% of the time, Pallas kernels for 0%

profile of v15, /device:TPU:1, one launch (start us, length us, event | category | flops | bytes accessed | tf_op | source)
XLA Modules:
  0.0 107.2 jit_solution(12023335278848634259)
XLA Ops:
  0.0 1.6 %broadcast_in_dim.4 = bf16[256,4,128]{2,0,1:T(8,128)(2,1)} broadcast(bf16[256,128]{1,0:T(8,128)(2,1)} %param.9), dimensions={0,2} | broadcast | bytes 327680 | tf_op jit(solution)/shard_map/broadcast_in_dim | solution.py:47
  1.7 4.8 %all-to-all-start = ((bf16[256,4,128]{2,0,1:T(8,128)(2,1)}), bf16[256,4,128]{2,0,1:T(8,128)(2,1)S(1)}, u32[]{:S(2)}, u32[]{:S(2)}) async-start(bf16[256,4,128]{2,0,1:T(8,128)(2,1)} %broadcast_in_dim.4), calls=%async_computation | async-start | bytes 524288 | tf_op jit(solution)/shard_map/all_to_all | solution.py:48
  6.5 0.1 copy.32
  6.7 0.8 copy-done.2
  7.5 0.2 copy.31
  7.7 4.3 %all-to-all-done = bf16[256,4,128]{2,0,1:T(8,128)(2,1)S(1)} async-done(((bf16[256,4,128]{2,0,1:T(8,128)(2,1)}), bf16[256,4,128]{2,0,1:T(8,128)(2,1)S(1)}, u32[]{:S(2)}, u32[]{:S(2)}) %all-to-all-start) | async-done | bytes 262176 | tf_op jit(solution)/shard_map/all_to_all | solution.py:48
  12.0 0.2 copy.30
  12.3 0.6 copy-done.4
  12.9 0.3 fusion
  13.2 0.1 copy.33
  13.4 0.9 reshape.119
  14.3 21.3 %all-to-all-start.1 = ((bf16[128,2,896]{2,1,0:T(2,128)(2,1)}), bf16[128,2,896]{2,1,0:T(2,128)(2,1)S(1)}, u32[]{:S(2)}, u32[]{:S(2)}) async-start(bf16[128,2,896]{2,1,0:T(2,128)(2,1)} %reshape.119), calls=%async_computation.1 | async-start | bytes 917504 | tf_op jit(solution)/shard_map/all_to_all | solution.py:103
  35.6 0.6 dynamic_slice.17
  36.3 0.2 dynamic-slice_reduce_fusion.3
  36.5 1.0 fusion.32
  37.6 0.6 fusion.39
  38.1 1.1 %fusion.34 = (f32[256,256]{1,0:T(8,128)S(1)}, f32[256,256]{1,0:T(8,128)S(1)}) fusion(s32[256]{0:T(256)S(1)} %fusion.50), kind=kLoop, calls=%fused_computation.67 | loop fusion | flops 917504 | bytes 525312 | tf_op jit(solution)/shard_map/sin | solution.py:36
  39.3 0.7 copy-done.3
  39.9 0.2 dynamic-slice_reduce_fusion.2
  40.2 23.6 %all-to-all-done.1 = bf16[128,2,896]{2,1,0:T(2,128)(2,1)S(1)} async-done(((bf16[128,2,896]{2,1,0:T(2,128)(2,1)}), bf16[128,2,896]{2,1,0:T(2,128)(2,1)S(1)}, u32[]{:S(2)}, u32[]{:S(2)}) %all-to-all-start.1) | async-done | bytes 458784 | tf_op jit(solution)/shard_map/all_to_all | solution.py:103
  63.7 0.7 copy.34
  64.5 0.1 copy.35
  64.7 0.2 copy.36
  64.9 0.3 copy.41
  65.2 0.6 add_reduce-precision_fusion
  65.8 0.5 convert_reduce_fusion
  66.3 1.3 %slice_reduce_fusion = (f32[32768]{0:T(1024)S(1)}, f32[32768]{0:T(1024)S(1)}) fusion(f32[3,32768]{1,0:T(4,128)S(1)} %add_reduce-precision_fusion, f32[1,32768]{1,0:T(1,128)S(1)} %get-tuple-element.21, f32[]{:T(128)} %bitcast.10), kind=kLoop, calls=%fused_computation.55 | loop fusion | flops 32768 | bytes 524292 | tf_op jit(solution)/shard_map/slice | solution.py:119
  67.9 0.2 fusion.45
  68.1 0.2 fusion.42
  68.3 0.2 fusion.1
  68.5 0.2 multiply_subtract_fusion.1
  68.7 0.3 fusion.53
  69.0 0.3 fusion.52
  69.2 0.3 convolution_add_fusion.2
  69.5 0.3 multiply_subtract_fusion
  69.8 0.3 fusion.54
  70.1 0.3 fusion.55
  70.4 0.3 convolution_subtract_fusion
  70.7 0.3 convolution_add_fusion.1
  70.9 0.3 fusion.17
  71.3 0.3 fusion.5
  71.6 23.7 %all_to_all.20 = bf16[128,2,128]{2,1,0:T(2,128)(2,1)S(1)} all-to-all(bf16[128,2,128]{2,1,0:T(2,128)(2,1)S(1)} %reshape.125), channel_id=1, replica_groups=mesh['tm'=128,'chan'=4] {'tm'}, dimensions={0} | all-to-all | bytes 131072 | tf_op jit(solution)/shard_map/all_to_all | solution.py:125
  95.5 0.7 broadcast_in_dim.5
  96.2 3.4 %all-to-all-start.3 = ((bf16[256,4,128]{2,0,1:T(8,128)(2,1)}), bf16[256,4,128]{2,0,1:T(8,128)(2,1)S(1)}, u32[]{:S(2)}, u32[]{:S(2)}) async-start(bf16[256,4,128]{2,0,1:T(8,128)(2,1)} %broadcast_in_dim.5), calls=%async_computation.3 | async-start | bytes 524288 | tf_op jit(solution)/shard_map/all_to_all | solution.py:48
  99.6 5.9 %all-to-all-done.3 = bf16[256,4,128]{2,0,1:T(8,128)(2,1)S(1)} async-done(((bf16[256,4,128]{2,0,1:T(8,128)(2,1)}), bf16[256,4,128]{2,0,1:T(8,128)(2,1)S(1)}, u32[]{:S(2)}, u32[]{:S(2)}) %all-to-all-start.3) | async-done | bytes 262176 | tf_op jit(solution)/shard_map/all_to_all | solution.py:48
  105.5 0.1 copy.39
  105.6 0.6 copy-done.6
  106.3 0.9 fusion.6
  (27 shorter events, 0.8 us)
Async XLA Ops:
  0.0 105.6 %copy-start = (bf16[512,512]{1,0:T(8,128)(2,1)S(1)}, bf16[512,512]{1,0:T(8,128)(2,1)}, u32[]{:S(2)}) copy-start(bf16[512,512]{1,0:T(8,128)(2,1)} %param.16) | copy-start | bytes 1572868
  0.0 6.5 %copy-start.1 = (f32[2,1,2,256,128]{4,3,2,1,0:T(8,128)S(1)}, f32[2,1,2,256,128]{4,3,2,1,0:T(8,128)}, u32[]{:S(2)}) copy-start(f32[2,1,2,256,128]{4,3,2,1,0:T(8,128)} %param.14) | copy-start | bytes 1572868
  1.7 10.4 %all-to-all-start = ((bf16[256,4,128]{2,0,1:T(8,128)(2,1)}), bf16[256,4,128]{2,0,1:T(8,128)(2,1)S(1)}, u32[]{:S(2)}, u32[]{:S(2)}) async-start(bf16[256,4,128]{2,0,1:T(8,128)(2,1)} %broadcast_in_dim.4), calls=%async_computation | async-start | bytes 524288 | tf_op jit(solution)/shard_map/all_to_all | solution.py:48
  6.5 1.0 copy-start.2
  12.2 0.7 copy-start.4
  14.3 21.3 %copy-start.7 = (f32[128]{0:T(128)S(1)}, f32[128]{0:T(128)}, u32[]{:S(2)}) copy-start(f32[128]{0:T(128)} %param.15) | copy-start | bytes 1540
  14.3 49.4 %all-to-all-start.1 = ((bf16[128,2,896]{2,1,0:T(2,128)(2,1)}), bf16[128,2,896]{2,1,0:T(2,128)(2,1)S(1)}, u32[]{:S(2)}, u32[]{:S(2)}) async-start(bf16[128,2,896]{2,1,0:T(2,128)(2,1)} %reshape.119), calls=%async_computation.1 | async-start | bytes 917504 | tf_op jit(solution)/shard_map/all_to_all | solution.py:103
  35.6 0.7 copy-start.5
  39.3 0.7 copy-start.3
  96.2 9.3 %all-to-all-start.3 = ((bf16[256,4,128]{2,0,1:T(8,128)(2,1)}), bf16[256,4,128]{2,0,1:T(8,128)(2,1)S(1)}, u32[]{:S(2)}, u32[]{:S(2)}) async-start(bf16[256,4,128]{2,0,1:T(8,128)(2,1)} %broadcast_in_dim.5), calls=%async_computation.3 | async-start | bytes 524288 | tf_op jit(solution)/shard_map/all_to_all | solution.py:48
  105.6 0.7 copy-start.6
